TPU v7x, 1024 devices: a whole 4x4x32 slice. The times are simulated.
1024 devices in a mesh: seq: 16 (over z_lo), head: 4 (over z_hi, core), fsdp: 16 (over x, y).
Axes of the slice: x: 4, y: 4, z: 32 (z_hi: 2, z_lo: 16; z = z_hi * 16 + z_lo), core: 2. Of those that a mesh axis runs over, the one named last changes fastest.
Arguments:
- queries: bfloat16 [16, 6144, 1536], P('fsdp', 'seq', 'head'), may hold values from -40 to 40
- keys: bfloat16 [16, 6144, 1536], P('fsdp', 'seq', 'head'), may hold values from -40 to 40
- values: bfloat16 [16, 6144, 1536], P('fsdp', 'seq', 'head'), may hold values from -6 to 6
- q_gain: float32 [128], replicated, may hold values from 1.2 to 5.5
- k_gain: float32 [128], replicated, may hold values from 1.2 to 5.5
- d_out: bfloat16 [16, 6144, 1536], P('fsdp', 'seq', 'head'), may hold values from -18 to 18
- window: int32 [16, 16, 3], P('fsdp', 'seq'), may hold values from -1 to 15, as said below
Outputs:
- attended: bfloat16 [16, 6144, 1536], P('fsdp', 'seq', 'head')
- grad_queries: bfloat16 [16, 6144, 1536], P('fsdp', 'seq', 'head')
- grad_keys: bfloat16 [16, 6144, 1536], P('fsdp', 'seq', 'head')
- grad_values: bfloat16 [16, 6144, 1536], P('fsdp', 'seq', 'head')
- q_gain_grad: float32 [128], replicated
- k_gain_grad: float32 [128], replicated
Inputs may be any that keep to these rules, and one draw needn't show every extreme that they name: `window`: row (s, t) names tile t, and may name t - 1 and t + 1 where those tiles exist, each at most once and in any order; its other entries are -1. In every sample some row names three tiles.
All inputs are finite; a program needn't handle non-finite values.
Results may differ from a plain program's by a relative error of at most 0.013.
The roundings to bfloat16 on the way count: a program that leaves them out, or rounds other values in their place, can miss the bound.
Values may be sent and summed in bfloat16 or wider, within the bound.
No kernel may reach another device: no remote copies, remote signals or barrier semaphores. Data moves between devices by JAX's collectives and lax.ppermute only.
A program may use at most 32 MiB of HBM per device.

v0:
```python
import math

import jax
import jax.numpy as jnp
from jax import lax
from jax.sharding import PartitionSpec as P

EPSILON = 1e-06


def extended_2(cells, sides, width):
    for axis, dim in sides:
        count = lax.axis_size(axis)
        ends = count - 1
        head = lax.slice_in_dim(cells, 0, width, axis=dim)
        tail = lax.slice_in_dim(cells, cells.shape[dim] - width, cells.shape[dim], axis=dim)
        cells = jnp.concatenate(
            [
                lax.ppermute(tail, axis, [(i, (i + 1) % count) for i in range(ends)]),
                cells,
                lax.ppermute(head, axis, [((i + 1) % count, i) for i in range(ends)]),
            ],
            axis=dim,
        )
    return cells


def normalize(raw_rows, gain_vector):
    shaped = raw_rows.astype(jnp.float32).reshape(
        raw_rows.shape[0], raw_rows.shape[1], -1, gain_vector.shape[0]
    )
    factor = lax.rsqrt(jnp.mean(shaped * shaped, axis=-1, keepdims=True) + EPSILON)
    unit_rows = shaped * factor
    return (unit_rows, factor, (unit_rows * gain_vector).astype(jnp.bfloat16))


def restore(grad_norm, unit_rows, factor, gain_vector):
    scaled = grad_norm * gain_vector
    inner_mean = jnp.mean(scaled * unit_rows, axis=-1, keepdims=True)
    return factor * (scaled - unit_rows * inner_mean)


def head_pass(operands, allowed, score_scale):
    query_rows, key_rows, value_rows, grad_rows = operands
    scores = (
        jnp.einsum("sqd,skd->sqk", query_rows, key_rows, preferred_element_type=jnp.float32)
        * score_scale
    )
    scores = jnp.where(allowed[:, None, :], scores, -jnp.inf)
    row_max = jnp.max(scores, axis=-1, keepdims=True)
    row_sum = jnp.sum(jnp.exp(scores - row_max), axis=-1, keepdims=True)
    log_total = row_max + jnp.log(row_sum)
    attn_weights = jnp.exp(scores - log_total).astype(jnp.bfloat16)
    attended = jnp.einsum(
        "sqk,skd->sqd", attn_weights, value_rows, preferred_element_type=jnp.float32
    ).astype(jnp.bfloat16)
    row_inner = jnp.sum(
        grad_rows.astype(jnp.float32) * attended.astype(jnp.float32), axis=-1, keepdims=True
    )
    grad_weights = jnp.einsum(
        "sqd,skd->sqk", grad_rows, value_rows, preferred_element_type=jnp.float32
    )
    grad_scores = (attn_weights.astype(jnp.float32) * (grad_weights - row_inner)).astype(
        jnp.bfloat16
    )
    grad_query = (
        jnp.einsum("sqk,skd->sqd", grad_scores, key_rows, preferred_element_type=jnp.float32)
        * score_scale
    )
    return (attended, log_total[..., 0], row_inner[..., 0], grad_query, attn_weights, grad_scores)


def key_terms(grad_scores, attn_weights, query_norm, grad_out, score_scale):
    key_part = (
        jnp.einsum("hsqk,sqhd->skhd", grad_scores, query_norm, preferred_element_type=jnp.float32)
        * score_scale
    )
    value_part = jnp.einsum(
        "hsqk,sqhd->skhd", attn_weights, grad_out, preferred_element_type=jnp.float32
    )
    return (key_part, value_part)


def pack_terms(key_part, value_part):
    sample_count, tile_rows = (key_part.shape[0], key_part.shape[1])
    joined = jnp.concatenate(
        [
            key_part.reshape(sample_count, tile_rows, -1),
            value_part.reshape(sample_count, tile_rows, -1),
        ],
        axis=2,
    )
    return joined.astype(jnp.bfloat16)


def per_device(queries, keys, values, q_gain, k_gain, d_out, window):
    sample_count, tile_rows, columns = queries.shape
    head_size = q_gain.shape[0]
    head_count = columns // head_size
    score_scale = 1.0 / math.sqrt(head_size)
    q_unit, q_factor, q_norm = normalize(queries, q_gain)
    k_unit, k_factor, k_norm = normalize(keys, k_gain)
    packed = jnp.concatenate([k_norm.reshape(sample_count, tile_rows, columns), values], axis=2)
    extended = extended_2(packed, (("seq", 1),), tile_rows)
    key_all = extended[..., :columns].reshape(sample_count, 3 * tile_rows, head_count, head_size)
    value_all = extended[..., columns:].reshape(sample_count, 3 * tile_rows, head_count, head_size)
    tile_index = lax.axis_index("seq")
    tile_count = lax.axis_size("seq")
    listing = window[:, 0, :]

    def listed(target):
        return jnp.any(listing == target, axis=-1) & (target >= 0) & (target < tile_count)

    left_ok = listed(tile_index - 1)
    right_ok = listed(tile_index + 1)
    block_flags = jnp.stack([left_ok, listed(tile_index), right_ok], axis=1)
    allowed = jnp.repeat(block_flags, tile_rows, axis=1)
    grad_out = d_out.reshape(sample_count, tile_rows, head_count, head_size)
    operands = (
        jnp.moveaxis(q_norm, 2, 0),
        jnp.moveaxis(key_all, 2, 0),
        jnp.moveaxis(value_all, 2, 0),
        jnp.moveaxis(grad_out, 2, 0),
    )
    results = lax.map(lambda per_head: head_pass(per_head, allowed, score_scale), operands)
    attended, log_total, row_inner, grad_query, attn_weights, grad_scores = results
    attended = jnp.moveaxis(attended, 0, 2).reshape(sample_count, tile_rows, columns)
    grad_qnorm = jnp.moveaxis(grad_query, 0, 2)
    key_every, value_every = key_terms(grad_scores, attn_weights, q_norm, grad_out, score_scale)
    left_terms = (key_every[:, :tile_rows], value_every[:, :tile_rows])
    own_terms = (key_every[:, tile_rows : 2 * tile_rows], value_every[:, tile_rows : 2 * tile_rows])
    right_terms = (key_every[:, 2 * tile_rows :], value_every[:, 2 * tile_rows :])
    outgoing = jnp.concatenate(
        [pack_terms(left_terms[0], left_terms[1]), pack_terms(right_terms[0], right_terms[1])],
        axis=1,
    )
    returned = extended_2(outgoing, (("seq", 1),), tile_rows)
    incoming = returned[:, :tile_rows].astype(jnp.float32) + returned[:, 3 * tile_rows :].astype(
        jnp.float32
    )
    grad_knorm = own_terms[0] + incoming[..., :columns].reshape(
        sample_count, tile_rows, head_count, head_size
    )
    grad_vsum = own_terms[1] + incoming[..., columns:].reshape(
        sample_count, tile_rows, head_count, head_size
    )
    grad_queries = (
        restore(grad_qnorm, q_unit, q_factor, q_gain)
        .astype(jnp.bfloat16)
        .reshape(sample_count, tile_rows, columns)
    )
    grad_keys = (
        restore(grad_knorm, k_unit, k_factor, k_gain)
        .astype(jnp.bfloat16)
        .reshape(sample_count, tile_rows, columns)
    )
    grad_values = grad_vsum.astype(jnp.bfloat16).reshape(sample_count, tile_rows, columns)
    gain_terms = (
        jnp.sum(grad_qnorm * q_unit, axis=(0, 1, 2)),
        jnp.sum(grad_knorm * k_unit, axis=(0, 1, 2)),
    )
    q_total, k_total = lax.psum((gain_terms[0], gain_terms[1]), ("seq", "head", "fsdp"))
    pair_count = sample_count * lax.axis_size("fsdp") * head_count * lax.axis_size("head")
    return (
        attended,
        grad_queries,
        grad_keys,
        grad_values,
        q_total / pair_count,
        k_total / pair_count,
    )


def solution(mesh):
    return jax.shard_map(
        per_device,
        mesh=mesh,
        in_specs=(
            P("fsdp", "seq", "head"),
            P("fsdp", "seq", "head"),
            P("fsdp", "seq", "head"),
            P(),
            P(),
            P("fsdp", "seq", "head"),
            P("fsdp", "seq", None),
        ),
        out_specs=(
            P("fsdp", "seq", "head"),
            P("fsdp", "seq", "head"),
            P("fsdp", "seq", "head"),
            P("fsdp", "seq", "head"),
            P(),
            P(),
        ),
        check_vma=False,
    )
```

profile of v0, /device:TPU:24, one launch (start us, length us, event | category | flops | bytes accessed | tf_op | source)
XLA Modules:
  0.0 242.7 jit_solution(7391959657078029622)
XLA Ops:
  0.6 0.7 broadcast_bitcast_fusion
  1.3 1.2 copy.23
  2.5 1.2 copy.24
  3.7 0.9 multiply_reduce_fusion.4
  4.6 0.1 fusion.28
  4.7 0.9 pad_maximum_fusion.1
  5.6 1.3 collective-permute-start.1
  6.9 4.6 %collective-permute-start = (bf16[1,384,768]{1,2,0:T(8,128)(2,1)}, bf16[1,384,768]{1,2,0:T(8,128)(2,1)S(1)}, u32[]{:S(2)}, u32[]{:S(2)}) collective-permute-start(bf16[1,384,768]{1,2,0:T(8,128)(2,1)} %pad_maximum_fusion.1), channel_id=1, source_target_pairs={{0,64},{64,128},{128,192},{192,256},{256,320},{320,384},{384,448},... | collective-permute-start | bytes 1769480 | tf_op jit(solution)/shard_map/ppermute | solution.py:19
  11.5 0.2 copy.22
  11.9 0.7 compare_reduce_fusion.2
  12.6 0.2 copy.25
  14.7 0.1 add_bitcast_fusion
  14.8 0.1 fusion.29
  14.9 8.0 %collective-permute-done.1 = bf16[1,384,768]{1,2,0:T(8,128)(2,1)S(1)} collective-permute-done((bf16[1,384,768]{1,2,0:T(8,128)(2,1)}, bf16[1,384,768]{1,2,0:T(8,128)(2,1)S(1)}, u32[]{:S(2)}, u32[]{:S(2)}) %collective-permute-start.1) | collective-permute-done | bytes 589856 | tf_op jit(solution)/shard_map/ppermute | solution.py:21
  23.0 1.3 collective-permute-done
  24.3 0.2 pad_maximum_fusion
  24.4 0.1 fusion.33
  24.6 17.9 %while.17 = (s32[]{:T(128)}, bf16[3,1,384,128]{2,3,1,0:T(8,128)(2,1)}, f32[3,1,384,128]{2,3,0,1:T(8,128)}, bf16[3,1,384,1152]{3,2,1,0:T(8,128)(2,1)}, bf16[3,1,3...) while((s32[]{:T(128)}, ...), condition=%wide.region_9.10_spmd.clone, body=%wide.region_5.9_spmd.clone.sunk | while | flops 458145024 | bytes 14277640 | solution.py:125
  24.6 0.1 broadcast_in_dim.67
  24.7 0.5 fusion.50
  25.2 0.4 exponential_reduce_fusion.2
  25.6 1.2 bitcast_dynamic-update-slice_fusion.6
  26.9 1.0 bitcast_dynamic-update-slice_fusion.7
  28.0 1.4 bitcast_dynamic-update-slice_fusion.8
  29.3 0.4 fusion.51
  29.7 0.1 copy.48
  29.9 0.7 constant_dynamic-update-slice_fusion.2
  30.6 0.1 broadcast_in_dim.67
  30.7 0.5 fusion.50
  31.2 0.4 exponential_reduce_fusion.2
  31.6 1.3 bitcast_dynamic-update-slice_fusion.6
  32.9 1.0 bitcast_dynamic-update-slice_fusion.7
  34.0 1.4 bitcast_dynamic-update-slice_fusion.8
  35.3 0.4 fusion.51
  35.7 0.1 copy.48
  35.9 0.7 constant_dynamic-update-slice_fusion.2
  36.6 0.1 broadcast_in_dim.67
  36.6 0.5 fusion.50
  37.2 0.4 exponential_reduce_fusion.2
  37.6 1.2 bitcast_dynamic-update-slice_fusion.6
  38.8 1.0 bitcast_dynamic-update-slice_fusion.7
  39.9 1.4 bitcast_dynamic-update-slice_fusion.8
  41.3 0.4 fusion.51
  41.7 0.1 copy.48
  41.8 0.7 constant_dynamic-update-slice_fusion.2
  42.5 1.8 copy.32
  44.4 3.9 %fusion.38 = (bf16[1,1152,3,128]{1,3,2,0:T(8,128)(2,1)S(1)}, f32[1,1152,3,128]{1,3,2,0:T(8,128)}) fusion(bf16[3,1,384,1152]{3,2,1,0:T(8,128)(2,1)} %get-tuple-element.63, f32[384,3,128]{0,2,1:T(8,128)S(1)} %bitcast.143, f32[128]{0:T(128)S(1)} %copy-done.6, f32[384,3]{0,1:T(4,128)S(1)} %add_rsqrt_fusion.1), kind=kOutput, calls=%fused_computation.81 | convolution fusion | flops 341065728 | bytes 5903360 | tf_op jit(solution)/shard_map/hsqk,sqhd->skhd/dot_general | solution.py:75
  48.3 1.9 fusion.37
  50.4 1.4 collective-permute-start.3
  51.9 4.9 %collective-permute-start.2 = (bf16[1,384,768]{1,2,0:T(8,128)(2,1)S(1)}, bf16[1,384,768]{1,2,0:T(8,128)(2,1)S(1)}, u32[]{:S(2)}, u32[]{:S(2)}) collective-permute-start(bf16[1,384,768]{1,2,0:T(8,128)(2,1)S(1)} %pad_maximum_fusion.2), channel_id=1, source_target_pairs={{0,64},{64,128},{128,192},{192,256},{256,320},{320,384},{384,448},... | collective-permute-start | bytes 1769480 | tf_op jit(solution)/shard_map/ppermute | solution.py:19
  56.8 0.2 fusion.26
  57.0 0.1 multiply_convert_fusion.2
  57.2 0.9 copy.33
  58.1 9.1 %collective-permute-done.3 = bf16[1,384,768]{1,2,0:T(8,128)(2,1)S(1)} collective-permute-done((bf16[1,384,768]{1,2,0:T(8,128)(2,1)S(1)}, bf16[1,384,768]{1,2,0:T(8,128)(2,1)S(1)}, u32[]{:S(2)}, u32[]{:S(2)}) %collective-permute-start.3) | collective-permute-done | bytes 589856 | tf_op jit(solution)/shard_map/ppermute | solution.py:21
  67.1 1.2 collective-permute-done.2
  68.4 0.1 convert_add_fusion
  68.5 0.1 fusion.34
  68.6 1.3 fusion.25
  69.9 0.9 copy.35
  70.8 0.2 multiply_reduce_fusion.1
  71.0 0.2 multiply_convert_fusion
  71.2 0.9 copy.34
  72.1 170.1 %all-reduce = (f32[128]{0:T(128)S(1)}, f32[128]{0:T(128)S(1)}) all-reduce(f32[128]{0:T(128)S(1)} %get-tuple-element.112, f32[128]{0:T(128)S(1)} %get-tuple-element.110), channel_id=1, replica_groups=mesh['seq'=16,'head'=4,'fsdp'=16] {'seq','head','fsdp'}, use_global_device_ids=true, to_apply=%region_13.14 | all-reduce | flops 256 | bytes 2048 | tf_op jit(solution)/shard_map/psum | solution.py:162
  242.2 0.5 broadcast_multiply_fusion.2
  (41 shorter events, 0.7 us)
Async XLA Ops:
  2.5 9.1 %copy-start.4 = (bf16[1,384,384]{2,1,0:T(8,128)(2,1)S(1)}, bf16[1,384,384]{2,1,0:T(8,128)(2,1)}, u32[]{:S(2)}) copy-start(bf16[1,384,384]{2,1,0:T(8,128)(2,1)} %param.9) | copy-start | bytes 884740
  4.7 7.2 %copy-start.8 = (s32[1,1,3]{2,1,0:T(1,128)S(1)}, s32[1,1,3]{2,1,0:T(1,128)}, u32[]{:S(2)}) copy-start(s32[1,1,3]{2,1,0:T(1,128)} %param.15) | copy-start | bytes 40
  4.7 7.8 %copy-start.5 = (bf16[1,384,384]{2,1,0:T(8,128)(2,1)S(1)}, bf16[1,384,384]{2,1,0:T(8,128)(2,1)}, u32[]{:S(2)}) copy-start(bf16[1,384,384]{2,1,0:T(8,128)(2,1)} %param.14) | copy-start | bytes 884740
  4.7 10.1 %copy-start.6 = (f32[128]{0:T(128)S(1)}, f32[128]{0:T(128)}, u32[]{:S(2)}) copy-start(f32[128]{0:T(128)} %param.12) | copy-start | bytes 1540
  5.6 17.3 %collective-permute-start.1 = (bf16[1,384,768]{1,2,0:T(8,128)(2,1)}, bf16[1,384,768]{1,2,0:T(8,128)(2,1)S(1)}, u32[]{:S(2)}, u32[]{:S(2)}) collective-permute-start(bf16[1,384,768]{1,2,0:T(8,128)(2,1)} %pad_maximum_fusion.1), channel_id=1, source_target_pairs={{64,0},{128,64},{192,128},{256,192},{320,256},{384,320},{448,384},... | collective-permute-start | bytes 1769480 | tf_op jit(solution)/shard_map/ppermute | solution.py:21
  6.9 17.3 %collective-permute-start = (bf16[1,384,768]{1,2,0:T(8,128)(2,1)}, bf16[1,384,768]{1,2,0:T(8,128)(2,1)S(1)}, u32[]{:S(2)}, u32[]{:S(2)}) collective-permute-start(bf16[1,384,768]{1,2,0:T(8,128)(2,1)} %pad_maximum_fusion.1), channel_id=1, source_target_pairs={{0,64},{64,128},{128,192},{192,256},{256,320},{320,384},{384,448},... | collective-permute-start | bytes 1769480 | tf_op jit(solution)/shard_map/ppermute | solution.py:19
  44.4 4.0 %copy-start.2 = (bf16[3,1,384,1152]{3,2,1,0:T(8,128)(2,1)S(1)}, bf16[3,1,384,1152]{3,2,1,0:T(8,128)(2,1)}, u32[]{:S(2)}) copy-start(bf16[3,1,384,1152]{3,2,1,0:T(8,128)(2,1)} %get-tuple-element.64) | copy-start | bytes 7962628
  50.3 6.6 %copy-start.3 = (f32[3,1,384,128]{2,3,0,1:T(8,128)S(1)}, f32[3,1,384,128]{2,3,0,1:T(8,128)}, u32[]{:S(2)}) copy-start(f32[3,1,384,128]{2,3,0,1:T(8,128)} %get-tuple-element.62) | copy-start | bytes 1769476
  50.4 16.7 %collective-permute-start.3 = (bf16[1,384,768]{1,2,0:T(8,128)(2,1)S(1)}, bf16[1,384,768]{1,2,0:T(8,128)(2,1)S(1)}, u32[]{:S(2)}, u32[]{:S(2)}) collective-permute-start(bf16[1,384,768]{1,2,0:T(8,128)(2,1)S(1)} %pad_maximum_fusion.3), channel_id=1, source_target_pairs={{64,0},{128,64},{192,128},{256,192},{320,256},{384,320},{448,384},... | collective-permute-start | bytes 1769480 | tf_op jit(solution)/shard_map/ppermute | solution.py:21
  51.9 16.5 %collective-permute-start.2 = (bf16[1,384,768]{1,2,0:T(8,128)(2,1)S(1)}, bf16[1,384,768]{1,2,0:T(8,128)(2,1)S(1)}, u32[]{:S(2)}, u32[]{:S(2)}) collective-permute-start(bf16[1,384,768]{1,2,0:T(8,128)(2,1)S(1)} %pad_maximum_fusion.2), channel_id=1, source_target_pairs={{0,64},{64,128},{128,192},{192,256},{256,320},{320,384},{384,448},... | collective-permute-start | bytes 1769480 | tf_op jit(solution)/shard_map/ppermute | solution.py:19
  68.5 2.3 copy-start
  68.5 2.3 copy-start.1
  68.5 2.3 copy-start.7
where the time goes:
time: 245 us; the launch traced here: 243 us
  blocking collectives  170 us (69%)
  waiting for transfers between devices  19.6 us (8%)
  matrix products  15.8 us (6%)
  starting transfers between devices  12.2 us (5%)
  local copies, waits for them, and re-layouts  11.1 us (5%)
  other arithmetic  10.9 us (4%)
  between operations  2.84 us (1%)
    psum x1, blocking collectives, per_device(): lax.psum((gain_terms[0], gain_terms[1]), ('seq', 'head', 'fsdp'))  170 us
    ppermute x2, waiting for transfers between devices, extended_2(): lax.ppermute(head, axis, [((i + 1) % count, i) for i in range(ends)])  17.1 us
    ppermute x2, starting transfers between devices, extended_2(): lax.ppermute(tail, axis, [(i, (i + 1) % count) for i in range(ends)])  9.51 us
    unnamed x26, local copies, waits for them, and re-layouts  7.39 us
  transfers between devices with their start and end apart: 4, of which 4 were waited for; matrix products, arithmetic and copies ran while one was open for 1% of the time, Pallas kernels for 0%

commit v1 on v0

--- a/solution.py
+++ b/solution.py
@@ -25,6 +25,16 @@
     return cells
 
 
+def butterfly_sum(value, axes):
+    for axis in axes:
+        count = lax.axis_size(axis)
+        step = 1
+        while step < count:
+            value = value + lax.ppermute(value, axis, [(i, i ^ step) for i in range(count)])
+            step *= 2
+    return value
+
+
 def normalize(raw_rows, gain_vector):
     shaped = raw_rows.astype(jnp.float32).reshape(
         raw_rows.shape[0], raw_rows.shape[1], -1, gain_vector.shape[0]
@@ -99,10 +109,11 @@
     head_count = columns // head_size
     score_scale = 1.0 / math.sqrt(head_size)
     q_unit, q_factor, q_norm = normalize(queries, q_gain)
-    k_unit, k_factor, k_norm = normalize(keys, k_gain)
-    packed = jnp.concatenate([k_norm.reshape(sample_count, tile_rows, columns), values], axis=2)
+    packed = jnp.concatenate([keys, values], axis=2)
     extended = extended_2(packed, (("seq", 1),), tile_rows)
-    key_all = extended[..., :columns].reshape(sample_count, 3 * tile_rows, head_count, head_size)
+    k_unit_all, k_factor_all, key_all = normalize(extended[..., :columns], k_gain)
+    k_unit = k_unit_all[:, tile_rows : 2 * tile_rows]
+    k_factor = k_factor_all[:, tile_rows : 2 * tile_rows]
     value_all = extended[..., columns:].reshape(sample_count, 3 * tile_rows, head_count, head_size)
     tile_index = lax.axis_index("seq")
     tile_count = lax.axis_size("seq")
@@ -155,11 +166,22 @@
         .reshape(sample_count, tile_rows, columns)
     )
     grad_values = grad_vsum.astype(jnp.bfloat16).reshape(sample_count, tile_rows, columns)
-    gain_terms = (
-        jnp.sum(grad_qnorm * q_unit, axis=(0, 1, 2)),
-        jnp.sum(grad_knorm * k_unit, axis=(0, 1, 2)),
-    )
-    q_total, k_total = lax.psum((gain_terms[0], gain_terms[1]), ("seq", "head", "fsdp"))
+    near_terms = jnp.concatenate(
+        [
+            left_terms[0].astype(jnp.bfloat16).astype(jnp.float32),
+            own_terms[0],
+            right_terms[0].astype(jnp.bfloat16).astype(jnp.float32),
+        ],
+        axis=1,
+    )
+    gain_terms = jnp.concatenate(
+        [
+            jnp.sum(grad_qnorm * q_unit, axis=(0, 1, 2)),
+            jnp.sum(near_terms * k_unit_all, axis=(0, 1, 2)),
+        ]
+    )
+    gain_totals = butterfly_sum(gain_terms, ("seq", "head", "fsdp"))
+    q_total, k_total = gain_totals[:head_size], gain_totals[head_size:]
     pair_count = sample_count * lax.axis_size("fsdp") * head_count * lax.axis_size("head")
     return (
         attended,

time: 245 us -> 168 us (0.69)
  blocking collectives: 170 us -> 0 us
  starting transfers between devices: 12.2 us -> 87.5 us
  waiting for transfers between devices: 19.6 us -> 33.8 us
  other arithmetic: 10.9 us -> 14.4 us
    psum x1 -> x0, blocking collectives: 170 us -> none  [per_device(): lax.psum((gain_terms[0], gain_terms[1]), ('seq', 'head', 'fsdp'))]
    ppermute x0 -> x10, starting transfers between devices: none -> 75.3 us  [butterfly_sum(): lax.ppermute(value, axis, [(i, i ^ step) for i in range(count)])]
    ppermute x0 -> x10, waiting for transfers between devices: none -> 13.3 us  [butterfly_sum(): lax.ppermute(value, axis, [(i, i ^ step) for i in range(count)])]
    unnamed x26 -> x28, local copies, waits for them, and re-layouts: 7.39 us -> 9.27 us
  transfers between devices with their start and end apart: 4 -> 14, of which waited for: 4 -> 12; matrix products, arithmetic and copies ran while one was open for 1% -> 5% of each run, Pallas kernels for 0% -> 0%
where the time goes in v1:
time: 168 us; the launch traced here: 166 us
  starting transfers between devices  87.5 us (52%)
  waiting for transfers between devices  33.8 us (20%)
  matrix products  14.5 us (9%)
  other arithmetic  14.4 us (9%)
  local copies, waits for them, and re-layouts  13.1 us (8%)
  between operations  2.97 us (2%)
    ppermute x10, starting transfers between devices, butterfly_sum(): lax.ppermute(value, axis, [(i, i ^ step) for i in range(count)])  75.3 us
    ppermute x2, waiting for transfers between devices, extended_2(): lax.ppermute(head, axis, [((i + 1) % count, i) for i in range(ends)])  18 us
    ppermute x10, waiting for transfers between devices, butterfly_sum(): lax.ppermute(value, axis, [(i, i ^ step) for i in range(count)])  13.3 us
    ppermute x2, starting transfers between devices, extended_2(): lax.ppermute(tail, axis, [(i, (i + 1) % count) for i in range(ends)])  9.53 us
    unnamed x28, local copies, waits for them, and re-layouts  9.27 us
    dot_general x3, matrix products, head_pass(): jnp.einsum('sqd,skd->sqk', grad_rows, value_rows, preferred_element_type=...  4.08 us
    dynamic_update_slice x3, other arithmetic, per_device(): lax.map(lambda per_head: head_pass(per_head, allowed, score_scale), opera...  3.73 us
  transfers between devices with their start and end apart: 14, of which 12 were waited for; matrix products, arithmetic and copies ran while one was open for 5% of the time, Pallas kernels for 0%

profile of v1, /device:TPU:24, one launch (start us, length us, event | category | flops | bytes accessed | tf_op | source)
XLA Modules:
  0.0 166.3 jit_solution(3264230014266284524)
XLA Ops:
  0.6 1.2 copy.41
  1.9 1.2 copy.42
  3.1 0.9 pad_maximum_fusion.1
  4.0 1.3 collective-permute-start.1
  5.3 4.6 %collective-permute-start = (bf16[1,384,768]{1,2,0:T(8,128)(2,1)}, bf16[1,384,768]{1,2,0:T(8,128)(2,1)S(1)}, u32[]{:S(2)}, u32[]{:S(2)}) collective-permute-start(bf16[1,384,768]{1,2,0:T(8,128)(2,1)} %pad_maximum_fusion.1), channel_id=1, source_target_pairs={{0,64},{64,128},{128,192},{192,256},{256,320},{320,384},{384,448},... | collective-permute-start | bytes 1769480 | tf_op jit(solution)/shard_map/ppermute | solution.py:19
  10.2 0.7 compare_reduce_fusion.2
  13.3 8.0 %collective-permute-done.1 = bf16[1,384,768]{1,2,0:T(8,128)(2,1)S(1)} collective-permute-done((bf16[1,384,768]{1,2,0:T(8,128)(2,1)}, bf16[1,384,768]{1,2,0:T(8,128)(2,1)S(1)}, u32[]{:S(2)}, u32[]{:S(2)}) %collective-permute-start.1) | collective-permute-done | bytes 589856 | tf_op jit(solution)/shard_map/ppermute | solution.py:21
  21.3 1.3 collective-permute-done
  23.0 1.1 copy-done
  24.2 0.5 copy-done.8
  24.7 1.5 fusion.26
  26.2 18.0 %while.17 = (s32[]{:T(128)}, bf16[3,1,384,128]{2,3,1,0:T(8,128)(2,1)}, f32[3,1,384,128]{2,3,0,1:T(8,128)}, bf16[3,1,384,1152]{3,2,1,0:T(8,128)(2,1)}, bf16[3,1,3...) while((s32[]{:T(128)}, ...), condition=%wide.region_9.10_spmd.clone, body=%wide.region_5.9_spmd.clone.sunk | while | flops 458145024 | bytes 14277640 | solution.py:136
  26.3 0.5 fusion.52
  26.8 0.4 exponential_reduce_fusion.2
  27.3 1.2 bitcast_dynamic-update-slice_fusion.6
  28.5 1.0 bitcast_dynamic-update-slice_fusion.7
  29.6 1.4 bitcast_dynamic-update-slice_fusion.8
  31.5 0.7 constant_dynamic-update-slice_fusion.2
  32.3 0.5 fusion.52
  32.8 0.4 exponential_reduce_fusion.2
  33.2 1.3 bitcast_dynamic-update-slice_fusion.6
  34.5 1.0 bitcast_dynamic-update-slice_fusion.7
  35.6 1.4 bitcast_dynamic-update-slice_fusion.8
  37.5 0.7 constant_dynamic-update-slice_fusion.2
  38.3 0.5 fusion.52
  38.8 0.4 exponential_reduce_fusion.2
  39.3 1.2 bitcast_dynamic-update-slice_fusion.6
  40.5 1.0 bitcast_dynamic-update-slice_fusion.7
  41.6 1.4 bitcast_dynamic-update-slice_fusion.8
  42.9 0.4 fusion.53
  43.5 0.7 constant_dynamic-update-slice_fusion.2
  44.2 2.6 %fusion.22 = f32[1,1152,3,128]{1,3,2,0:T(8,128)S(1)} fusion(bf16[3,1,384,1152]{3,2,1,0:T(8,128)(2,1)} %get-tuple-element.63, f32[384,3,128]{0,2,1:T(8,128)S(1)} %bitcast.142, f32[128]{0:T(128)S(1)} %copy-done.7, f32[384,3]{0,1:T(4,128)S(1)} %add_rsqrt_fusion.1), kind=kOutput, calls=%fused_computation.35 | convolution fusion | flops 340623360 | bytes 5018624 | tf_op jit(solution)/shard_map/hsqk,sqhd->skhd/dot_general | solution.py:85
  46.9 1.9 %fusion.40 = (bf16[1,1152,3,128]{1,3,2,0:T(8,128)(2,1)S(1)}, f32[1,1152,3,128]{1,3,2,0:T(8,128)}) fusion(bf16[384,3,128]{0,2,1:T(8,128)(2,1)S(1)} %bitcast.149, bf16[3,1,384,1152]{3,2,1,0:T(8,128)(2,1)S(1)} %copy-done.2), kind=kOutput, calls=%fused_computation.90 | convolution fusion | flops 340180992 | bytes 5603328 | tf_op jit(solution)/shard_map/hsqk,sqhd->skhd/dot_general | solution.py:88
  49.0 1.4 collective-permute-start.3
  50.5 4.9 %collective-permute-start.2 = (bf16[1,384,768]{1,2,0:T(8,128)(2,1)S(1)}, bf16[1,384,768]{1,2,0:T(8,128)(2,1)S(1)}, u32[]{:S(2)}, u32[]{:S(2)}) collective-permute-start(bf16[1,384,768]{1,2,0:T(8,128)(2,1)S(1)} %pad_maximum_fusion.2), channel_id=1, source_target_pairs={{0,64},{64,128},{128,192},{192,256},{256,320},{320,384},{384,448},... | collective-permute-start | bytes 1769480 | tf_op jit(solution)/shard_map/ppermute | solution.py:19
  55.8 10.0 %collective-permute-done.3 = bf16[1,384,768]{1,2,0:T(8,128)(2,1)S(1)} collective-permute-done((bf16[1,384,768]{1,2,0:T(8,128)(2,1)S(1)}, bf16[1,384,768]{1,2,0:T(8,128)(2,1)S(1)}, u32[]{:S(2)}, u32[]{:S(2)}) %collective-permute-start.3) | collective-permute-done | bytes 589856 | tf_op jit(solution)/shard_map/ppermute | solution.py:21
  65.7 1.2 collective-permute-done.2
  67.1 0.9 fusion.38
  68.0 1.4 fusion.35
  70.0 4.4 %collective-permute-start.4 = (f32[256]{0:T(256)S(1)}, f32[256]{0:T(256)S(1)}, u32[]{:S(2)}, u32[]{:S(2)}) collective-permute-start(f32[256]{0:T(256)S(1)} %pad_maximum_fusion.4), channel_id=1, source_target_pairs={{0,64},{64,0},{128,192},{192,128},{256,320},{320,256},{384,448},{4... | collective-permute-start | bytes 3080 | tf_op jit(solution)/shard_map/ppermute | solution.py:33
  74.4 1.5 collective-permute-done.4
  76.0 7.0 %collective-permute-start.5 = (f32[256]{0:T(256)S(1)}, f32[256]{0:T(256)S(1)}, u32[]{:S(2)}, u32[]{:S(2)}) collective-permute-start(f32[256]{0:T(256)S(1)} %fusion.32), channel_id=1, source_target_pairs={{0,128},{64,192},{128,0},{192,64},{256,384},{320,448},{384,256},{4... | collective-permute-start | bytes 3080 | tf_op jit(solution)/shard_map/ppermute | solution.py:33
  83.0 1.5 collective-permute-done.5
  84.5 9.4 %collective-permute-start.6 = (f32[256]{0:T(256)S(1)}, f32[256]{0:T(256)S(1)}, u32[]{:S(2)}, u32[]{:S(2)}) collective-permute-start(f32[256]{0:T(256)S(1)} %add.90), channel_id=1, source_target_pairs={{0,256},{64,320},{128,384},{192,448},{256,0},{320,64},{384,128},{4... | collective-permute-start | bytes 3080 | tf_op jit(solution)/shard_map/ppermute | solution.py:33
  93.9 1.5 collective-permute-done.6
  95.5 15.7 %collective-permute-start.7 = (f32[256]{0:T(256)S(1)}, f32[256]{0:T(256)S(1)}, u32[]{:S(2)}, u32[]{:S(2)}) collective-permute-start(f32[256]{0:T(256)S(1)} %add.91), channel_id=1, source_target_pairs={{0,512},{64,576},{128,640},{192,704},{256,768},{320,832},{384,896}... | collective-permute-start | bytes 3080 | tf_op jit(solution)/shard_map/ppermute | solution.py:33
  111.2 1.5 collective-permute-done.7
  112.7 1.9 %collective-permute-start.8 = (f32[256]{0:T(256)S(1)}, f32[256]{0:T(256)S(1)}, u32[]{:S(2)}, u32[]{:S(2)}) collective-permute-start(f32[256]{0:T(256)S(1)} %add.92), channel_id=1, source_target_pairs={{0,16},{16,0},{32,48},{48,32},{1,17},{17,1},{33,49},{49,33},{2,18}... | collective-permute-start | bytes 3080 | tf_op jit(solution)/shard_map/ppermute | solution.py:33
  114.7 1.1 collective-permute-done.8
  115.8 22.8 %collective-permute-start.9 = (f32[256]{0:T(256)S(1)}, f32[256]{0:T(256)S(1)}, u32[]{:S(2)}, u32[]{:S(2)}) collective-permute-start(f32[256]{0:T(256)S(1)} %add.93), channel_id=1, source_target_pairs={{0,32},{16,48},{32,0},{48,16},{1,33},{17,49},{33,1},{49,17},{2,34}... | collective-permute-start | bytes 3080 | tf_op jit(solution)/shard_map/ppermute | solution.py:33
  138.7 1.4 collective-permute-done.9
  140.1 2.6 %collective-permute-start.10 = (f32[256]{0:T(256)S(1)}, f32[256]{0:T(256)S(1)}, u32[]{:S(2)}, u32[]{:S(2)}) collective-permute-start(f32[256]{0:T(256)S(1)} %add.94), channel_id=1, source_target_pairs={{0,1},{1,0},{2,3},{3,2},{4,5},{5,4},{6,7},{7,6},{8,9},{9,8},{10,11... | collective-permute-start | bytes 3080 | tf_op jit(solution)/shard_map/ppermute | solution.py:33
  142.7 1.8 %copy.50 = bf16[1,384,384]{2,1,0:T(8,128)(2,1)} copy(bf16[1,384,384]{1,2,0:T(8,128)(2,1)} %bitcast.14) | data formatting | bytes 589824
  144.6 0.9 copy.51
  145.5 3.1 %collective-permute-start.11 = (f32[256]{0:T(256)S(1)}, f32[256]{0:T(256)S(1)}, u32[]{:S(2)}, u32[]{:S(2)}) collective-permute-start(f32[256]{0:T(256)S(1)} %add.95), channel_id=1, source_target_pairs={{0,2},{1,3},{2,0},{3,1},{4,6},{5,7},{6,4},{7,5},{8,10},{9,11},{10,... | collective-permute-start | bytes 3080 | tf_op jit(solution)/shard_map/ppermute | solution.py:33
  148.7 3.8 %collective-permute-done.11 = f32[256]{0:T(256)S(1)} collective-permute-done((f32[256]{0:T(256)S(1)}, f32[256]{0:T(256)S(1)}, u32[]{:S(2)}, u32[]{:S(2)}) %collective-permute-start.11) | collective-permute-done | bytes 1056 | tf_op jit(solution)/shard_map/ppermute | solution.py:33
  152.5 3.4 %collective-permute-start.12 = (f32[256]{0:T(256)S(1)}, f32[256]{0:T(256)S(1)}, u32[]{:S(2)}, u32[]{:S(2)}) collective-permute-start(f32[256]{0:T(256)S(1)} %add.96), channel_id=1, source_target_pairs={{0,4},{1,5},{2,6},{3,7},{4,0},{5,1},{6,2},{7,3},{8,12},{9,13},{10,... | collective-permute-start | bytes 3080 | tf_op jit(solution)/shard_map/ppermute | solution.py:33
  155.9 1.2 multiply_convert_fusion.1
  157.1 0.8 collective-permute-done.12
  158.0 4.9 %collective-permute-start.13 = (f32[256]{0:T(256)S(1)}, f32[256]{0:T(256)S(1)}, u32[]{:S(2)}, u32[]{:S(2)}) collective-permute-start(f32[256]{0:T(256)S(1)} %add.97), channel_id=1, source_target_pairs={{0,8},{1,9},{2,10},{3,11},{4,12},{5,13},{6,14},{7,15},{8,0},{9,1},... | collective-permute-start | bytes 3080 | tf_op jit(solution)/shard_map/ppermute | solution.py:33
  162.9 1.1 fusion.27
  164.0 0.9 copy.53
  164.9 0.9 copy.52
  165.8 0.5 slice_multiply_fusion
  (77 shorter events, 4.4 us)
Async XLA Ops:
  0.6 9.2 %copy-start.5 = (bf16[1,384,384]{2,1,0:T(8,128)(2,1)S(1)}, bf16[1,384,384]{2,1,0:T(8,128)(2,1)}, u32[]{:S(2)}) copy-start(bf16[1,384,384]{2,1,0:T(8,128)(2,1)} %param.9) | copy-start | bytes 884740
  3.0 7.2 %copy-start.9 = (s32[1,1,3]{2,1,0:T(1,128)S(1)}, s32[1,1,3]{2,1,0:T(1,128)}, u32[]{:S(2)}) copy-start(s32[1,1,3]{2,1,0:T(1,128)} %param.15) | copy-start | bytes 40
  3.0 7.8 %copy-start.6 = (bf16[1,384,384]{2,1,0:T(8,128)(2,1)S(1)}, bf16[1,384,384]{2,1,0:T(8,128)(2,1)}, u32[]{:S(2)}) copy-start(bf16[1,384,384]{2,1,0:T(8,128)(2,1)} %param.14) | copy-start | bytes 884740
  3.1 10.1 %copy-start.7 = (f32[128]{0:T(128)S(1)}, f32[128]{0:T(128)}, u32[]{:S(2)}) copy-start(f32[128]{0:T(128)} %param.12) | copy-start | bytes 1540
  4.0 17.3 %collective-permute-start.1 = (bf16[1,384,768]{1,2,0:T(8,128)(2,1)}, bf16[1,384,768]{1,2,0:T(8,128)(2,1)S(1)}, u32[]{:S(2)}, u32[]{:S(2)}) collective-permute-start(bf16[1,384,768]{1,2,0:T(8,128)(2,1)} %pad_maximum_fusion.1), channel_id=1, source_target_pairs={{64,0},{128,64},{192,128},{256,192},{320,256},{384,320},{448,384},... | collective-permute-start | bytes 1769480 | tf_op jit(solution)/shard_map/ppermute | solution.py:21
  5.3 17.3 %collective-permute-start = (bf16[1,384,768]{1,2,0:T(8,128)(2,1)}, bf16[1,384,768]{1,2,0:T(8,128)(2,1)S(1)}, u32[]{:S(2)}, u32[]{:S(2)}) collective-permute-start(bf16[1,384,768]{1,2,0:T(8,128)(2,1)} %pad_maximum_fusion.1), channel_id=1, source_target_pairs={{0,64},{64,128},{128,192},{192,256},{256,320},{320,384},{384,448},... | collective-permute-start | bytes 1769480 | tf_op jit(solution)/shard_map/ppermute | solution.py:19
  22.8 1.3 copy-start
  24.1 0.7 copy-start.8
  44.2 2.7 %copy-start.2 = (bf16[3,1,384,1152]{3,2,1,0:T(8,128)(2,1)S(1)}, bf16[3,1,384,1152]{3,2,1,0:T(8,128)(2,1)}, u32[]{:S(2)}) copy-start(bf16[3,1,384,1152]{3,2,1,0:T(8,128)(2,1)} %get-tuple-element.64) | copy-start | bytes 7962628
  49.0 6.6 %copy-start.3 = (f32[3,1,384,128]{2,3,0,1:T(8,128)S(1)}, f32[3,1,384,128]{2,3,0,1:T(8,128)}, u32[]{:S(2)}) copy-start(f32[3,1,384,128]{2,3,0,1:T(8,128)} %get-tuple-element.62) | copy-start | bytes 1769476
  49.0 16.8 %collective-permute-start.3 = (bf16[1,384,768]{1,2,0:T(8,128)(2,1)S(1)}, bf16[1,384,768]{1,2,0:T(8,128)(2,1)S(1)}, u32[]{:S(2)}, u32[]{:S(2)}) collective-permute-start(bf16[1,384,768]{1,2,0:T(8,128)(2,1)S(1)} %pad_maximum_fusion.3), channel_id=1, source_target_pairs={{64,0},{128,64},{192,128},{256,192},{320,256},{384,320},{448,384},... | collective-permute-start | bytes 1769480 | tf_op jit(solution)/shard_map/ppermute | solution.py:21
  50.5 16.5 %collective-permute-start.2 = (bf16[1,384,768]{1,2,0:T(8,128)(2,1)S(1)}, bf16[1,384,768]{1,2,0:T(8,128)(2,1)S(1)}, u32[]{:S(2)}, u32[]{:S(2)}) collective-permute-start(bf16[1,384,768]{1,2,0:T(8,128)(2,1)S(1)} %pad_maximum_fusion.2), channel_id=1, source_target_pairs={{0,64},{64,128},{128,192},{192,256},{256,320},{320,384},{384,448},... | collective-permute-start | bytes 1769480 | tf_op jit(solution)/shard_map/ppermute | solution.py:19
  68.0 1.7 copy-start.1
  70.0 5.9 %collective-permute-start.4 = (f32[256]{0:T(256)S(1)}, f32[256]{0:T(256)S(1)}, u32[]{:S(2)}, u32[]{:S(2)}) collective-permute-start(f32[256]{0:T(256)S(1)} %pad_maximum_fusion.4), channel_id=1, source_target_pairs={{0,64},{64,0},{128,192},{192,128},{256,320},{320,256},{384,448},{4... | collective-permute-start | bytes 3080 | tf_op jit(solution)/shard_map/ppermute | solution.py:33
  76.0 8.6 %collective-permute-start.5 = (f32[256]{0:T(256)S(1)}, f32[256]{0:T(256)S(1)}, u32[]{:S(2)}, u32[]{:S(2)}) collective-permute-start(f32[256]{0:T(256)S(1)} %fusion.32), channel_id=1, source_target_pairs={{0,128},{64,192},{128,0},{192,64},{256,384},{320,448},{384,256},{4... | collective-permute-start | bytes 3080 | tf_op jit(solution)/shard_map/ppermute | solution.py:33
  84.5 10.9 %collective-permute-start.6 = (f32[256]{0:T(256)S(1)}, f32[256]{0:T(256)S(1)}, u32[]{:S(2)}, u32[]{:S(2)}) collective-permute-start(f32[256]{0:T(256)S(1)} %add.90), channel_id=1, source_target_pairs={{0,256},{64,320},{128,384},{192,448},{256,0},{320,64},{384,128},{4... | collective-permute-start | bytes 3080 | tf_op jit(solution)/shard_map/ppermute | solution.py:33
  95.5 17.3 %collective-permute-start.7 = (f32[256]{0:T(256)S(1)}, f32[256]{0:T(256)S(1)}, u32[]{:S(2)}, u32[]{:S(2)}) collective-permute-start(f32[256]{0:T(256)S(1)} %add.91), channel_id=1, source_target_pairs={{0,512},{64,576},{128,640},{192,704},{256,768},{320,832},{384,896}... | collective-permute-start | bytes 3080 | tf_op jit(solution)/shard_map/ppermute | solution.py:33
  112.7 3.0 %collective-permute-start.8 = (f32[256]{0:T(256)S(1)}, f32[256]{0:T(256)S(1)}, u32[]{:S(2)}, u32[]{:S(2)}) collective-permute-start(f32[256]{0:T(256)S(1)} %add.92), channel_id=1, source_target_pairs={{0,16},{16,0},{32,48},{48,32},{1,17},{17,1},{33,49},{49,33},{2,18}... | collective-permute-start | bytes 3080 | tf_op jit(solution)/shard_map/ppermute | solution.py:33
  115.8 24.3 %collective-permute-start.9 = (f32[256]{0:T(256)S(1)}, f32[256]{0:T(256)S(1)}, u32[]{:S(2)}, u32[]{:S(2)}) collective-permute-start(f32[256]{0:T(256)S(1)} %add.93), channel_id=1, source_target_pairs={{0,32},{16,48},{32,0},{48,16},{1,33},{17,49},{33,1},{49,17},{2,34}... | collective-permute-start | bytes 3080 | tf_op jit(solution)/shard_map/ppermute | solution.py:33
  138.7 24.2 %copy-start.4 = (f32[1,384,384]{1,2,0:T(8,128)S(1)}, f32[1,384,384]{1,2,0:T(8,128)}, u32[]{:S(2)}) copy-start(f32[1,384,384]{1,2,0:T(8,128)} %get-tuple-element.177) | copy-start | bytes 1769476
  140.1 5.5 %collective-permute-start.10 = (f32[256]{0:T(256)S(1)}, f32[256]{0:T(256)S(1)}, u32[]{:S(2)}, u32[]{:S(2)}) collective-permute-start(f32[256]{0:T(256)S(1)} %add.94), channel_id=1, source_target_pairs={{0,1},{1,0},{2,3},{3,2},{4,5},{5,4},{6,7},{7,6},{8,9},{9,8},{10,11... | collective-permute-start | bytes 3080 | tf_op jit(solution)/shard_map/ppermute | solution.py:33
  145.5 7.0 %collective-permute-start.11 = (f32[256]{0:T(256)S(1)}, f32[256]{0:T(256)S(1)}, u32[]{:S(2)}, u32[]{:S(2)}) collective-permute-start(f32[256]{0:T(256)S(1)} %add.95), channel_id=1, source_target_pairs={{0,2},{1,3},{2,0},{3,1},{4,6},{5,7},{6,4},{7,5},{8,10},{9,11},{10,... | collective-permute-start | bytes 3080 | tf_op jit(solution)/shard_map/ppermute | solution.py:33
  152.5 5.5 %collective-permute-start.12 = (f32[256]{0:T(256)S(1)}, f32[256]{0:T(256)S(1)}, u32[]{:S(2)}, u32[]{:S(2)}) collective-permute-start(f32[256]{0:T(256)S(1)} %add.96), channel_id=1, source_target_pairs={{0,4},{1,5},{2,6},{3,7},{4,0},{5,1},{6,2},{7,3},{8,12},{9,13},{10,... | collective-permute-start | bytes 3080 | tf_op jit(solution)/shard_map/ppermute | solution.py:33
  158.0 7.9 %collective-permute-start.13 = (f32[256]{0:T(256)S(1)}, f32[256]{0:T(256)S(1)}, u32[]{:S(2)}, u32[]{:S(2)}) collective-permute-start(f32[256]{0:T(256)S(1)} %add.97), channel_id=1, source_target_pairs={{0,8},{1,9},{2,10},{3,11},{4,12},{5,13},{6,14},{7,15},{8,0},{9,1},... | collective-permute-start | bytes 3080 | tf_op jit(solution)/shard_map/ppermute | solution.py:33

commit v2 on v1

--- a/solution.py
+++ b/solution.py
@@ -133,7 +133,7 @@
         jnp.moveaxis(value_all, 2, 0),
         jnp.moveaxis(grad_out, 2, 0),
     )
-    results = lax.map(lambda per_head: head_pass(per_head, allowed, score_scale), operands)
+    results = jax.vmap(lambda per_head: head_pass(per_head, allowed, score_scale))(operands)
     attended, log_total, row_inner, grad_query, attn_weights, grad_scores = results
     attended = jnp.moveaxis(attended, 0, 2).reshape(sample_count, tile_rows, columns)
     grad_qnorm = jnp.moveaxis(grad_query, 0, 2)

time: 168 us -> 153 us (0.911)
  matrix products: 14.5 us -> 7.47 us
  other arithmetic: 14.4 us -> 10.3 us
  local copies, waits for them, and re-layouts: 13.1 us -> 10 us
    ppermute x2, waiting for transfers between devices: 2.54 us -> 10.2 us  [extended_2(): lax.ppermute(tail, axis, [(i, (i + 1) % count) for i in range(ends)])]
    ppermute x2, waiting for transfers between devices: 18 us -> 12.2 us  [extended_2(): lax.ppermute(head, axis, [((i + 1) % count, i) for i in range(ends)])]
    dynamic_update_slice x3 -> x0, other arithmetic: 3.73 us -> none  [per_device(): lax.map(lambda per_head: head_pass(per_head, allowed, score_scale), opera...]
    dot_general x3 -> x1, matrix products: 4.08 us -> 0.96 us  [head_pass(): jnp.einsum('sqd,skd->sqk', grad_rows, value_rows, preferred_element_type=...]
    dynamic_update_slice x6 -> x0, local copies, waits for them, and re-layouts: 2.51 us -> none  [per_device(): lax.map(lambda per_head: head_pass(per_head, allowed, score_scale), opera...]
    dot_general x1, matrix products: 2.63 us -> 0.76 us  [key_terms(): jnp.einsum('hsqk,sqhd->skhd', grad_scores, query_norm, preferred_element_...]
    unnamed x28 -> x24, local copies, waits for them, and re-layouts: 9.27 us -> 8.87 us
  transfers between devices with their start and end apart: 14 -> 14, of which waited for: 12 -> 12; matrix products, arithmetic and copies ran while one was open for 5% -> 8% of each run, Pallas kernels for 0% -> 0%
where the time goes in v2:
time: 153 us; the launch traced here: 151 us
  starting transfers between devices  86 us (56%)
  waiting for transfers between devices  34.5 us (23%)
  other arithmetic  10.3 us (7%)
  local copies, waits for them, and re-layouts  10 us (7%)
  matrix products  7.47 us (5%)
  between operations  2.97 us (2%)
    ppermute x10, starting transfers between devices, butterfly_sum(): lax.ppermute(value, axis, [(i, i ^ step) for i in range(count)])  74.4 us
    ppermute x2, waiting for transfers between devices, extended_2(): lax.ppermute(head, axis, [((i + 1) % count, i) for i in range(ends)])  12.2 us
    ppermute x10, waiting for transfers between devices, butterfly_sum(): lax.ppermute(value, axis, [(i, i ^ step) for i in range(count)])  12.1 us
    ppermute x2, waiting for transfers between devices, extended_2(): lax.ppermute(tail, axis, [(i, (i + 1) % count) for i in range(ends)])  10.2 us
    ppermute x2, starting transfers between devices, extended_2(): lax.ppermute(tail, axis, [(i, (i + 1) % count) for i in range(ends)])  9 us
    unnamed x24, local copies, waits for them, and re-layouts  8.87 us
  transfers between devices with their start and end apart: 14, of which 12 were waited for; matrix products, arithmetic and copies ran while one was open for 8% of the time, Pallas kernels for 0%

profile of v2, /device:TPU:24, one launch (start us, length us, event | category | flops | bytes accessed | tf_op | source)
XLA Modules:
  0.0 151.3 jit_solution(12019476929403576211)
XLA Ops:
  0.7 1.2 copy.47
  1.9 1.2 copy.48
  3.1 0.1 pad_maximum_fusion.1
  3.1 1.3 collective-permute-start.1
  4.4 4.6 %collective-permute-start = (bf16[1,384,768]{1,2,0:T(8,128)(2,1)S(1)}, bf16[1,384,768]{1,2,0:T(8,128)(2,1)S(1)}, u32[]{:S(2)}, u32[]{:S(2)}) collective-permute-start(bf16[1,384,768]{1,2,0:T(8,128)(2,1)S(1)} %pad_maximum_fusion.1), channel_id=1, source_target_pairs={{0,64},{64,128},{128,192},{192,256},{256,320},{320,384},{384,448},... | collective-permute-start | bytes 1769480 | tf_op jit(solution)/shard_map/ppermute | solution.py:19
  9.1 0.7 compare_reduce_fusion.2
  11.7 0.1 add_bitcast_fusion
  11.8 0.1 broadcast_in_dim.16
  11.9 0.2 copy.51
  12.1 0.2 copy.46
  12.4 7.9 %collective-permute-done.1 = bf16[1,384,768]{1,2,0:T(8,128)(2,1)S(1)} collective-permute-done((bf16[1,384,768]{1,2,0:T(8,128)(2,1)S(1)}, bf16[1,384,768]{1,2,0:T(8,128)(2,1)S(1)}, u32[]{:S(2)}, u32[]{:S(2)}) %collective-permute-start.1) | collective-permute-done | bytes 589856 | tf_op jit(solution)/shard_map/ppermute | solution.py:21
  20.3 1.2 collective-permute-done
  21.5 0.2 pad_maximum_fusion
  21.6 0.2 fusion.18
  21.8 0.1 multiply_reduce_fusion
  22.0 0.1 broadcast_multiply_fusion
  22.1 0.5 copy-done.5
  22.7 1.2 fusion.21
  23.8 1.2 exponential_reduce_fusion
  25.0 1.0 exponential_convert_fusion
  26.0 1.9 %fusion.22 = (bf16[1,1152,3,128]{1,3,2,0:T(8,128)(2,1)S(1)}, f32[1,1152,3,128]{1,3,2,0:T(8,128)}) fusion(bf16[384,3,128]{0,2,1:T(8,128)(2,1)S(1)} %bitcast.103, bf16[3,384,1152]{2,1,0:T(8,128)(2,1)S(1)} %exponential_convert_fusion), kind=kOutput, calls=%fused_computation.65 | convolution fusion | flops 340180992 | bytes 5603328 | tf_op jit(solution)/shard_map/hsqk,sqhd->skhd/dot_general | solution.py:88
  28.0 1.6 %multiply_reduce_fusion.4 = (f32[3,384]{1,0:T(4,128)S(1)}, bf16[3,384,128]{1,2,0:T(8,128)(2,1)}) fusion(bf16[3,1,384,128]{2,3,0,1:T(8,128)(2,1)S(1)} %bitcast.104, bf16[3,384,1152]{2,1,0:T(8,128)(2,1)S(1)} %exponential_convert_fusion, bf16[3,1152,128]{1,2,0:T(8,128)(2,1)S(1)} %bitcast.97), kind=kOutput, calls=%fused_computation.35 | convolution fusion | flops 340474752 | bytes 4133376 | tf_op jit(solution)/shard_map/vmap(sqk,skd->sqd)/dot_general | solution.py:64
  29.6 1.0 fusion
  30.6 0.8 fusion.1
  31.3 0.1 fusion.17
  31.4 0.1 pad_maximum_fusion.2
  31.5 4.4 %collective-permute-start.2 = (bf16[1,384,768]{1,2,0:T(8,128)(2,1)S(1)}, bf16[1,384,768]{1,2,0:T(8,128)(2,1)S(1)}, u32[]{:S(2)}, u32[]{:S(2)}) collective-permute-start(bf16[1,384,768]{1,2,0:T(8,128)(2,1)S(1)} %pad_maximum_fusion.2), channel_id=1, source_target_pairs={{0,64},{64,128},{128,192},{192,256},{256,320},{320,384},{384,448},... | collective-permute-start | bytes 1769480 | tf_op jit(solution)/shard_map/ppermute | solution.py:19
  35.9 0.1 pad_maximum_fusion.3
  36.0 1.3 collective-permute-start.3
  37.4 1.0 multiply_reduce_fusion.1
  38.4 9.1 %collective-permute-done.2 = bf16[1,384,768]{1,2,0:T(8,128)(2,1)S(1)} collective-permute-done((bf16[1,384,768]{1,2,0:T(8,128)(2,1)S(1)}, bf16[1,384,768]{1,2,0:T(8,128)(2,1)S(1)}, u32[]{:S(2)}, u32[]{:S(2)}) %collective-permute-start.2) | collective-permute-done | bytes 589856 | tf_op jit(solution)/shard_map/ppermute | solution.py:19
  47.5 4.4 %collective-permute-done.3 = bf16[1,384,768]{1,2,0:T(8,128)(2,1)S(1)} collective-permute-done((bf16[1,384,768]{1,2,0:T(8,128)(2,1)S(1)}, bf16[1,384,768]{1,2,0:T(8,128)(2,1)S(1)}, u32[]{:S(2)}, u32[]{:S(2)}) %collective-permute-start.3) | collective-permute-done | bytes 589856 | tf_op jit(solution)/shard_map/ppermute | solution.py:21
  51.8 0.1 convert_add_fusion
  51.9 0.9 fusion.19
  52.9 0.2 fusion.16
  53.0 0.3 fusion.2
  53.4 4.5 %collective-permute-start.4 = (f32[256]{0:T(256)S(1)}, f32[256]{0:T(256)S(1)}, u32[]{:S(2)}, u32[]{:S(2)}) collective-permute-start(f32[256]{0:T(256)S(1)} %pad_maximum_fusion.4), channel_id=1, source_target_pairs={{0,64},{64,0},{128,192},{192,128},{256,320},{320,256},{384,448},{4... | collective-permute-start | bytes 3080 | tf_op jit(solution)/shard_map/ppermute | solution.py:33
  57.9 1.5 %collective-permute-done.4 = f32[256]{0:T(256)S(1)} collective-permute-done((f32[256]{0:T(256)S(1)}, f32[256]{0:T(256)S(1)}, u32[]{:S(2)}, u32[]{:S(2)}) %collective-permute-start.4) | collective-permute-done | bytes 1056 | tf_op jit(solution)/shard_map/ppermute | solution.py:33
  59.4 8.0 %collective-permute-start.5 = (f32[256]{0:T(256)S(1)}, f32[256]{0:T(256)S(1)}, u32[]{:S(2)}, u32[]{:S(2)}) collective-permute-start(f32[256]{0:T(256)S(1)} %fusion.12), channel_id=1, source_target_pairs={{0,128},{64,192},{128,0},{192,64},{256,384},{320,448},{384,256},{4... | collective-permute-start | bytes 3080 | tf_op jit(solution)/shard_map/ppermute | solution.py:33
  67.4 1.5 %collective-permute-done.5 = f32[256]{0:T(256)S(1)} collective-permute-done((f32[256]{0:T(256)S(1)}, f32[256]{0:T(256)S(1)}, u32[]{:S(2)}, u32[]{:S(2)}) %collective-permute-start.5) | collective-permute-done | bytes 1056 | tf_op jit(solution)/shard_map/ppermute | solution.py:33
  68.9 9.1 %collective-permute-start.6 = (f32[256]{0:T(256)S(1)}, f32[256]{0:T(256)S(1)}, u32[]{:S(2)}, u32[]{:S(2)}) collective-permute-start(f32[256]{0:T(256)S(1)} %add.88), channel_id=1, source_target_pairs={{0,256},{64,320},{128,384},{192,448},{256,0},{320,64},{384,128},{4... | collective-permute-start | bytes 3080 | tf_op jit(solution)/shard_map/ppermute | solution.py:33
  78.0 1.5 %collective-permute-done.6 = f32[256]{0:T(256)S(1)} collective-permute-done((f32[256]{0:T(256)S(1)}, f32[256]{0:T(256)S(1)}, u32[]{:S(2)}, u32[]{:S(2)}) %collective-permute-start.6) | collective-permute-done | bytes 1056 | tf_op jit(solution)/shard_map/ppermute | solution.py:33
  79.6 14.4 %collective-permute-start.7 = (f32[256]{0:T(256)S(1)}, f32[256]{0:T(256)S(1)}, u32[]{:S(2)}, u32[]{:S(2)}) collective-permute-start(f32[256]{0:T(256)S(1)} %add.89), channel_id=1, source_target_pairs={{0,512},{64,576},{128,640},{192,704},{256,768},{320,832},{384,896}... | collective-permute-start | bytes 3080 | tf_op jit(solution)/shard_map/ppermute | solution.py:33
  94.0 1.5 %collective-permute-done.7 = f32[256]{0:T(256)S(1)} collective-permute-done((f32[256]{0:T(256)S(1)}, f32[256]{0:T(256)S(1)}, u32[]{:S(2)}, u32[]{:S(2)}) %collective-permute-start.7) | collective-permute-done | bytes 1056 | tf_op jit(solution)/shard_map/ppermute | solution.py:33
  95.5 1.9 %collective-permute-start.8 = (f32[256]{0:T(256)S(1)}, f32[256]{0:T(256)S(1)}, u32[]{:S(2)}, u32[]{:S(2)}) collective-permute-start(f32[256]{0:T(256)S(1)} %add.90), channel_id=1, source_target_pairs={{0,16},{16,0},{32,48},{48,32},{1,17},{17,1},{33,49},{49,33},{2,18}... | collective-permute-start | bytes 3080 | tf_op jit(solution)/shard_map/ppermute | solution.py:33
  97.5 1.1 collective-permute-done.8
  98.6 22.8 %collective-permute-start.9 = (f32[256]{0:T(256)S(1)}, f32[256]{0:T(256)S(1)}, u32[]{:S(2)}, u32[]{:S(2)}) collective-permute-start(f32[256]{0:T(256)S(1)} %add.91), channel_id=1, source_target_pairs={{0,32},{16,48},{32,0},{48,16},{1,33},{17,49},{33,1},{49,17},{2,34}... | collective-permute-start | bytes 3080 | tf_op jit(solution)/shard_map/ppermute | solution.py:33
  121.4 0.9 multiply_convert_fusion.3
  122.2 0.7 collective-permute-done.9
  122.9 0.5 add.92
  123.4 2.6 %collective-permute-start.10 = (f32[256]{0:T(256)}, f32[256]{0:T(256)}, u32[]{:S(2)}, u32[]{:S(2)}) collective-permute-start(f32[256]{0:T(256)} %add.92), channel_id=1, source_target_pairs={{0,1},{1,0},{2,3},{3,2},{4,5},{5,4},{6,7},{7,6},{8,9},{9,8},{10,11... | collective-permute-start | bytes 3080 | tf_op jit(solution)/shard_map/ppermute | solution.py:33
  126.1 1.8 %copy.56 = bf16[1,384,384]{2,1,0:T(8,128)(2,1)} copy(bf16[1,384,384]{1,2,0:T(8,128)(2,1)} %bitcast.113) | data formatting | bytes 589824
  127.9 1.8 %copy.57 = bf16[1,384,384]{2,1,0:T(8,128)(2,1)} copy(bf16[1,384,384]{1,2,0:T(8,128)(2,1)} %bitcast.109) | data formatting | bytes 589824
  129.8 0.7 add.93
  130.5 2.8 %collective-permute-start.11 = (f32[256]{0:T(256)S(1)}, f32[256]{0:T(256)S(1)}, u32[]{:S(2)}, u32[]{:S(2)}) collective-permute-start(f32[256]{0:T(256)S(1)} %add.93), channel_id=1, source_target_pairs={{0,2},{1,3},{2,0},{3,1},{4,6},{5,7},{6,4},{7,5},{8,10},{9,11},{10,... | collective-permute-start | bytes 3080 | tf_op jit(solution)/shard_map/ppermute | solution.py:33
  133.3 4.1 %collective-permute-done.11 = f32[256]{0:T(256)S(1)} collective-permute-done((f32[256]{0:T(256)S(1)}, f32[256]{0:T(256)S(1)}, u32[]{:S(2)}, u32[]{:S(2)}) %collective-permute-start.11) | collective-permute-done | bytes 1056 | tf_op jit(solution)/shard_map/ppermute | solution.py:33
  137.5 3.4 %collective-permute-start.12 = (f32[256]{0:T(256)S(1)}, f32[256]{0:T(256)S(1)}, u32[]{:S(2)}, u32[]{:S(2)}) collective-permute-start(f32[256]{0:T(256)S(1)} %add.94), channel_id=1, source_target_pairs={{0,4},{1,5},{2,6},{3,7},{4,0},{5,1},{6,2},{7,3},{8,12},{9,13},{10,... | collective-permute-start | bytes 3080 | tf_op jit(solution)/shard_map/ppermute | solution.py:33
  140.8 2.0 %multiply_convert_fusion.1 = bf16[1,384,3,128]{1,3,2,0:T(8,128)(2,1)} fusion(f32[1,1152,3,128]{1,3,2,0:T(8,128)S(1)} %broadcast_multiply_fusion, f32[384,3]{0,1:T(4,128)S(1)} %broadcast_multiply_fusion.1, f32[384,3]{0,1:T(4,128)S(1)} %slice_bitcast_fusion, f32[128]{0:T(128)} %param.11, f32[1,384,3,128]{1,3,2,0:T(8,128)} %bitcast.96, ...), kind=kLoop, calls=%fused_computation.29 | loop fusion | flops 884736 | bytes 2074112 | tf_op jit(solution)/shard_map/convert_element_type | solution.py:165
  142.8 0.1 collective-permute-done.12
  142.9 4.9 %collective-permute-start.13 = (f32[256]{0:T(256)S(1)}, f32[256]{0:T(256)S(1)}, u32[]{:S(2)}, u32[]{:S(2)}) collective-permute-start(f32[256]{0:T(256)S(1)} %add.95), channel_id=1, source_target_pairs={{0,8},{1,9},{2,10},{3,11},{4,12},{5,13},{6,14},{7,15},{8,0},{9,1},... | collective-permute-start | bytes 3080 | tf_op jit(solution)/shard_map/ppermute | solution.py:33
  147.9 1.1 fusion.5
  149.0 0.9 copy.59
  149.9 0.9 copy.58
  150.8 0.5 slice_multiply_fusion
  (39 shorter events, 0.4 us)
Async XLA Ops:
  0.6 8.4 %copy-start.7 = (s32[1,1,3]{2,1,0:T(1,128)S(1)}, s32[1,1,3]{2,1,0:T(1,128)}, u32[]{:S(2)}) copy-start(s32[1,1,3]{2,1,0:T(1,128)} %param.13) | copy-start | bytes 40
  0.6 11.2 %copy-start.3 = (bf16[1,384,384]{2,1,0:T(8,128)(2,1)S(1)}, bf16[1,384,384]{2,1,0:T(8,128)(2,1)}, u32[]{:S(2)}) copy-start(bf16[1,384,384]{2,1,0:T(8,128)(2,1)} %param.12) | copy-start | bytes 884740
  0.7 11.4 %copy-start.4 = (bf16[1,384,384]{2,1,0:T(8,128)(2,1)S(1)}, bf16[1,384,384]{2,1,0:T(8,128)(2,1)}, u32[]{:S(2)}) copy-start(bf16[1,384,384]{2,1,0:T(8,128)(2,1)} %param.7) | copy-start | bytes 884740
  3.1 17.1 %collective-permute-start.1 = (bf16[1,384,768]{1,2,0:T(8,128)(2,1)S(1)}, bf16[1,384,768]{1,2,0:T(8,128)(2,1)S(1)}, u32[]{:S(2)}, u32[]{:S(2)}) collective-permute-start(bf16[1,384,768]{1,2,0:T(8,128)(2,1)S(1)} %pad_maximum_fusion.1), channel_id=1, source_target_pairs={{64,0},{128,64},{192,128},{256,192},{320,256},{384,320},{448,384},... | collective-permute-start | bytes 1769480 | tf_op jit(solution)/shard_map/ppermute | solution.py:21
  4.4 17.0 %collective-permute-start = (bf16[1,384,768]{1,2,0:T(8,128)(2,1)S(1)}, bf16[1,384,768]{1,2,0:T(8,128)(2,1)S(1)}, u32[]{:S(2)}, u32[]{:S(2)}) collective-permute-start(bf16[1,384,768]{1,2,0:T(8,128)(2,1)S(1)} %pad_maximum_fusion.1), channel_id=1, source_target_pairs={{0,64},{64,128},{128,192},{192,256},{256,320},{320,384},{384,448},... | collective-permute-start | bytes 1769480 | tf_op jit(solution)/shard_map/ppermute | solution.py:19
  22.0 0.7 copy-start.5
  22.0 0.7 copy-start.6
  31.5 16.0 %collective-permute-start.2 = (bf16[1,384,768]{1,2,0:T(8,128)(2,1)S(1)}, bf16[1,384,768]{1,2,0:T(8,128)(2,1)S(1)}, u32[]{:S(2)}, u32[]{:S(2)}) collective-permute-start(bf16[1,384,768]{1,2,0:T(8,128)(2,1)S(1)} %pad_maximum_fusion.2), channel_id=1, source_target_pairs={{0,64},{64,128},{128,192},{192,256},{256,320},{320,384},{384,448},... | collective-permute-start | bytes 1769480 | tf_op jit(solution)/shard_map/ppermute | solution.py:19
  36.0 15.9 %collective-permute-start.3 = (bf16[1,384,768]{1,2,0:T(8,128)(2,1)S(1)}, bf16[1,384,768]{1,2,0:T(8,128)(2,1)S(1)}, u32[]{:S(2)}, u32[]{:S(2)}) collective-permute-start(bf16[1,384,768]{1,2,0:T(8,128)(2,1)S(1)} %pad_maximum_fusion.3), channel_id=1, source_target_pairs={{64,0},{128,64},{192,128},{256,192},{320,256},{384,320},{448,384},... | collective-permute-start | bytes 1769480 | tf_op jit(solution)/shard_map/ppermute | solution.py:21
  52.9 69.4 %copy-start = (f32[1,384,384]{1,2,0:T(8,128)}, f32[1,384,384]{1,2,0:T(8,128)S(1)}, u32[]{:S(2)}) copy-start(f32[1,384,384]{1,2,0:T(8,128)S(1)} %get-tuple-element.36) | copy-start | bytes 1769476
  53.4 6.0 %collective-permute-start.4 = (f32[256]{0:T(256)S(1)}, f32[256]{0:T(256)S(1)}, u32[]{:S(2)}, u32[]{:S(2)}) collective-permute-start(f32[256]{0:T(256)S(1)} %pad_maximum_fusion.4), channel_id=1, source_target_pairs={{0,64},{64,0},{128,192},{192,128},{256,320},{320,256},{384,448},{4... | collective-permute-start | bytes 3080 | tf_op jit(solution)/shard_map/ppermute | solution.py:33
  59.4 9.5 %collective-permute-start.5 = (f32[256]{0:T(256)S(1)}, f32[256]{0:T(256)S(1)}, u32[]{:S(2)}, u32[]{:S(2)}) collective-permute-start(f32[256]{0:T(256)S(1)} %fusion.12), channel_id=1, source_target_pairs={{0,128},{64,192},{128,0},{192,64},{256,384},{320,448},{384,256},{4... | collective-permute-start | bytes 3080 | tf_op jit(solution)/shard_map/ppermute | solution.py:33
  68.9 10.6 %collective-permute-start.6 = (f32[256]{0:T(256)S(1)}, f32[256]{0:T(256)S(1)}, u32[]{:S(2)}, u32[]{:S(2)}) collective-permute-start(f32[256]{0:T(256)S(1)} %add.88), channel_id=1, source_target_pairs={{0,256},{64,320},{128,384},{192,448},{256,0},{320,64},{384,128},{4... | collective-permute-start | bytes 3080 | tf_op jit(solution)/shard_map/ppermute | solution.py:33
  79.6 16.0 %collective-permute-start.7 = (f32[256]{0:T(256)S(1)}, f32[256]{0:T(256)S(1)}, u32[]{:S(2)}, u32[]{:S(2)}) collective-permute-start(f32[256]{0:T(256)S(1)} %add.89), channel_id=1, source_target_pairs={{0,512},{64,576},{128,640},{192,704},{256,768},{320,832},{384,896}... | collective-permute-start | bytes 3080 | tf_op jit(solution)/shard_map/ppermute | solution.py:33
  95.5 3.0 %collective-permute-start.8 = (f32[256]{0:T(256)S(1)}, f32[256]{0:T(256)S(1)}, u32[]{:S(2)}, u32[]{:S(2)}) collective-permute-start(f32[256]{0:T(256)S(1)} %add.90), channel_id=1, source_target_pairs={{0,16},{16,0},{32,48},{48,32},{1,17},{17,1},{33,49},{49,33},{2,18}... | collective-permute-start | bytes 3080 | tf_op jit(solution)/shard_map/ppermute | solution.py:33
  98.6 24.3 %collective-permute-start.9 = (f32[256]{0:T(256)S(1)}, f32[256]{0:T(256)S(1)}, u32[]{:S(2)}, u32[]{:S(2)}) collective-permute-start(f32[256]{0:T(256)S(1)} %add.91), channel_id=1, source_target_pairs={{0,32},{16,48},{32,0},{48,16},{1,33},{17,49},{33,1},{49,17},{2,34}... | collective-permute-start | bytes 3080 | tf_op jit(solution)/shard_map/ppermute | solution.py:33
  123.4 6.4 %collective-permute-start.10 = (f32[256]{0:T(256)}, f32[256]{0:T(256)}, u32[]{:S(2)}, u32[]{:S(2)}) collective-permute-start(f32[256]{0:T(256)} %add.92), channel_id=1, source_target_pairs={{0,1},{1,0},{2,3},{3,2},{4,5},{5,4},{6,7},{7,6},{8,9},{9,8},{10,11... | collective-permute-start | bytes 3080 | tf_op jit(solution)/shard_map/ppermute | solution.py:33
  129.8 18.1 %copy-start.1 = (f32[1,384,384]{1,2,0:T(8,128)S(1)}, f32[1,384,384]{1,2,0:T(8,128)}, u32[]{:S(2)}) copy-start(f32[1,384,384]{1,2,0:T(8,128)} %get-tuple-element.35) | copy-start | bytes 1769476
  130.5 7.0 %collective-permute-start.11 = (f32[256]{0:T(256)S(1)}, f32[256]{0:T(256)S(1)}, u32[]{:S(2)}, u32[]{:S(2)}) collective-permute-start(f32[256]{0:T(256)S(1)} %add.93), channel_id=1, source_target_pairs={{0,2},{1,3},{2,0},{3,1},{4,6},{5,7},{6,4},{7,5},{8,10},{9,11},{10,... | collective-permute-start | bytes 3080 | tf_op jit(solution)/shard_map/ppermute | solution.py:33
  137.5 5.5 %collective-permute-start.12 = (f32[256]{0:T(256)S(1)}, f32[256]{0:T(256)S(1)}, u32[]{:S(2)}, u32[]{:S(2)}) collective-permute-start(f32[256]{0:T(256)S(1)} %add.94), channel_id=1, source_target_pairs={{0,4},{1,5},{2,6},{3,7},{4,0},{5,1},{6,2},{7,3},{8,12},{9,13},{10,... | collective-permute-start | bytes 3080 | tf_op jit(solution)/shard_map/ppermute | solution.py:33
  142.8 7.1 %copy-start.2 = (bf16[1,384,3,128]{1,3,2,0:T(8,128)(2,1)S(1)}, bf16[1,384,3,128]{1,3,2,0:T(8,128)(2,1)}, u32[]{:S(2)}) copy-start(bf16[1,384,3,128]{1,3,2,0:T(8,128)(2,1)} %multiply_convert_fusion.1) | copy-start | bytes 884740
  142.9 7.9 %collective-permute-start.13 = (f32[256]{0:T(256)S(1)}, f32[256]{0:T(256)S(1)}, u32[]{:S(2)}, u32[]{:S(2)}) collective-permute-start(f32[256]{0:T(256)S(1)} %add.95), channel_id=1, source_target_pairs={{0,8},{1,9},{2,10},{3,11},{4,12},{5,13},{6,14},{7,15},{8,0},{9,1},... | collective-permute-start | bytes 3080 | tf_op jit(solution)/shard_map/ppermute | solution.py:33

commit v3 on v2

--- a/solution.py
+++ b/solution.py
@@ -145,27 +145,11 @@
         [pack_terms(left_terms[0], left_terms[1]), pack_terms(right_terms[0], right_terms[1])],
         axis=1,
     )
-    returned = extended_2(outgoing, (("seq", 1),), tile_rows)
-    incoming = returned[:, :tile_rows].astype(jnp.float32) + returned[:, 3 * tile_rows :].astype(
-        jnp.float32
-    )
-    grad_knorm = own_terms[0] + incoming[..., :columns].reshape(
-        sample_count, tile_rows, head_count, head_size
-    )
-    grad_vsum = own_terms[1] + incoming[..., columns:].reshape(
-        sample_count, tile_rows, head_count, head_size
-    )
     grad_queries = (
         restore(grad_qnorm, q_unit, q_factor, q_gain)
         .astype(jnp.bfloat16)
         .reshape(sample_count, tile_rows, columns)
     )
-    grad_keys = (
-        restore(grad_knorm, k_unit, k_factor, k_gain)
-        .astype(jnp.bfloat16)
-        .reshape(sample_count, tile_rows, columns)
-    )
-    grad_values = grad_vsum.astype(jnp.bfloat16).reshape(sample_count, tile_rows, columns)
     near_terms = jnp.concatenate(
         [
             left_terms[0].astype(jnp.bfloat16).astype(jnp.float32),
@@ -181,6 +165,23 @@
         ]
     )
     gain_totals = butterfly_sum(gain_terms, ("seq", "head", "fsdp"))
+    returned = extended_2(outgoing, (("seq", 1),), tile_rows)
+    returned, gain_totals = lax.optimization_barrier((returned, gain_totals))
+    incoming = returned[:, :tile_rows].astype(jnp.float32) + returned[:, 3 * tile_rows :].astype(
+        jnp.float32
+    )
+    grad_knorm = own_terms[0] + incoming[..., :columns].reshape(
+        sample_count, tile_rows, head_count, head_size
+    )
+    grad_vsum = own_terms[1] + incoming[..., columns:].reshape(
+        sample_count, tile_rows, head_count, head_size
+    )
+    grad_keys = (
+        restore(grad_knorm, k_unit, k_factor, k_gain)
+        .astype(jnp.bfloat16)
+        .reshape(sample_count, tile_rows, columns)
+    )
+    grad_values = grad_vsum.astype(jnp.bfloat16).reshape(sample_count, tile_rows, columns)
     q_total, k_total = gain_totals[:head_size], gain_totals[head_size:]
     pair_count = sample_count * lax.axis_size("fsdp") * head_count * lax.axis_size("head")
     return (

time: 153 us -> 148 us (0.967)
  waiting for transfers between devices: 34.5 us -> 19.6 us
  other arithmetic: 10.3 us -> 17 us
  local copies, waits for them, and re-layouts: 10 us -> 11.8 us
    ppermute x2, waiting for transfers between devices: 10.2 us -> 1.18 us  [extended_2(): lax.ppermute(tail, axis, [(i, (i + 1) % count) for i in range(ends)])]
    ppermute x2, waiting for transfers between devices: 12.2 us -> 7.84 us  [extended_2(): lax.ppermute(head, axis, [((i + 1) % count, i) for i in range(ends)])]
    concatenate x1 -> x2, other arithmetic: 0.15 us -> 3.48 us  [extended_2(): jnp.concatenate([lax.ppermute(tail, axis, [(i, (i + 1) % count) for i in...]
    unnamed x24 -> x32, local copies, waits for them, and re-layouts: 8.87 us -> 10.6 us
    concatenate x2, other arithmetic: 0.12 us -> 1.75 us  [pack_terms(): jnp.concatenate([key_part.reshape(sample_count, tile_rows, -1), value_par...]
    ppermute x10, waiting for transfers between devices: 12.1 us -> 10.6 us  [butterfly_sum(): lax.ppermute(value, axis, [(i, i ^ step) for i in range(count)])]
  transfers between devices with their start and end apart: 14 -> 14, of which waited for: 12 -> 9; matrix products, arithmetic and copies ran while one was open for 8% -> 7% of each run, Pallas kernels for 0% -> 0%
where the time goes in v3:
time: 148 us; the launch traced here: 146 us
  starting transfers between devices  86.8 us (59%)
  waiting for transfers between devices  19.6 us (13%)
  other arithmetic  17 us (11%)
  local copies, waits for them, and re-layouts  11.8 us (8%)
  matrix products  7.49 us (5%)
  between operations  3.04 us (2%)
    ppermute x10, starting transfers between devices, butterfly_sum(): lax.ppermute(value, axis, [(i, i ^ step) for i in range(count)])  74.9 us
    unnamed x32, local copies, waits for them, and re-layouts  10.6 us
    ppermute x10, waiting for transfers between devices, butterfly_sum(): lax.ppermute(value, axis, [(i, i ^ step) for i in range(count)])  10.6 us
    ppermute x2, starting transfers between devices, extended_2(): lax.ppermute(tail, axis, [(i, (i + 1) % count) for i in range(ends)])  9.32 us
    ppermute x2, waiting for transfers between devices, extended_2(): lax.ppermute(head, axis, [((i + 1) % count, i) for i in range(ends)])  7.84 us
    concatenate x2, other arithmetic, extended_2(): jnp.concatenate([lax.ppermute(tail, axis, [(i, (i + 1) % count) for i in...  3.48 us
  transfers between devices with their start and end apart: 14, of which 9 were waited for; matrix products, arithmetic and copies ran while one was open for 7% of the time, Pallas kernels for 0%

profile of v3, /device:TPU:24, one launch (start us, length us, event | category | flops | bytes accessed | tf_op | source)
XLA Modules:
  0.0 145.6 jit_solution(5804464015076487268)
XLA Ops:
  0.7 1.2 copy.47
  1.9 1.2 copy.48
  3.1 0.1 pad_maximum_fusion.2
  3.1 1.3 collective-permute-start.1
  4.4 4.6 %collective-permute-start = (bf16[1,384,768]{1,2,0:T(8,128)(2,1)S(1)}, bf16[1,384,768]{1,2,0:T(8,128)(2,1)S(1)}, u32[]{:S(2)}, u32[]{:S(2)}) collective-permute-start(bf16[1,384,768]{1,2,0:T(8,128)(2,1)S(1)} %pad_maximum_fusion.2), channel_id=1, source_target_pairs={{0,64},{64,128},{128,192},{192,256},{256,320},{320,384},{384,448},... | collective-permute-start | bytes 1769480 | tf_op jit(solution)/shard_map/ppermute | solution.py:19
  9.1 0.7 compare_reduce_fusion.2
  11.7 0.1 add_bitcast_fusion
  11.8 0.1 broadcast_in_dim.16
  11.9 0.2 copy.51
  12.1 0.2 copy.46
  12.4 0.1 multiply_reduce_fusion.5
  12.4 7.8 %collective-permute-done.1 = bf16[1,384,768]{1,2,0:T(8,128)(2,1)S(1)} collective-permute-done((bf16[1,384,768]{1,2,0:T(8,128)(2,1)S(1)}, bf16[1,384,768]{1,2,0:T(8,128)(2,1)S(1)}, u32[]{:S(2)}, u32[]{:S(2)}) %collective-permute-start.1) | collective-permute-done | bytes 589856 | tf_op jit(solution)/shard_map/ppermute | solution.py:21
  20.3 1.2 collective-permute-done
  21.5 0.2 pad_maximum_fusion.1
  21.6 0.2 fusion.17
  21.8 0.1 multiply_reduce_fusion
  22.0 0.1 broadcast_multiply_fusion
  22.1 0.3 copy-done.8
  22.5 0.0 copy-done.9
  22.5 1.2 fusion.20
  23.7 1.2 exponential_reduce_fusion
  24.8 1.0 exponential_convert_fusion
  25.8 1.6 %multiply_reduce_fusion.4 = (f32[3,384]{1,0:T(4,128)S(1)}, bf16[3,384,128]{1,2,0:T(8,128)(2,1)}) fusion(bf16[3,1,384,128]{2,3,0,1:T(8,128)(2,1)S(1)} %bitcast.109, bf16[3,384,1152]{2,1,0:T(8,128)(2,1)S(1)} %exponential_convert_fusion, bf16[3,1152,128]{1,2,0:T(8,128)(2,1)S(1)} %bitcast.103), kind=kOutput, calls=%fused_computation.36 | convolution fusion | flops 340474752 | bytes 4133376 | tf_op jit(solution)/shard_map/vmap(sqk,skd->sqd)/dot_general | solution.py:64
  27.4 1.0 fusion
  28.4 1.0 multiply_reduce_fusion.2
  29.4 0.8 fusion.1
  30.3 0.1 fusion.16
  30.5 0.3 fusion.2
  30.8 4.4 %collective-permute-start.4 = (f32[256]{0:T(256)S(1)}, f32[256]{0:T(256)S(1)}, u32[]{:S(2)}, u32[]{:S(2)}) collective-permute-start(f32[256]{0:T(256)S(1)} %pad_maximum_fusion.5), channel_id=1, source_target_pairs={{0,64},{64,0},{128,192},{192,128},{256,320},{320,256},{384,448},{4... | collective-permute-start | bytes 3080 | tf_op jit(solution)/shard_map/ppermute | solution.py:33
  35.2 1.5 %collective-permute-done.4 = f32[256]{0:T(256)S(1)} collective-permute-done((f32[256]{0:T(256)S(1)}, f32[256]{0:T(256)S(1)}, u32[]{:S(2)}, u32[]{:S(2)}) %collective-permute-start.4) | collective-permute-done | bytes 1056 | tf_op jit(solution)/shard_map/ppermute | solution.py:33
  36.8 5.8 %collective-permute-start.5 = (f32[256]{0:T(256)S(1)}, f32[256]{0:T(256)S(1)}, u32[]{:S(2)}, u32[]{:S(2)}) collective-permute-start(f32[256]{0:T(256)S(1)} %fusion.12), channel_id=1, source_target_pairs={{0,128},{64,192},{128,0},{192,64},{256,384},{320,448},{384,256},{4... | collective-permute-start | bytes 3080 | tf_op jit(solution)/shard_map/ppermute | solution.py:33
  42.6 1.5 %collective-permute-done.5 = f32[256]{0:T(256)S(1)} collective-permute-done((f32[256]{0:T(256)S(1)}, f32[256]{0:T(256)S(1)}, u32[]{:S(2)}, u32[]{:S(2)}) %collective-permute-start.5) | collective-permute-done | bytes 1056 | tf_op jit(solution)/shard_map/ppermute | solution.py:33
  44.1 9.4 %collective-permute-start.6 = (f32[256]{0:T(256)S(1)}, f32[256]{0:T(256)S(1)}, u32[]{:S(2)}, u32[]{:S(2)}) collective-permute-start(f32[256]{0:T(256)S(1)} %add.85), channel_id=1, source_target_pairs={{0,256},{64,320},{128,384},{192,448},{256,0},{320,64},{384,128},{4... | collective-permute-start | bytes 3080 | tf_op jit(solution)/shard_map/ppermute | solution.py:33
  53.5 1.5 %collective-permute-done.6 = f32[256]{0:T(256)S(1)} collective-permute-done((f32[256]{0:T(256)S(1)}, f32[256]{0:T(256)S(1)}, u32[]{:S(2)}, u32[]{:S(2)}) %collective-permute-start.6) | collective-permute-done | bytes 1056 | tf_op jit(solution)/shard_map/ppermute | solution.py:33
  55.1 15.7 %collective-permute-start.7 = (f32[256]{0:T(256)S(1)}, f32[256]{0:T(256)S(1)}, u32[]{:S(2)}, u32[]{:S(2)}) collective-permute-start(f32[256]{0:T(256)S(1)} %add.86), channel_id=1, source_target_pairs={{0,512},{64,576},{128,640},{192,704},{256,768},{320,832},{384,896}... | collective-permute-start | bytes 3080 | tf_op jit(solution)/shard_map/ppermute | solution.py:33
  70.8 1.9 %fusion.21 = (bf16[1,1152,3,128]{1,3,2,0:T(8,128)(2,1)S(1)}, f32[1,1152,3,128]{1,3,2,0:T(8,128)}) fusion(bf16[384,3,128]{0,2,1:T(8,128)(2,1)S(1)} %bitcast.111, bf16[3,384,1152]{2,1,0:T(8,128)(2,1)S(1)} %exponential_convert_fusion), kind=kOutput, calls=%fused_computation.65 | convolution fusion | flops 340180992 | bytes 5603328 | tf_op jit(solution)/shard_map/hsqk,sqhd->skhd/dot_general | solution.py:88
  72.7 1.9 %collective-permute-start.8 = (f32[256]{0:T(256)S(1)}, f32[256]{0:T(256)S(1)}, u32[]{:S(2)}, u32[]{:S(2)}) collective-permute-start(f32[256]{0:T(256)S(1)} %add.87), channel_id=1, source_target_pairs={{0,16},{16,0},{32,48},{48,32},{1,17},{17,1},{33,49},{49,33},{2,18}... | collective-permute-start | bytes 3080 | tf_op jit(solution)/shard_map/ppermute | solution.py:33
  74.6 0.1 fusion.19
  74.7 1.0 collective-permute-done.8
  75.8 22.7 %collective-permute-start.9 = (f32[256]{0:T(256)S(1)}, f32[256]{0:T(256)S(1)}, u32[]{:S(2)}, u32[]{:S(2)}) collective-permute-start(f32[256]{0:T(256)S(1)} %add.88), channel_id=1, source_target_pairs={{0,32},{16,48},{32,0},{48,16},{1,33},{17,49},{33,1},{49,17},{2,34}... | collective-permute-start | bytes 3080 | tf_op jit(solution)/shard_map/ppermute | solution.py:33
  98.5 0.9 pad_maximum_fusion.4
  99.4 0.6 collective-permute-done.9
  100.0 2.6 %collective-permute-start.10 = (f32[256]{0:T(256)S(1)}, f32[256]{0:T(256)S(1)}, u32[]{:S(2)}, u32[]{:S(2)}) collective-permute-start(f32[256]{0:T(256)S(1)} %add.89), channel_id=1, source_target_pairs={{0,1},{1,0},{2,3},{3,2},{4,5},{5,4},{6,7},{7,6},{8,9},{9,8},{10,11... | collective-permute-start | bytes 3080 | tf_op jit(solution)/shard_map/ppermute | solution.py:33
  102.7 0.9 pad_maximum_fusion.3
  103.5 4.7 %collective-permute-start.2 = (bf16[1,384,768]{1,2,0:T(8,128)(2,1)}, bf16[1,384,768]{1,2,0:T(8,128)(2,1)}, u32[]{:S(2)}, u32[]{:S(2)}) collective-permute-start(bf16[1,384,768]{1,2,0:T(8,128)(2,1)} %pad_maximum_fusion.3), channel_id=1, source_target_pairs={{0,64},{64,128},{128,192},{192,256},{256,320},{320,384},{384,448},... | collective-permute-start | bytes 1769480 | tf_op jit(solution)/shard_map/ppermute | solution.py:19
  108.3 1.3 collective-permute-start.3
  109.6 3.9 %collective-permute-start.11 = (f32[256]{0:T(256)S(1)}, f32[256]{0:T(256)S(1)}, u32[]{:S(2)}, u32[]{:S(2)}) collective-permute-start(f32[256]{0:T(256)S(1)} %add.90), channel_id=1, source_target_pairs={{0,2},{1,3},{2,0},{3,1},{4,6},{5,7},{6,4},{7,5},{8,10},{9,11},{10,... | collective-permute-start | bytes 3080 | tf_op jit(solution)/shard_map/ppermute | solution.py:33
  113.5 3.1 %collective-permute-done.11 = f32[256]{0:T(256)S(1)} collective-permute-done((f32[256]{0:T(256)S(1)}, f32[256]{0:T(256)S(1)}, u32[]{:S(2)}, u32[]{:S(2)}) %collective-permute-start.11) | collective-permute-done | bytes 1056 | tf_op jit(solution)/shard_map/ppermute | solution.py:33
  116.6 3.4 %collective-permute-start.12 = (f32[256]{0:T(256)S(1)}, f32[256]{0:T(256)S(1)}, u32[]{:S(2)}, u32[]{:S(2)}) collective-permute-start(f32[256]{0:T(256)S(1)} %add.91), channel_id=1, source_target_pairs={{0,4},{1,5},{2,6},{3,7},{4,0},{5,1},{6,2},{7,3},{8,12},{9,13},{10,... | collective-permute-start | bytes 3080 | tf_op jit(solution)/shard_map/ppermute | solution.py:33
  120.0 0.9 multiply_convert_fusion.3
  120.8 1.2 collective-permute-done.12
  122.0 5.1 %collective-permute-start.13 = (f32[256]{0:T(256)S(1)}, f32[256]{0:T(256)}, u32[]{:S(2)}, u32[]{:S(2)}) collective-permute-start(f32[256]{0:T(256)S(1)} %add.92), channel_id=1, source_target_pairs={{0,8},{1,9},{2,10},{3,11},{4,12},{5,13},{6,14},{7,15},{8,0},{9,1},... | collective-permute-start | bytes 3080 | tf_op jit(solution)/shard_map/ppermute | solution.py:33
  127.1 1.8 %copy.56 = bf16[1,384,384]{2,1,0:T(8,128)(2,1)} copy(bf16[1,384,384]{1,2,0:T(8,128)(2,1)} %bitcast.117) | data formatting | bytes 589824
  129.0 1.8 %copy.57 = bf16[1,384,384]{2,1,0:T(8,128)(2,1)} copy(bf16[1,384,384]{1,2,0:T(8,128)(2,1)} %bitcast.115) | data formatting | bytes 589824
  130.8 1.2 add.93
  132.0 3.3 %pad_maximum_fusion = bf16[1,1536,768]{1,2,0:T(8,128)(2,1)S(1)} fusion(bf16[1,384,768]{1,2,0:T(8,128)(2,1)} %collective-permute-done.3, bf16[1,384,384]{1,2,0:T(8,128)(2,1)} %bitcast.106, bf16[1,384,384]{1,2,0:T(8,128)(2,1)} %bitcast.99, bf16[1,384,384]{1,2,0:T(8,128)(2,1)} %bitcast.108, bf16[1,384,384]{1,2,0:T(8,128)(2,1)} %bitcast.102, ...), kind=kLoop, calls=%fused_computation.8 | loop fusion | flops 14155776 | bytes 4718592 | tf_op jit(solution)/shard_map/concatenate | solution.py:17
  135.4 0.1 convert_add_fusion
  135.5 0.9 fusion.18
  136.4 1.8 %fusion.5 = bf16[1,384,3,128]{1,3,2,0:T(8,128)(2,1)} fusion(f32[1,384,3,128]{1,3,2,0:T(8,128)S(1)} %bitcast.113, f32[1,1152,3,128]{1,3,2,0:T(8,128)} %get-tuple-element.51), kind=kLoop, calls=%fused_computation.23 | loop fusion | flops 294912 | bytes 1474560 | tf_op jit(solution)/shard_map/convert_element_type | solution.py:184
  138.3 1.8 %copy.59 = bf16[1,384,384]{2,1,0:T(8,128)(2,1)} copy(bf16[1,384,384]{1,2,0:T(8,128)(2,1)} %bitcast.116) | data formatting | bytes 589824
  140.1 0.5 slice_multiply_fusion
  140.6 1.2 multiply_reduce_fusion.1
  141.8 1.9 %multiply_convert_fusion.1 = bf16[1,384,3,128]{1,3,2,0:T(8,128)(2,1)} fusion(f32[1,1152,3,128]{1,3,2,0:T(8,128)S(1)} %broadcast_multiply_fusion, f32[384,3]{0,1:T(4,128)S(1)} %broadcast_multiply_fusion.1, f32[384,3]{0,1:T(4,128)S(1)} %slice_bitcast_fusion, f32[128]{0:T(128)S(1)} %copy-done.9, f32[1,384,3,128]{1,3,2,0:T(8,128)} %bitcast.96, ...), kind=kLoop, calls=%fused_computation.29 | loop fusion | flops 884736 | bytes 2074112 | tf_op jit(solution)/shard_map/convert_element_type | solution.py:181
  143.8 1.8 %copy.58 = bf16[1,384,384]{2,1,0:T(8,128)(2,1)} copy(bf16[1,384,384]{1,2,0:T(8,128)(2,1)} %bitcast.114) | data formatting | bytes 589824
  (49 shorter events, 0.4 us)
Async XLA Ops:
  0.6 8.4 %copy-start.11 = (s32[1,1,3]{2,1,0:T(1,128)S(1)}, s32[1,1,3]{2,1,0:T(1,128)}, u32[]{:S(2)}) copy-start(s32[1,1,3]{2,1,0:T(1,128)} %param.13) | copy-start | bytes 40
  0.6 11.2 %copy-start.6 = (bf16[1,384,384]{2,1,0:T(8,128)(2,1)S(1)}, bf16[1,384,384]{2,1,0:T(8,128)(2,1)}, u32[]{:S(2)}) copy-start(bf16[1,384,384]{2,1,0:T(8,128)(2,1)} %param.12) | copy-start | bytes 884740
  0.7 11.4 %copy-start.7 = (bf16[1,384,384]{2,1,0:T(8,128)(2,1)S(1)}, bf16[1,384,384]{2,1,0:T(8,128)(2,1)}, u32[]{:S(2)}) copy-start(bf16[1,384,384]{2,1,0:T(8,128)(2,1)} %param.7) | copy-start | bytes 884740
  3.1 17.1 %collective-permute-start.1 = (bf16[1,384,768]{1,2,0:T(8,128)(2,1)S(1)}, bf16[1,384,768]{1,2,0:T(8,128)(2,1)S(1)}, u32[]{:S(2)}, u32[]{:S(2)}) collective-permute-start(bf16[1,384,768]{1,2,0:T(8,128)(2,1)S(1)} %pad_maximum_fusion.2), channel_id=1, source_target_pairs={{64,0},{128,64},{192,128},{256,192},{320,256},{384,320},{448,384},... | collective-permute-start | bytes 1769480 | tf_op jit(solution)/shard_map/ppermute | solution.py:21
  4.4 17.0 %collective-permute-start = (bf16[1,384,768]{1,2,0:T(8,128)(2,1)S(1)}, bf16[1,384,768]{1,2,0:T(8,128)(2,1)S(1)}, u32[]{:S(2)}, u32[]{:S(2)}) collective-permute-start(bf16[1,384,768]{1,2,0:T(8,128)(2,1)S(1)} %pad_maximum_fusion.2), channel_id=1, source_target_pairs={{0,64},{64,128},{128,192},{192,256},{256,320},{320,384},{384,448},... | collective-permute-start | bytes 1769480 | tf_op jit(solution)/shard_map/ppermute | solution.py:19
  12.1 15.3 %copy-start.4 = (bf16[1,384,384]{1,2,0:T(8,128)(2,1)}, bf16[1,384,384]{1,2,0:T(8,128)(2,1)S(1)}, u32[]{:S(2)}) copy-start(bf16[1,384,384]{1,2,0:T(8,128)(2,1)S(1)} %copy.51) | copy-start | bytes 884740
  21.8 0.7 copy-start.8
  21.8 0.7 copy-start.9
  30.3 68.1 %copy-start.1 = (bf16[1,384,3,128]{1,3,2,0:T(8,128)(2,1)}, bf16[1,384,3,128]{1,3,2,0:T(8,128)(2,1)S(1)}, u32[]{:S(2)}) copy-start(bf16[1,384,3,128]{1,3,2,0:T(8,128)(2,1)S(1)} %get-tuple-element.34) | copy-start | bytes 884740
  30.4 72.3 %copy-start = (bf16[1,384,3,128]{1,3,2,0:T(8,128)(2,1)}, bf16[1,384,3,128]{1,3,2,0:T(8,128)(2,1)S(1)}, u32[]{:S(2)}) copy-start(bf16[1,384,3,128]{1,3,2,0:T(8,128)(2,1)S(1)} %get-tuple-element.33) | copy-start | bytes 884740
  30.4 40.4 %copy-start.5 = (bf16[1,384,384]{1,2,0:T(8,128)(2,1)S(1)}, bf16[1,384,384]{1,2,0:T(8,128)(2,1)}, u32[]{:S(2)}) copy-start(bf16[1,384,384]{1,2,0:T(8,128)(2,1)} %copy-done.4) | copy-start | bytes 884740
  30.8 5.9 %collective-permute-start.4 = (f32[256]{0:T(256)S(1)}, f32[256]{0:T(256)S(1)}, u32[]{:S(2)}, u32[]{:S(2)}) collective-permute-start(f32[256]{0:T(256)S(1)} %pad_maximum_fusion.5), channel_id=1, source_target_pairs={{0,64},{64,0},{128,192},{192,128},{256,320},{320,256},{384,448},{4... | collective-permute-start | bytes 3080 | tf_op jit(solution)/shard_map/ppermute | solution.py:33
  36.8 7.4 %collective-permute-start.5 = (f32[256]{0:T(256)S(1)}, f32[256]{0:T(256)S(1)}, u32[]{:S(2)}, u32[]{:S(2)}) collective-permute-start(f32[256]{0:T(256)S(1)} %fusion.12), channel_id=1, source_target_pairs={{0,128},{64,192},{128,0},{192,64},{256,384},{320,448},{384,256},{4... | collective-permute-start | bytes 3080 | tf_op jit(solution)/shard_map/ppermute | solution.py:33
  44.1 10.9 %collective-permute-start.6 = (f32[256]{0:T(256)S(1)}, f32[256]{0:T(256)S(1)}, u32[]{:S(2)}, u32[]{:S(2)}) collective-permute-start(f32[256]{0:T(256)S(1)} %add.85), channel_id=1, source_target_pairs={{0,256},{64,320},{128,384},{192,448},{256,0},{320,64},{384,128},{4... | collective-permute-start | bytes 3080 | tf_op jit(solution)/shard_map/ppermute | solution.py:33
  55.1 17.7 %collective-permute-start.7 = (f32[256]{0:T(256)S(1)}, f32[256]{0:T(256)S(1)}, u32[]{:S(2)}, u32[]{:S(2)}) collective-permute-start(f32[256]{0:T(256)S(1)} %add.86), channel_id=1, source_target_pairs={{0,512},{64,576},{128,640},{192,704},{256,768},{320,832},{384,896}... | collective-permute-start | bytes 3080 | tf_op jit(solution)/shard_map/ppermute | solution.py:33
  72.7 3.0 %collective-permute-start.8 = (f32[256]{0:T(256)S(1)}, f32[256]{0:T(256)S(1)}, u32[]{:S(2)}, u32[]{:S(2)}) collective-permute-start(f32[256]{0:T(256)S(1)} %add.87), channel_id=1, source_target_pairs={{0,16},{16,0},{32,48},{48,32},{1,17},{17,1},{33,49},{49,33},{2,18}... | collective-permute-start | bytes 3080 | tf_op jit(solution)/shard_map/ppermute | solution.py:33
  74.7 46.1 %copy-start.2 = (bf16[1,384,3,128]{1,3,2,0:T(8,128)(2,1)}, bf16[1,384,3,128]{1,3,2,0:T(8,128)(2,1)S(1)}, u32[]{:S(2)}) copy-start(bf16[1,384,3,128]{1,3,2,0:T(8,128)(2,1)S(1)} %get-tuple-element.39) | copy-start | bytes 884740
  74.7 47.3 %copy-start.3 = (bf16[1,384,3,128]{1,3,2,0:T(8,128)(2,1)}, bf16[1,384,3,128]{1,3,2,0:T(8,128)(2,1)S(1)}, u32[]{:S(2)}) copy-start(bf16[1,384,3,128]{1,3,2,0:T(8,128)(2,1)S(1)} %get-tuple-element.40) | copy-start | bytes 884740
  75.8 24.3 %collective-permute-start.9 = (f32[256]{0:T(256)S(1)}, f32[256]{0:T(256)S(1)}, u32[]{:S(2)}, u32[]{:S(2)}) collective-permute-start(f32[256]{0:T(256)S(1)} %add.88), channel_id=1, source_target_pairs={{0,32},{16,48},{32,0},{48,16},{1,33},{17,49},{33,1},{49,17},{2,34}... | collective-permute-start | bytes 3080 | tf_op jit(solution)/shard_map/ppermute | solution.py:33
  100.0 9.6 %collective-permute-start.10 = (f32[256]{0:T(256)S(1)}, f32[256]{0:T(256)S(1)}, u32[]{:S(2)}, u32[]{:S(2)}) collective-permute-start(f32[256]{0:T(256)S(1)} %add.89), channel_id=1, source_target_pairs={{0,1},{1,0},{2,3},{3,2},{4,5},{5,4},{6,7},{7,6},{8,9},{9,8},{10,11... | collective-permute-start | bytes 3080 | tf_op jit(solution)/shard_map/ppermute | solution.py:33
  103.5 28.5 %collective-permute-start.2 = (bf16[1,384,768]{1,2,0:T(8,128)(2,1)}, bf16[1,384,768]{1,2,0:T(8,128)(2,1)}, u32[]{:S(2)}, u32[]{:S(2)}) collective-permute-start(bf16[1,384,768]{1,2,0:T(8,128)(2,1)} %pad_maximum_fusion.3), channel_id=1, source_target_pairs={{0,64},{64,128},{128,192},{192,256},{256,320},{320,384},{384,448},... | collective-permute-start | bytes 1769480 | tf_op jit(solution)/shard_map/ppermute | solution.py:19
  108.3 23.7 %collective-permute-start.3 = (bf16[1,384,768]{1,2,0:T(8,128)(2,1)}, bf16[1,384,768]{1,2,0:T(8,128)(2,1)}, u32[]{:S(2)}, u32[]{:S(2)}) collective-permute-start(bf16[1,384,768]{1,2,0:T(8,128)(2,1)} %pad_maximum_fusion.4), channel_id=1, source_target_pairs={{64,0},{128,64},{192,128},{256,192},{320,256},{384,320},{448,384},... | collective-permute-start | bytes 1769480 | tf_op jit(solution)/shard_map/ppermute | solution.py:21
  109.6 7.0 %collective-permute-start.11 = (f32[256]{0:T(256)S(1)}, f32[256]{0:T(256)S(1)}, u32[]{:S(2)}, u32[]{:S(2)}) collective-permute-start(f32[256]{0:T(256)S(1)} %add.90), channel_id=1, source_target_pairs={{0,2},{1,3},{2,0},{3,1},{4,6},{5,7},{6,4},{7,5},{8,10},{9,11},{10,... | collective-permute-start | bytes 3080 | tf_op jit(solution)/shard_map/ppermute | solution.py:33
  116.6 5.5 %collective-permute-start.12 = (f32[256]{0:T(256)S(1)}, f32[256]{0:T(256)S(1)}, u32[]{:S(2)}, u32[]{:S(2)}) collective-permute-start(f32[256]{0:T(256)S(1)} %add.91), channel_id=1, source_target_pairs={{0,4},{1,5},{2,6},{3,7},{4,0},{5,1},{6,2},{7,3},{8,12},{9,13},{10,... | collective-permute-start | bytes 3080 | tf_op jit(solution)/shard_map/ppermute | solution.py:33
  122.0 8.8 %collective-permute-start.13 = (f32[256]{0:T(256)S(1)}, f32[256]{0:T(256)}, u32[]{:S(2)}, u32[]{:S(2)}) collective-permute-start(f32[256]{0:T(256)S(1)} %add.92), channel_id=1, source_target_pairs={{0,8},{1,9},{2,10},{3,11},{4,12},{5,13},{6,14},{7,15},{8,0},{9,1},... | collective-permute-start | bytes 3080 | tf_op jit(solution)/shard_map/ppermute | solution.py:33
  135.5 4.6 %copy-start.10 = (f32[256]{0:T(256)S(1)}, f32[256]{0:T(256)}, u32[]{:S(2)}) copy-start(f32[256]{0:T(256)} %add.93) | copy-start | bytes 3076

commit v4 on v3

--- a/solution.py
+++ b/solution.py
@@ -141,10 +141,6 @@
     left_terms = (key_every[:, :tile_rows], value_every[:, :tile_rows])
     own_terms = (key_every[:, tile_rows : 2 * tile_rows], value_every[:, tile_rows : 2 * tile_rows])
     right_terms = (key_every[:, 2 * tile_rows :], value_every[:, 2 * tile_rows :])
-    outgoing = jnp.concatenate(
-        [pack_terms(left_terms[0], left_terms[1]), pack_terms(right_terms[0], right_terms[1])],
-        axis=1,
-    )
     grad_queries = (
         restore(grad_qnorm, q_unit, q_factor, q_gain)
         .astype(jnp.bfloat16)
@@ -165,11 +161,17 @@
         ]
     )
     gain_totals = butterfly_sum(gain_terms, ("seq", "head", "fsdp"))
-    returned = extended_2(outgoing, (("seq", 1),), tile_rows)
-    returned, gain_totals = lax.optimization_barrier((returned, gain_totals))
-    incoming = returned[:, :tile_rows].astype(jnp.float32) + returned[:, 3 * tile_rows :].astype(
-        jnp.float32
-    )
+    ends = tile_count - 1
+    from_left = lax.ppermute(
+        pack_terms(right_terms[0], right_terms[1]), "seq", [(i, i + 1) for i in range(ends)]
+    )
+    from_right = lax.ppermute(
+        pack_terms(left_terms[0], left_terms[1]), "seq", [(i + 1, i) for i in range(ends)]
+    )
+    from_left, from_right, gain_totals = lax.optimization_barrier(
+        (from_left, from_right, gain_totals)
+    )
+    incoming = from_left.astype(jnp.float32) + from_right.astype(jnp.float32)
     grad_knorm = own_terms[0] + incoming[..., :columns].reshape(
         sample_count, tile_rows, head_count, head_size
     )

time: 148 us -> 144 us (0.973); the launches traced: 146 us -> 143 us
  other arithmetic: 17 us -> 13.9 us
    ppermute x0 -> x2, starting transfers between devices: none -> 6.65 us  [the longest x1 5.37 us: per_device(): lax.ppermute(pack_terms(right_terms[0], right_terms[1]), 'seq', [(i, i +...]
    ppermute x2 -> x1, starting transfers between devices: 9.32 us -> 4.58 us  [extended_2(): lax.ppermute(tail, axis, [(i, (i + 1) % count) for i in range(ends)])]
    concatenate x2 -> x1, other arithmetic: 3.48 us -> 0.15 us  [extended_2(): jnp.concatenate([lax.ppermute(tail, axis, [(i, (i + 1) % count) for i in...]
    unnamed x32 -> x26, local copies, waits for them, and re-layouts: 10.6 us -> 10.8 us
    ppermute x2 -> x1, waiting for transfers between devices: 7.84 us -> 7.84 us  [extended_2(): lax.ppermute(head, axis, [((i + 1) % count, i) for i in range(ends)])]
  transfers between devices with their start and end apart: 14 -> 14, of which waited for: 9 -> 9; matrix products, arithmetic and copies ran while one was open for 7% -> 8% of each run, Pallas kernels for 0% -> 0%
where the time goes in v4:
time: 144 us; the launch traced here: 143 us
  starting transfers between devices  87.2 us (61%)
  waiting for transfers between devices  19.6 us (14%)
  other arithmetic  13.9 us (10%)
  local copies, waits for them, and re-layouts  12 us (8%)
  matrix products  7.48 us (5%)
  between operations  2.97 us (2%)
    ppermute x10, starting transfers between devices, butterfly_sum(): lax.ppermute(value, axis, [(i, i ^ step) for i in range(count)])  74.7 us
    unnamed x26, local copies, waits for them, and re-layouts  10.8 us
    ppermute x10, waiting for transfers between devices, butterfly_sum(): lax.ppermute(value, axis, [(i, i ^ step) for i in range(count)])  10.5 us
    ppermute x1, waiting for transfers between devices, extended_2(): lax.ppermute(head, axis, [((i + 1) % count, i) for i in range(ends)])  7.84 us
    ppermute x1, starting transfers between devices, per_device(): lax.ppermute(pack_terms(right_terms[0], right_terms[1]), 'seq', [(i, i +...  5.37 us
    ppermute x1, starting transfers between devices, extended_2(): lax.ppermute(tail, axis, [(i, (i + 1) % count) for i in range(ends)])  4.58 us
  transfers between devices with their start and end apart: 14, of which 9 were waited for; matrix products, arithmetic and copies ran while one was open for 8% of the time, Pallas kernels for 0%

profile of v4, /device:TPU:24, one launch (start us, length us, event | category | flops | bytes accessed | tf_op | source)
XLA Modules:
  0.0 143.1 jit_solution(17999054537143611116)
XLA Ops:
  0.7 1.2 copy.47
  1.9 1.2 copy.48
  3.1 0.1 pad_maximum_fusion.1
  3.1 1.3 collective-permute-start.1
  4.4 4.6 %collective-permute-start = (bf16[1,384,768]{1,2,0:T(8,128)(2,1)S(1)}, bf16[1,384,768]{1,2,0:T(8,128)(2,1)S(1)}, u32[]{:S(2)}, u32[]{:S(2)}) collective-permute-start(bf16[1,384,768]{1,2,0:T(8,128)(2,1)S(1)} %pad_maximum_fusion.1), channel_id=1, source_target_pairs={{0,64},{64,128},{128,192},{192,256},{256,320},{320,384},{384,448},... | collective-permute-start | bytes 1769480 | tf_op jit(solution)/shard_map/ppermute | solution.py:19
  9.1 0.7 compare_reduce_fusion.2
  11.7 0.1 add_bitcast_fusion
  11.8 0.1 broadcast_in_dim.16
  11.9 0.2 copy.51
  12.1 0.2 copy.46
  12.4 0.1 multiply_reduce_fusion.5
  12.4 7.8 %collective-permute-done.1 = bf16[1,384,768]{1,2,0:T(8,128)(2,1)S(1)} collective-permute-done((bf16[1,384,768]{1,2,0:T(8,128)(2,1)S(1)}, bf16[1,384,768]{1,2,0:T(8,128)(2,1)S(1)}, u32[]{:S(2)}, u32[]{:S(2)}) %collective-permute-start.1) | collective-permute-done | bytes 589856 | tf_op jit(solution)/shard_map/ppermute | solution.py:21
  20.3 1.2 collective-permute-done
  21.5 0.2 pad_maximum_fusion
  21.6 0.2 fusion.17
  21.8 0.1 multiply_reduce_fusion
  22.0 0.0 copy-start.6
  22.0 0.1 broadcast_multiply_fusion
  22.1 0.5 copy-done.5
  22.6 0.0 copy-done.6
  22.7 1.2 fusion.20
  23.8 1.2 exponential_reduce_fusion
  25.0 1.0 exponential_convert_fusion
  26.0 1.6 %multiply_reduce_fusion.4 = (f32[3,384]{1,0:T(4,128)S(1)}, bf16[3,384,128]{1,2,0:T(8,128)(2,1)}) fusion(bf16[3,1,384,128]{2,3,0,1:T(8,128)(2,1)S(1)} %bitcast.103, bf16[3,384,1152]{2,1,0:T(8,128)(2,1)S(1)} %exponential_convert_fusion, bf16[3,1152,128]{1,2,0:T(8,128)(2,1)S(1)} %bitcast.97), kind=kOutput, calls=%fused_computation.35 | convolution fusion | flops 340474752 | bytes 4133376 | tf_op jit(solution)/shard_map/vmap(sqk,skd->sqd)/dot_general | solution.py:64
  27.6 1.0 fusion
  28.6 1.0 multiply_reduce_fusion.2
  29.6 0.8 fusion.1
  30.4 0.1 fusion.16
  30.6 0.3 fusion.2
  31.0 4.4 %collective-permute-start.4 = (f32[256]{0:T(256)S(1)}, f32[256]{0:T(256)S(1)}, u32[]{:S(2)}, u32[]{:S(2)}) collective-permute-start(f32[256]{0:T(256)S(1)} %pad_maximum_fusion.4), channel_id=1, source_target_pairs={{0,64},{64,0},{128,192},{192,128},{256,320},{320,256},{384,448},{4... | collective-permute-start | bytes 3080 | tf_op jit(solution)/shard_map/ppermute | solution.py:33
  35.4 1.5 %collective-permute-done.4 = f32[256]{0:T(256)S(1)} collective-permute-done((f32[256]{0:T(256)S(1)}, f32[256]{0:T(256)S(1)}, u32[]{:S(2)}, u32[]{:S(2)}) %collective-permute-start.4) | collective-permute-done | bytes 1056 | tf_op jit(solution)/shard_map/ppermute | solution.py:33
  36.9 5.8 %collective-permute-start.5 = (f32[256]{0:T(256)S(1)}, f32[256]{0:T(256)S(1)}, u32[]{:S(2)}, u32[]{:S(2)}) collective-permute-start(f32[256]{0:T(256)S(1)} %fusion.12), channel_id=1, source_target_pairs={{0,128},{64,192},{128,0},{192,64},{256,384},{320,448},{384,256},{4... | collective-permute-start | bytes 3080 | tf_op jit(solution)/shard_map/ppermute | solution.py:33
  42.8 1.5 %collective-permute-done.5 = f32[256]{0:T(256)S(1)} collective-permute-done((f32[256]{0:T(256)S(1)}, f32[256]{0:T(256)S(1)}, u32[]{:S(2)}, u32[]{:S(2)}) %collective-permute-start.5) | collective-permute-done | bytes 1056 | tf_op jit(solution)/shard_map/ppermute | solution.py:33
  44.3 9.4 %collective-permute-start.6 = (f32[256]{0:T(256)S(1)}, f32[256]{0:T(256)S(1)}, u32[]{:S(2)}, u32[]{:S(2)}) collective-permute-start(f32[256]{0:T(256)S(1)} %add.85), channel_id=1, source_target_pairs={{0,256},{64,320},{128,384},{192,448},{256,0},{320,64},{384,128},{4... | collective-permute-start | bytes 3080 | tf_op jit(solution)/shard_map/ppermute | solution.py:33
  53.7 1.5 %collective-permute-done.6 = f32[256]{0:T(256)S(1)} collective-permute-done((f32[256]{0:T(256)S(1)}, f32[256]{0:T(256)S(1)}, u32[]{:S(2)}, u32[]{:S(2)}) %collective-permute-start.6) | collective-permute-done | bytes 1056 | tf_op jit(solution)/shard_map/ppermute | solution.py:33
  55.2 15.7 %collective-permute-start.7 = (f32[256]{0:T(256)S(1)}, f32[256]{0:T(256)S(1)}, u32[]{:S(2)}, u32[]{:S(2)}) collective-permute-start(f32[256]{0:T(256)S(1)} %add.86), channel_id=1, source_target_pairs={{0,512},{64,576},{128,640},{192,704},{256,768},{320,832},{384,896}... | collective-permute-start | bytes 3080 | tf_op jit(solution)/shard_map/ppermute | solution.py:33
  70.9 1.9 %fusion.21 = (bf16[1,1152,3,128]{1,3,2,0:T(8,128)(2,1)S(1)}, f32[1,1152,3,128]{1,3,2,0:T(8,128)}) fusion(bf16[384,3,128]{0,2,1:T(8,128)(2,1)S(1)} %bitcast.105, bf16[3,384,1152]{2,1,0:T(8,128)(2,1)S(1)} %exponential_convert_fusion), kind=kOutput, calls=%fused_computation.64 | convolution fusion | flops 340180992 | bytes 5603328 | tf_op jit(solution)/shard_map/hsqk,sqhd->skhd/dot_general | solution.py:88
  72.9 1.9 %collective-permute-start.8 = (f32[256]{0:T(256)S(1)}, f32[256]{0:T(256)S(1)}, u32[]{:S(2)}, u32[]{:S(2)}) collective-permute-start(f32[256]{0:T(256)S(1)} %add.87), channel_id=1, source_target_pairs={{0,16},{16,0},{32,48},{48,32},{1,17},{17,1},{33,49},{49,33},{2,18}... | collective-permute-start | bytes 3080 | tf_op jit(solution)/shard_map/ppermute | solution.py:33
  74.8 0.1 fusion.19
  74.9 1.0 collective-permute-done.8
  75.9 22.7 %collective-permute-start.9 = (f32[256]{0:T(256)S(1)}, f32[256]{0:T(256)S(1)}, u32[]{:S(2)}, u32[]{:S(2)}) collective-permute-start(f32[256]{0:T(256)S(1)} %add.88), channel_id=1, source_target_pairs={{0,32},{16,48},{32,0},{48,16},{1,33},{17,49},{33,1},{49,17},{2,34}... | collective-permute-start | bytes 3080 | tf_op jit(solution)/shard_map/ppermute | solution.py:33
  98.6 0.9 pad_maximum_fusion.2
  99.5 0.6 collective-permute-done.9
  100.2 2.6 %collective-permute-start.10 = (f32[256]{0:T(256)S(1)}, f32[256]{0:T(256)S(1)}, u32[]{:S(2)}, u32[]{:S(2)}) collective-permute-start(f32[256]{0:T(256)S(1)} %add.89), channel_id=1, source_target_pairs={{0,1},{1,0},{2,3},{3,2},{4,5},{5,4},{6,7},{7,6},{8,9},{9,8},{10,11... | collective-permute-start | bytes 3080 | tf_op jit(solution)/shard_map/ppermute | solution.py:33
  102.8 0.9 pad_maximum_fusion.3
  103.7 1.3 collective-permute-start.3
  105.0 5.4 %collective-permute-start.2 = (bf16[1,384,768]{1,2,0:T(8,128)(2,1)}, bf16[1,384,768]{1,2,0:T(8,128)(2,1)}, u32[]{:S(2)}, u32[]{:S(2)}) collective-permute-start(bf16[1,384,768]{1,2,0:T(8,128)(2,1)} %pad_maximum_fusion.2), channel_id=1, source_target_pairs={{0,64},{64,128},{128,192},{192,256},{256,320},{320,384},{384,448},... | collective-permute-start | bytes 1769480 | tf_op jit(solution)/shard_map/ppermute | solution.py:165
  110.4 3.9 %collective-permute-start.11 = (f32[256]{0:T(256)S(1)}, f32[256]{0:T(256)S(1)}, u32[]{:S(2)}, u32[]{:S(2)}) collective-permute-start(f32[256]{0:T(256)S(1)} %add.90), channel_id=1, source_target_pairs={{0,2},{1,3},{2,0},{3,1},{4,6},{5,7},{6,4},{7,5},{8,10},{9,11},{10,... | collective-permute-start | bytes 3080 | tf_op jit(solution)/shard_map/ppermute | solution.py:33
  114.2 3.1 %collective-permute-done.11 = f32[256]{0:T(256)S(1)} collective-permute-done((f32[256]{0:T(256)S(1)}, f32[256]{0:T(256)S(1)}, u32[]{:S(2)}, u32[]{:S(2)}) %collective-permute-start.11) | collective-permute-done | bytes 1056 | tf_op jit(solution)/shard_map/ppermute | solution.py:33
  117.3 3.4 %collective-permute-start.12 = (f32[256]{0:T(256)S(1)}, f32[256]{0:T(256)S(1)}, u32[]{:S(2)}, u32[]{:S(2)}) collective-permute-start(f32[256]{0:T(256)S(1)} %add.91), channel_id=1, source_target_pairs={{0,4},{1,5},{2,6},{3,7},{4,0},{5,1},{6,2},{7,3},{8,12},{9,13},{10,... | collective-permute-start | bytes 3080 | tf_op jit(solution)/shard_map/ppermute | solution.py:33
  120.7 0.9 multiply_convert_fusion.3
  121.6 1.2 collective-permute-done.12
  122.8 4.9 %collective-permute-start.13 = (f32[256]{0:T(256)S(1)}, f32[256]{0:T(256)}, u32[]{:S(2)}, u32[]{:S(2)}) collective-permute-start(f32[256]{0:T(256)S(1)} %add.92), channel_id=1, source_target_pairs={{0,8},{1,9},{2,10},{3,11},{4,12},{5,13},{6,14},{7,15},{8,0},{9,1},... | collective-permute-start | bytes 3080 | tf_op jit(solution)/shard_map/ppermute | solution.py:33
  127.7 1.8 %copy.56 = bf16[1,384,384]{2,1,0:T(8,128)(2,1)} copy(bf16[1,384,384]{1,2,0:T(8,128)(2,1)} %bitcast.113) | data formatting | bytes 589824
  129.6 1.8 %copy.57 = bf16[1,384,384]{2,1,0:T(8,128)(2,1)} copy(bf16[1,384,384]{1,2,0:T(8,128)(2,1)} %bitcast.109) | data formatting | bytes 589824
  131.4 1.3 add.93
  132.7 1.4 convert_add_fusion
  134.1 0.9 fusion.18
  135.0 1.8 %fusion.5 = bf16[1,384,3,128]{1,3,2,0:T(8,128)(2,1)} fusion(f32[1,384,3,128]{1,3,2,0:T(8,128)S(1)} %bitcast.107, f32[1,1152,3,128]{1,3,2,0:T(8,128)} %get-tuple-element.53), kind=kLoop, calls=%fused_computation.22 | loop fusion | flops 294912 | bytes 1474560 | tf_op jit(solution)/shard_map/convert_element_type | solution.py:186
  136.8 1.8 %copy.59 = bf16[1,384,384]{2,1,0:T(8,128)(2,1)} copy(bf16[1,384,384]{1,2,0:T(8,128)(2,1)} %bitcast.110) | data formatting | bytes 589824
  138.6 0.5 slice_multiply_fusion
  139.2 1.2 multiply_reduce_fusion.1
  140.4 0.9 multiply_convert_fusion.1
  141.3 1.8 %copy.58 = bf16[1,384,384]{2,1,0:T(8,128)(2,1)} copy(bf16[1,384,384]{1,2,0:T(8,128)(2,1)} %bitcast.108) | data formatting | bytes 589824
  (42 shorter events, 0.3 us)
Async XLA Ops:
  0.6 8.4 %copy-start.8 = (s32[1,1,3]{2,1,0:T(1,128)S(1)}, s32[1,1,3]{2,1,0:T(1,128)}, u32[]{:S(2)}) copy-start(s32[1,1,3]{2,1,0:T(1,128)} %param.13) | copy-start | bytes 40
  0.6 11.2 %copy-start.3 = (bf16[1,384,384]{2,1,0:T(8,128)(2,1)S(1)}, bf16[1,384,384]{2,1,0:T(8,128)(2,1)}, u32[]{:S(2)}) copy-start(bf16[1,384,384]{2,1,0:T(8,128)(2,1)} %param.12) | copy-start | bytes 884740
  0.7 11.4 %copy-start.4 = (bf16[1,384,384]{2,1,0:T(8,128)(2,1)S(1)}, bf16[1,384,384]{2,1,0:T(8,128)(2,1)}, u32[]{:S(2)}) copy-start(bf16[1,384,384]{2,1,0:T(8,128)(2,1)} %param.7) | copy-start | bytes 884740
  3.1 17.1 %collective-permute-start.1 = (bf16[1,384,768]{1,2,0:T(8,128)(2,1)S(1)}, bf16[1,384,768]{1,2,0:T(8,128)(2,1)S(1)}, u32[]{:S(2)}, u32[]{:S(2)}) collective-permute-start(bf16[1,384,768]{1,2,0:T(8,128)(2,1)S(1)} %pad_maximum_fusion.1), channel_id=1, source_target_pairs={{64,0},{128,64},{192,128},{256,192},{320,256},{384,320},{448,384},... | collective-permute-start | bytes 1769480 | tf_op jit(solution)/shard_map/ppermute | solution.py:21
  4.4 17.0 %collective-permute-start = (bf16[1,384,768]{1,2,0:T(8,128)(2,1)S(1)}, bf16[1,384,768]{1,2,0:T(8,128)(2,1)S(1)}, u32[]{:S(2)}, u32[]{:S(2)}) collective-permute-start(bf16[1,384,768]{1,2,0:T(8,128)(2,1)S(1)} %pad_maximum_fusion.1), channel_id=1, source_target_pairs={{0,64},{64,128},{128,192},{192,256},{256,320},{320,384},{384,448},... | collective-permute-start | bytes 1769480 | tf_op jit(solution)/shard_map/ppermute | solution.py:19
  12.1 15.5 %copy-start.1 = (bf16[1,384,384]{1,2,0:T(8,128)(2,1)}, bf16[1,384,384]{1,2,0:T(8,128)(2,1)S(1)}, u32[]{:S(2)}) copy-start(bf16[1,384,384]{1,2,0:T(8,128)(2,1)S(1)} %copy.51) | copy-start | bytes 884740
  22.0 0.7 copy-start.5
  22.0 0.7 copy-start.6
  30.6 40.4 %copy-start.2 = (bf16[1,384,384]{1,2,0:T(8,128)(2,1)S(1)}, bf16[1,384,384]{1,2,0:T(8,128)(2,1)}, u32[]{:S(2)}) copy-start(bf16[1,384,384]{1,2,0:T(8,128)(2,1)} %copy-done.1) | copy-start | bytes 884740
  31.0 5.9 %collective-permute-start.4 = (f32[256]{0:T(256)S(1)}, f32[256]{0:T(256)S(1)}, u32[]{:S(2)}, u32[]{:S(2)}) collective-permute-start(f32[256]{0:T(256)S(1)} %pad_maximum_fusion.4), channel_id=1, source_target_pairs={{0,64},{64,0},{128,192},{192,128},{256,320},{320,256},{384,448},{4... | collective-permute-start | bytes 3080 | tf_op jit(solution)/shard_map/ppermute | solution.py:33
  36.9 7.3 %collective-permute-start.5 = (f32[256]{0:T(256)S(1)}, f32[256]{0:T(256)S(1)}, u32[]{:S(2)}, u32[]{:S(2)}) collective-permute-start(f32[256]{0:T(256)S(1)} %fusion.12), channel_id=1, source_target_pairs={{0,128},{64,192},{128,0},{192,64},{256,384},{320,448},{384,256},{4... | collective-permute-start | bytes 3080 | tf_op jit(solution)/shard_map/ppermute | solution.py:33
  44.3 10.9 %collective-permute-start.6 = (f32[256]{0:T(256)S(1)}, f32[256]{0:T(256)S(1)}, u32[]{:S(2)}, u32[]{:S(2)}) collective-permute-start(f32[256]{0:T(256)S(1)} %add.85), channel_id=1, source_target_pairs={{0,256},{64,320},{128,384},{192,448},{256,0},{320,64},{384,128},{4... | collective-permute-start | bytes 3080 | tf_op jit(solution)/shard_map/ppermute | solution.py:33
  55.2 17.6 %collective-permute-start.7 = (f32[256]{0:T(256)S(1)}, f32[256]{0:T(256)S(1)}, u32[]{:S(2)}, u32[]{:S(2)}) collective-permute-start(f32[256]{0:T(256)S(1)} %add.86), channel_id=1, source_target_pairs={{0,512},{64,576},{128,640},{192,704},{256,768},{320,832},{384,896}... | collective-permute-start | bytes 3080 | tf_op jit(solution)/shard_map/ppermute | solution.py:33
  72.9 3.0 %collective-permute-start.8 = (f32[256]{0:T(256)S(1)}, f32[256]{0:T(256)S(1)}, u32[]{:S(2)}, u32[]{:S(2)}) collective-permute-start(f32[256]{0:T(256)S(1)} %add.87), channel_id=1, source_target_pairs={{0,16},{16,0},{32,48},{48,32},{1,17},{17,1},{33,49},{49,33},{2,18}... | collective-permute-start | bytes 3080 | tf_op jit(solution)/shard_map/ppermute | solution.py:33
  75.9 24.3 %collective-permute-start.9 = (f32[256]{0:T(256)S(1)}, f32[256]{0:T(256)S(1)}, u32[]{:S(2)}, u32[]{:S(2)}) collective-permute-start(f32[256]{0:T(256)S(1)} %add.88), channel_id=1, source_target_pairs={{0,32},{16,48},{32,0},{48,16},{1,33},{17,49},{33,1},{49,17},{2,34}... | collective-permute-start | bytes 3080 | tf_op jit(solution)/shard_map/ppermute | solution.py:33
  100.2 10.2 %collective-permute-start.10 = (f32[256]{0:T(256)S(1)}, f32[256]{0:T(256)S(1)}, u32[]{:S(2)}, u32[]{:S(2)}) collective-permute-start(f32[256]{0:T(256)S(1)} %add.89), channel_id=1, source_target_pairs={{0,1},{1,0},{2,3},{3,2},{4,5},{5,4},{6,7},{7,6},{8,9},{9,8},{10,11... | collective-permute-start | bytes 3080 | tf_op jit(solution)/shard_map/ppermute | solution.py:33
  103.7 29.0 %collective-permute-start.3 = (bf16[1,384,768]{1,2,0:T(8,128)(2,1)}, bf16[1,384,768]{1,2,0:T(8,128)(2,1)}, u32[]{:S(2)}, u32[]{:S(2)}) collective-permute-start(bf16[1,384,768]{1,2,0:T(8,128)(2,1)} %pad_maximum_fusion.3), channel_id=1, source_target_pairs={{64,0},{128,64},{192,128},{256,192},{320,256},{384,320},{448,384},... | collective-permute-start | bytes 1769480 | tf_op jit(solution)/shard_map/ppermute | solution.py:168
  105.0 27.7 %collective-permute-start.2 = (bf16[1,384,768]{1,2,0:T(8,128)(2,1)}, bf16[1,384,768]{1,2,0:T(8,128)(2,1)}, u32[]{:S(2)}, u32[]{:S(2)}) collective-permute-start(bf16[1,384,768]{1,2,0:T(8,128)(2,1)} %pad_maximum_fusion.2), channel_id=1, source_target_pairs={{0,64},{64,128},{128,192},{192,256},{256,320},{320,384},{384,448},... | collective-permute-start | bytes 1769480 | tf_op jit(solution)/shard_map/ppermute | solution.py:165
  110.4 7.0 %collective-permute-start.11 = (f32[256]{0:T(256)S(1)}, f32[256]{0:T(256)S(1)}, u32[]{:S(2)}, u32[]{:S(2)}) collective-permute-start(f32[256]{0:T(256)S(1)} %add.90), channel_id=1, source_target_pairs={{0,2},{1,3},{2,0},{3,1},{4,6},{5,7},{6,4},{7,5},{8,10},{9,11},{10,... | collective-permute-start | bytes 3080 | tf_op jit(solution)/shard_map/ppermute | solution.py:33
  117.3 5.5 %collective-permute-start.12 = (f32[256]{0:T(256)S(1)}, f32[256]{0:T(256)S(1)}, u32[]{:S(2)}, u32[]{:S(2)}) collective-permute-start(f32[256]{0:T(256)S(1)} %add.91), channel_id=1, source_target_pairs={{0,4},{1,5},{2,6},{3,7},{4,0},{5,1},{6,2},{7,3},{8,12},{9,13},{10,... | collective-permute-start | bytes 3080 | tf_op jit(solution)/shard_map/ppermute | solution.py:33
  122.8 8.6 %collective-permute-start.13 = (f32[256]{0:T(256)S(1)}, f32[256]{0:T(256)}, u32[]{:S(2)}, u32[]{:S(2)}) collective-permute-start(f32[256]{0:T(256)S(1)} %add.92), channel_id=1, source_target_pairs={{0,8},{1,9},{2,10},{3,11},{4,12},{5,13},{6,14},{7,15},{8,0},{9,1},... | collective-permute-start | bytes 3080 | tf_op jit(solution)/shard_map/ppermute | solution.py:33
  134.0 4.6 %copy-start.7 = (f32[256]{0:T(256)S(1)}, f32[256]{0:T(256)}, u32[]{:S(2)}) copy-start(f32[256]{0:T(256)} %add.93) | copy-start | bytes 3076
  138.6 1.7 %copy-start = (f32[1,384,384]{1,2,0:T(8,128)S(1)}, f32[1,384,384]{1,2,0:T(8,128)}, u32[]{:S(2)}) copy-start(f32[1,384,384]{1,2,0:T(8,128)} %get-tuple-element.40) | copy-start | bytes 1769476

commit v5 on v4

--- a/solution.py
+++ b/solution.py
@@ -25,14 +25,33 @@
     return cells
 
 
-def butterfly_sum(value, axes):
-    for axis in axes:
-        count = lax.axis_size(axis)
-        step = 1
-        while step < count:
-            value = value + lax.ppermute(value, axis, [(i, i ^ step) for i in range(count)])
-            step *= 2
+def butterfly_sum(value, stages):
+    for axes, mask in stages:
+        count = math.prod(lax.axis_size(axis) for axis in axes)
+        value = value + lax.ppermute(value, axes, [(i, i ^ mask) for i in range(count)])
     return value
+
+
+def gain_stages():
+    seq_count = lax.axis_size("seq")
+    head_count = lax.axis_size("head")
+    fsdp_count = lax.axis_size("fsdp")
+    stages = []
+    step = 1
+    while step < seq_count:
+        stages.append((("seq",), step))
+        step *= 2
+    stages.append((("head",), 1))
+    half = seq_count // 2
+    step = 2
+    while step < head_count:
+        stages.append((("seq", "head"), half * head_count + step))
+        step *= 2
+    side = math.isqrt(fsdp_count)
+    for base in (1, side):
+        stages.append((("fsdp",), base))
+        stages.append((("fsdp",), 3 * base))
+    return stages
 
 
 def normalize(raw_rows, gain_vector):
@@ -160,7 +179,7 @@
             jnp.sum(near_terms * k_unit_all, axis=(0, 1, 2)),
         ]
     )
-    gain_totals = butterfly_sum(gain_terms, ("seq", "head", "fsdp"))
+    gain_totals = butterfly_sum(gain_terms, gain_stages())
     ends = tile_count - 1
     from_left = lax.ppermute(
         pack_terms(right_terms[0], right_terms[1]), "seq", [(i, i + 1) for i in range(ends)]

time: 144 us -> 141 us (0.979)
  starting transfers between devices: 87.2 us -> 83.5 us
    ppermute x10, starting transfers between devices: 74.7 us -> 71 us  [butterfly_sum(): lax.ppermute(value, axes, [(i, i ^ mask) for i in range(count)])]
where the time goes in v5:
time: 141 us; the launch traced here: 140 us
  starting transfers between devices  83.5 us (59%)
  waiting for transfers between devices  20.2 us (14%)
  other arithmetic  13.9 us (10%)
  local copies, waits for them, and re-layouts  12 us (9%)
  matrix products  7.48 us (5%)
  between operations  2.97 us (2%)
    ppermute x10, starting transfers between devices, butterfly_sum(): lax.ppermute(value, axes, [(i, i ^ mask) for i in range(count)])  71 us
    ppermute x10, waiting for transfers between devices, butterfly_sum(): lax.ppermute(value, axes, [(i, i ^ mask) for i in range(count)])  11.1 us
    unnamed x26, local copies, waits for them, and re-layouts  10.8 us
    ppermute x1, waiting for transfers between devices, extended_2(): lax.ppermute(head, axis, [((i + 1) % count, i) for i in range(ends)])  7.84 us
    ppermute x1, starting transfers between devices, per_device(): lax.ppermute(pack_terms(right_terms[0], right_terms[1]), 'seq', [(i, i +...  5.37 us
    ppermute x1, starting transfers between devices, extended_2(): lax.ppermute(tail, axis, [(i, (i + 1) % count) for i in range(ends)])  4.58 us
  transfers between devices with their start and end apart: 14, of which 9 were waited for; matrix products, arithmetic and copies ran while one was open for 8% of the time, Pallas kernels for 0%

profile of v5, /device:TPU:24, one launch (start us, length us, event | category | flops | bytes accessed | tf_op | source)
XLA Modules:
  0.0 140.0 jit_solution(5323300213983329750)
XLA Ops:
  0.7 1.2 copy.47
  1.9 1.2 copy.48
  3.1 0.1 pad_maximum_fusion.1
  3.1 1.3 collective-permute-start.1
  4.4 4.6 %collective-permute-start = (bf16[1,384,768]{1,2,0:T(8,128)(2,1)S(1)}, bf16[1,384,768]{1,2,0:T(8,128)(2,1)S(1)}, u32[]{:S(2)}, u32[]{:S(2)}) collective-permute-start(bf16[1,384,768]{1,2,0:T(8,128)(2,1)S(1)} %pad_maximum_fusion.1), channel_id=1, source_target_pairs={{0,64},{64,128},{128,192},{192,256},{256,320},{320,384},{384,448},... | collective-permute-start | bytes 1769480 | tf_op jit(solution)/shard_map/ppermute | solution.py:19
  9.1 0.7 compare_reduce_fusion.2
  11.7 0.1 add_bitcast_fusion
  11.8 0.1 broadcast_in_dim.16
  11.9 0.2 copy.51
  12.1 0.2 copy.46
  12.4 0.1 multiply_reduce_fusion.5
  12.4 7.8 %collective-permute-done.1 = bf16[1,384,768]{1,2,0:T(8,128)(2,1)S(1)} collective-permute-done((bf16[1,384,768]{1,2,0:T(8,128)(2,1)S(1)}, bf16[1,384,768]{1,2,0:T(8,128)(2,1)S(1)}, u32[]{:S(2)}, u32[]{:S(2)}) %collective-permute-start.1) | collective-permute-done | bytes 589856 | tf_op jit(solution)/shard_map/ppermute | solution.py:21
  20.3 1.2 collective-permute-done
  21.5 0.2 pad_maximum_fusion
  21.6 0.2 fusion.17
  21.8 0.1 multiply_reduce_fusion
  22.0 0.0 copy-start.6
  22.0 0.1 broadcast_multiply_fusion
  22.1 0.5 copy-done.5
  22.6 0.0 copy-done.6
  22.7 1.2 fusion.20
  23.8 1.2 exponential_reduce_fusion
  25.0 1.0 exponential_convert_fusion
  26.0 1.6 %multiply_reduce_fusion.4 = (f32[3,384]{1,0:T(4,128)S(1)}, bf16[3,384,128]{1,2,0:T(8,128)(2,1)}) fusion(bf16[3,1,384,128]{2,3,0,1:T(8,128)(2,1)S(1)} %bitcast.103, bf16[3,384,1152]{2,1,0:T(8,128)(2,1)S(1)} %exponential_convert_fusion, bf16[3,1152,128]{1,2,0:T(8,128)(2,1)S(1)} %bitcast.97), kind=kOutput, calls=%fused_computation.35 | convolution fusion | flops 340474752 | bytes 4133376 | tf_op jit(solution)/shard_map/vmap(sqk,skd->sqd)/dot_general | solution.py:83
  27.6 1.0 fusion
  28.6 1.0 multiply_reduce_fusion.2
  29.6 0.8 fusion.1
  30.4 0.1 fusion.16
  30.6 0.3 fusion.2
  31.0 4.4 %collective-permute-start.4 = (f32[256]{0:T(256)S(1)}, f32[256]{0:T(256)S(1)}, u32[]{:S(2)}, u32[]{:S(2)}) collective-permute-start(f32[256]{0:T(256)S(1)} %pad_maximum_fusion.4), channel_id=1, source_target_pairs={{0,64},{64,0},{128,192},{192,128},{256,320},{320,256},{384,448},{4... | collective-permute-start | bytes 3080 | tf_op jit(solution)/shard_map/ppermute | solution.py:31
  35.4 1.5 %collective-permute-done.4 = f32[256]{0:T(256)S(1)} collective-permute-done((f32[256]{0:T(256)S(1)}, f32[256]{0:T(256)S(1)}, u32[]{:S(2)}, u32[]{:S(2)}) %collective-permute-start.4) | collective-permute-done | bytes 1056 | tf_op jit(solution)/shard_map/ppermute | solution.py:31
  36.9 5.8 %collective-permute-start.5 = (f32[256]{0:T(256)S(1)}, f32[256]{0:T(256)S(1)}, u32[]{:S(2)}, u32[]{:S(2)}) collective-permute-start(f32[256]{0:T(256)S(1)} %fusion.12), channel_id=1, source_target_pairs={{0,128},{64,192},{128,0},{192,64},{256,384},{320,448},{384,256},{4... | collective-permute-start | bytes 3080 | tf_op jit(solution)/shard_map/ppermute | solution.py:31
  42.8 1.5 %collective-permute-done.5 = f32[256]{0:T(256)S(1)} collective-permute-done((f32[256]{0:T(256)S(1)}, f32[256]{0:T(256)S(1)}, u32[]{:S(2)}, u32[]{:S(2)}) %collective-permute-start.5) | collective-permute-done | bytes 1056 | tf_op jit(solution)/shard_map/ppermute | solution.py:31
  44.3 9.4 %collective-permute-start.6 = (f32[256]{0:T(256)S(1)}, f32[256]{0:T(256)S(1)}, u32[]{:S(2)}, u32[]{:S(2)}) collective-permute-start(f32[256]{0:T(256)S(1)} %add.85), channel_id=1, source_target_pairs={{0,256},{64,320},{128,384},{192,448},{256,0},{320,64},{384,128},{4... | collective-permute-start | bytes 3080 | tf_op jit(solution)/shard_map/ppermute | solution.py:31
  53.7 1.5 %collective-permute-done.6 = f32[256]{0:T(256)S(1)} collective-permute-done((f32[256]{0:T(256)S(1)}, f32[256]{0:T(256)S(1)}, u32[]{:S(2)}, u32[]{:S(2)}) %collective-permute-start.6) | collective-permute-done | bytes 1056 | tf_op jit(solution)/shard_map/ppermute | solution.py:31
  55.2 15.7 %collective-permute-start.7 = (f32[256]{0:T(256)S(1)}, f32[256]{0:T(256)S(1)}, u32[]{:S(2)}, u32[]{:S(2)}) collective-permute-start(f32[256]{0:T(256)S(1)} %add.86), channel_id=1, source_target_pairs={{0,512},{64,576},{128,640},{192,704},{256,768},{320,832},{384,896}... | collective-permute-start | bytes 3080 | tf_op jit(solution)/shard_map/ppermute | solution.py:31
  70.9 1.9 %fusion.21 = (bf16[1,1152,3,128]{1,3,2,0:T(8,128)(2,1)S(1)}, f32[1,1152,3,128]{1,3,2,0:T(8,128)}) fusion(bf16[384,3,128]{0,2,1:T(8,128)(2,1)S(1)} %bitcast.105, bf16[3,384,1152]{2,1,0:T(8,128)(2,1)S(1)} %exponential_convert_fusion), kind=kOutput, calls=%fused_computation.64 | convolution fusion | flops 340180992 | bytes 5603328 | tf_op jit(solution)/shard_map/hsqk,sqhd->skhd/dot_general | solution.py:107
  72.9 1.9 %collective-permute-start.8 = (f32[256]{0:T(256)S(1)}, f32[256]{0:T(256)S(1)}, u32[]{:S(2)}, u32[]{:S(2)}) collective-permute-start(f32[256]{0:T(256)S(1)} %add.87), channel_id=1, source_target_pairs={{0,16},{16,0},{32,48},{48,32},{1,17},{17,1},{33,49},{49,33},{2,18}... | collective-permute-start | bytes 3080 | tf_op jit(solution)/shard_map/ppermute | solution.py:31
  74.8 0.1 fusion.19
  74.9 1.0 collective-permute-done.8
  75.9 20.2 %collective-permute-start.9 = (f32[256]{0:T(256)S(1)}, f32[256]{0:T(256)S(1)}, u32[]{:S(2)}, u32[]{:S(2)}) collective-permute-start(f32[256]{0:T(256)S(1)} %add.88), channel_id=1, source_target_pairs={{0,544},{16,560},{32,512},{48,528},{64,608},{80,624},{96,576},{112... | collective-permute-start | bytes 3080 | tf_op jit(solution)/shard_map/ppermute | solution.py:31
  96.1 0.9 pad_maximum_fusion.2
  97.0 0.6 collective-permute-done.9
  97.6 2.6 %collective-permute-start.10 = (f32[256]{0:T(256)S(1)}, f32[256]{0:T(256)S(1)}, u32[]{:S(2)}, u32[]{:S(2)}) collective-permute-start(f32[256]{0:T(256)S(1)} %add.89), channel_id=1, source_target_pairs={{0,1},{1,0},{2,3},{3,2},{4,5},{5,4},{6,7},{7,6},{8,9},{9,8},{10,11... | collective-permute-start | bytes 3080 | tf_op jit(solution)/shard_map/ppermute | solution.py:31
  100.3 0.9 pad_maximum_fusion.3
  101.1 1.3 collective-permute-start.3
  102.4 5.4 %collective-permute-start.2 = (bf16[1,384,768]{1,2,0:T(8,128)(2,1)}, bf16[1,384,768]{1,2,0:T(8,128)(2,1)}, u32[]{:S(2)}, u32[]{:S(2)}) collective-permute-start(bf16[1,384,768]{1,2,0:T(8,128)(2,1)} %pad_maximum_fusion.2), channel_id=1, source_target_pairs={{0,64},{64,128},{128,192},{192,256},{256,320},{320,384},{384,448},... | collective-permute-start | bytes 1769480 | tf_op jit(solution)/shard_map/ppermute | solution.py:184
  107.8 3.0 %collective-permute-start.11 = (f32[256]{0:T(256)S(1)}, f32[256]{0:T(256)S(1)}, u32[]{:S(2)}, u32[]{:S(2)}) collective-permute-start(f32[256]{0:T(256)S(1)} %add.90), channel_id=1, source_target_pairs={{0,3},{1,2},{2,1},{3,0},{4,7},{5,6},{6,5},{7,4},{8,11},{9,10},{10,... | collective-permute-start | bytes 3080 | tf_op jit(solution)/shard_map/ppermute | solution.py:31
  110.8 3.7 %collective-permute-done.11 = f32[256]{0:T(256)S(1)} collective-permute-done((f32[256]{0:T(256)S(1)}, f32[256]{0:T(256)S(1)}, u32[]{:S(2)}, u32[]{:S(2)}) %collective-permute-start.11) | collective-permute-done | bytes 1056 | tf_op jit(solution)/shard_map/ppermute | solution.py:31
  114.5 3.4 %collective-permute-start.12 = (f32[256]{0:T(256)S(1)}, f32[256]{0:T(256)S(1)}, u32[]{:S(2)}, u32[]{:S(2)}) collective-permute-start(f32[256]{0:T(256)S(1)} %add.91), channel_id=1, source_target_pairs={{0,4},{1,5},{2,6},{3,7},{4,0},{5,1},{6,2},{7,3},{8,12},{9,13},{10,... | collective-permute-start | bytes 3080 | tf_op jit(solution)/shard_map/ppermute | solution.py:31
  117.9 0.9 multiply_convert_fusion.3
  118.7 1.2 collective-permute-done.12
  119.9 4.7 %collective-permute-start.13 = (f32[256]{0:T(256)S(1)}, f32[256]{0:T(256)}, u32[]{:S(2)}, u32[]{:S(2)}) collective-permute-start(f32[256]{0:T(256)S(1)} %add.92), channel_id=1, source_target_pairs={{0,12},{1,13},{2,14},{3,15},{4,8},{5,9},{6,10},{7,11},{8,4},{9,5},... | collective-permute-start | bytes 3080 | tf_op jit(solution)/shard_map/ppermute | solution.py:31
  124.6 1.8 %copy.56 = bf16[1,384,384]{2,1,0:T(8,128)(2,1)} copy(bf16[1,384,384]{1,2,0:T(8,128)(2,1)} %bitcast.113) | data formatting | bytes 589824
  126.5 1.8 %copy.57 = bf16[1,384,384]{2,1,0:T(8,128)(2,1)} copy(bf16[1,384,384]{1,2,0:T(8,128)(2,1)} %bitcast.109) | data formatting | bytes 589824
  128.3 1.3 add.93
  129.6 1.4 convert_add_fusion
  130.9 0.9 fusion.18
  131.9 1.8 %fusion.5 = bf16[1,384,3,128]{1,3,2,0:T(8,128)(2,1)} fusion(f32[1,384,3,128]{1,3,2,0:T(8,128)S(1)} %bitcast.107, f32[1,1152,3,128]{1,3,2,0:T(8,128)} %get-tuple-element.53), kind=kLoop, calls=%fused_computation.22 | loop fusion | flops 294912 | bytes 1474560 | tf_op jit(solution)/shard_map/convert_element_type | solution.py:205
  133.7 1.8 %copy.59 = bf16[1,384,384]{2,1,0:T(8,128)(2,1)} copy(bf16[1,384,384]{1,2,0:T(8,128)(2,1)} %bitcast.110) | data formatting | bytes 589824
  135.5 0.5 slice_multiply_fusion
  136.1 1.2 multiply_reduce_fusion.1
  137.3 0.9 multiply_convert_fusion.1
  138.2 1.8 %copy.58 = bf16[1,384,384]{2,1,0:T(8,128)(2,1)} copy(bf16[1,384,384]{1,2,0:T(8,128)(2,1)} %bitcast.108) | data formatting | bytes 589824
  (42 shorter events, 0.3 us)
Async XLA Ops:
  0.6 8.4 %copy-start.8 = (s32[1,1,3]{2,1,0:T(1,128)S(1)}, s32[1,1,3]{2,1,0:T(1,128)}, u32[]{:S(2)}) copy-start(s32[1,1,3]{2,1,0:T(1,128)} %param.13) | copy-start | bytes 40
  0.6 11.2 %copy-start.3 = (bf16[1,384,384]{2,1,0:T(8,128)(2,1)S(1)}, bf16[1,384,384]{2,1,0:T(8,128)(2,1)}, u32[]{:S(2)}) copy-start(bf16[1,384,384]{2,1,0:T(8,128)(2,1)} %param.12) | copy-start | bytes 884740
  0.7 11.4 %copy-start.4 = (bf16[1,384,384]{2,1,0:T(8,128)(2,1)S(1)}, bf16[1,384,384]{2,1,0:T(8,128)(2,1)}, u32[]{:S(2)}) copy-start(bf16[1,384,384]{2,1,0:T(8,128)(2,1)} %param.7) | copy-start | bytes 884740
  3.1 17.1 %collective-permute-start.1 = (bf16[1,384,768]{1,2,0:T(8,128)(2,1)S(1)}, bf16[1,384,768]{1,2,0:T(8,128)(2,1)S(1)}, u32[]{:S(2)}, u32[]{:S(2)}) collective-permute-start(bf16[1,384,768]{1,2,0:T(8,128)(2,1)S(1)} %pad_maximum_fusion.1), channel_id=1, source_target_pairs={{64,0},{128,64},{192,128},{256,192},{320,256},{384,320},{448,384},... | collective-permute-start | bytes 1769480 | tf_op jit(solution)/shard_map/ppermute | solution.py:21
  4.4 17.0 %collective-permute-start = (bf16[1,384,768]{1,2,0:T(8,128)(2,1)S(1)}, bf16[1,384,768]{1,2,0:T(8,128)(2,1)S(1)}, u32[]{:S(2)}, u32[]{:S(2)}) collective-permute-start(bf16[1,384,768]{1,2,0:T(8,128)(2,1)S(1)} %pad_maximum_fusion.1), channel_id=1, source_target_pairs={{0,64},{64,128},{128,192},{192,256},{256,320},{320,384},{384,448},... | collective-permute-start | bytes 1769480 | tf_op jit(solution)/shard_map/ppermute | solution.py:19
  12.1 15.5 %copy-start.1 = (bf16[1,384,384]{1,2,0:T(8,128)(2,1)}, bf16[1,384,384]{1,2,0:T(8,128)(2,1)S(1)}, u32[]{:S(2)}) copy-start(bf16[1,384,384]{1,2,0:T(8,128)(2,1)S(1)} %copy.51) | copy-start | bytes 884740
  22.0 0.7 copy-start.5
  22.0 0.7 copy-start.6
  30.6 40.4 %copy-start.2 = (bf16[1,384,384]{1,2,0:T(8,128)(2,1)S(1)}, bf16[1,384,384]{1,2,0:T(8,128)(2,1)}, u32[]{:S(2)}) copy-start(bf16[1,384,384]{1,2,0:T(8,128)(2,1)} %copy-done.1) | copy-start | bytes 884740
  31.0 5.9 %collective-permute-start.4 = (f32[256]{0:T(256)S(1)}, f32[256]{0:T(256)S(1)}, u32[]{:S(2)}, u32[]{:S(2)}) collective-permute-start(f32[256]{0:T(256)S(1)} %pad_maximum_fusion.4), channel_id=1, source_target_pairs={{0,64},{64,0},{128,192},{192,128},{256,320},{320,256},{384,448},{4... | collective-permute-start | bytes 3080 | tf_op jit(solution)/shard_map/ppermute | solution.py:31
  36.9 7.3 %collective-permute-start.5 = (f32[256]{0:T(256)S(1)}, f32[256]{0:T(256)S(1)}, u32[]{:S(2)}, u32[]{:S(2)}) collective-permute-start(f32[256]{0:T(256)S(1)} %fusion.12), channel_id=1, source_target_pairs={{0,128},{64,192},{128,0},{192,64},{256,384},{320,448},{384,256},{4... | collective-permute-start | bytes 3080 | tf_op jit(solution)/shard_map/ppermute | solution.py:31
  44.3 10.9 %collective-permute-start.6 = (f32[256]{0:T(256)S(1)}, f32[256]{0:T(256)S(1)}, u32[]{:S(2)}, u32[]{:S(2)}) collective-permute-start(f32[256]{0:T(256)S(1)} %add.85), channel_id=1, source_target_pairs={{0,256},{64,320},{128,384},{192,448},{256,0},{320,64},{384,128},{4... | collective-permute-start | bytes 3080 | tf_op jit(solution)/shard_map/ppermute | solution.py:31
  55.2 17.6 %collective-permute-start.7 = (f32[256]{0:T(256)S(1)}, f32[256]{0:T(256)S(1)}, u32[]{:S(2)}, u32[]{:S(2)}) collective-permute-start(f32[256]{0:T(256)S(1)} %add.86), channel_id=1, source_target_pairs={{0,512},{64,576},{128,640},{192,704},{256,768},{320,832},{384,896}... | collective-permute-start | bytes 3080 | tf_op jit(solution)/shard_map/ppermute | solution.py:31
  72.9 3.0 %collective-permute-start.8 = (f32[256]{0:T(256)S(1)}, f32[256]{0:T(256)S(1)}, u32[]{:S(2)}, u32[]{:S(2)}) collective-permute-start(f32[256]{0:T(256)S(1)} %add.87), channel_id=1, source_target_pairs={{0,16},{16,0},{32,48},{48,32},{1,17},{17,1},{33,49},{49,33},{2,18}... | collective-permute-start | bytes 3080 | tf_op jit(solution)/shard_map/ppermute | solution.py:31
  75.9 21.7 %collective-permute-start.9 = (f32[256]{0:T(256)S(1)}, f32[256]{0:T(256)S(1)}, u32[]{:S(2)}, u32[]{:S(2)}) collective-permute-start(f32[256]{0:T(256)S(1)} %add.88), channel_id=1, source_target_pairs={{0,544},{16,560},{32,512},{48,528},{64,608},{80,624},{96,576},{112... | collective-permute-start | bytes 3080 | tf_op jit(solution)/shard_map/ppermute | solution.py:31
  97.6 10.2 %collective-permute-start.10 = (f32[256]{0:T(256)S(1)}, f32[256]{0:T(256)S(1)}, u32[]{:S(2)}, u32[]{:S(2)}) collective-permute-start(f32[256]{0:T(256)S(1)} %add.89), channel_id=1, source_target_pairs={{0,1},{1,0},{2,3},{3,2},{4,5},{5,4},{6,7},{7,6},{8,9},{9,8},{10,11... | collective-permute-start | bytes 3080 | tf_op jit(solution)/shard_map/ppermute | solution.py:31
  101.1 28.4 %collective-permute-start.3 = (bf16[1,384,768]{1,2,0:T(8,128)(2,1)}, bf16[1,384,768]{1,2,0:T(8,128)(2,1)}, u32[]{:S(2)}, u32[]{:S(2)}) collective-permute-start(bf16[1,384,768]{1,2,0:T(8,128)(2,1)} %pad_maximum_fusion.3), channel_id=1, source_target_pairs={{64,0},{128,64},{192,128},{256,192},{320,256},{384,320},{448,384},... | collective-permute-start | bytes 1769480 | tf_op jit(solution)/shard_map/ppermute | solution.py:187
  102.4 27.1 %collective-permute-start.2 = (bf16[1,384,768]{1,2,0:T(8,128)(2,1)}, bf16[1,384,768]{1,2,0:T(8,128)(2,1)}, u32[]{:S(2)}, u32[]{:S(2)}) collective-permute-start(bf16[1,384,768]{1,2,0:T(8,128)(2,1)} %pad_maximum_fusion.2), channel_id=1, source_target_pairs={{0,64},{64,128},{128,192},{192,256},{256,320},{320,384},{384,448},... | collective-permute-start | bytes 1769480 | tf_op jit(solution)/shard_map/ppermute | solution.py:184
  107.8 6.7 %collective-permute-start.11 = (f32[256]{0:T(256)S(1)}, f32[256]{0:T(256)S(1)}, u32[]{:S(2)}, u32[]{:S(2)}) collective-permute-start(f32[256]{0:T(256)S(1)} %add.90), channel_id=1, source_target_pairs={{0,3},{1,2},{2,1},{3,0},{4,7},{5,6},{6,5},{7,4},{8,11},{9,10},{10,... | collective-permute-start | bytes 3080 | tf_op jit(solution)/shard_map/ppermute | solution.py:31
  114.5 5.5 %collective-permute-start.12 = (f32[256]{0:T(256)S(1)}, f32[256]{0:T(256)S(1)}, u32[]{:S(2)}, u32[]{:S(2)}) collective-permute-start(f32[256]{0:T(256)S(1)} %add.91), channel_id=1, source_target_pairs={{0,4},{1,5},{2,6},{3,7},{4,0},{5,1},{6,2},{7,3},{8,12},{9,13},{10,... | collective-permute-start | bytes 3080 | tf_op jit(solution)/shard_map/ppermute | solution.py:31
  119.9 8.4 %collective-permute-start.13 = (f32[256]{0:T(256)S(1)}, f32[256]{0:T(256)}, u32[]{:S(2)}, u32[]{:S(2)}) collective-permute-start(f32[256]{0:T(256)S(1)} %add.92), channel_id=1, source_target_pairs={{0,12},{1,13},{2,14},{3,15},{4,8},{5,9},{6,10},{7,11},{8,4},{9,5},... | collective-permute-start | bytes 3080 | tf_op jit(solution)/shard_map/ppermute | solution.py:31
  130.9 4.6 %copy-start.7 = (f32[256]{0:T(256)S(1)}, f32[256]{0:T(256)}, u32[]{:S(2)}) copy-start(f32[256]{0:T(256)} %add.93) | copy-start | bytes 3076
  135.5 1.7 %copy-start = (f32[1,384,384]{1,2,0:T(8,128)S(1)}, f32[1,384,384]{1,2,0:T(8,128)}, u32[]{:S(2)}) copy-start(f32[1,384,384]{1,2,0:T(8,128)} %get-tuple-element.40) | copy-start | bytes 1769476

commit v6 on v5

--- a/solution.py
+++ b/solution.py
@@ -128,14 +128,19 @@
     head_count = columns // head_size
     score_scale = 1.0 / math.sqrt(head_size)
     q_unit, q_factor, q_norm = normalize(queries, q_gain)
+    k_unit, k_factor, k_norm = normalize(keys, k_gain)
     packed = jnp.concatenate([keys, values], axis=2)
-    extended = extended_2(packed, (("seq", 1),), tile_rows)
-    k_unit_all, k_factor_all, key_all = normalize(extended[..., :columns], k_gain)
-    k_unit = k_unit_all[:, tile_rows : 2 * tile_rows]
-    k_factor = k_factor_all[:, tile_rows : 2 * tile_rows]
+    tile_count = lax.axis_size("seq")
+    ends = tile_count - 1
+    from_left = lax.ppermute(packed, "seq", [(i, i + 1) for i in range(ends)])
+    from_right = lax.ppermute(packed, "seq", [(i + 1, i) for i in range(ends)])
+    left_unit, _, left_norm = normalize(from_left[..., :columns], k_gain)
+    right_unit, _, right_norm = normalize(from_right[..., :columns], k_gain)
+    k_unit_all = jnp.concatenate([left_unit, k_unit, right_unit], axis=1)
+    key_all = jnp.concatenate([left_norm, k_norm, right_norm], axis=1)
+    extended = jnp.concatenate([from_left, packed, from_right], axis=1)
     value_all = extended[..., columns:].reshape(sample_count, 3 * tile_rows, head_count, head_size)
     tile_index = lax.axis_index("seq")
-    tile_count = lax.axis_size("seq")
     listing = window[:, 0, :]
 
     def listed(target):
@@ -180,7 +185,6 @@
         ]
     )
     gain_totals = butterfly_sum(gain_terms, gain_stages())
-    ends = tile_count - 1
     from_left = lax.ppermute(
         pack_terms(right_terms[0], right_terms[1]), "seq", [(i, i + 1) for i in range(ends)]
     )

time: 141 us -> 160 us (1.13)
  waiting for transfers between devices: 20.2 us -> 29.1 us
  other arithmetic: 13.9 us -> 21.9 us
  local copies, waits for them, and re-layouts: 12 us -> 15.6 us
  starting transfers between devices: 83.5 us -> 80 us
  matrix products: 7.48 us -> 9.2 us
    ppermute x10, waiting for transfers between devices: 11.1 us -> 23.5 us  [butterfly_sum(): lax.ppermute(value, axes, [(i, i ^ mask) for i in range(count)])]
    reshape x0 -> x7, local copies, waits for them, and re-layouts: none -> 5.13 us  [the longest x6 4.9 us: normalize(): raw_rows.astype(jnp.float32)]
    concatenate x3 -> x4, other arithmetic: 0.23 us -> 5.17 us  [the longest x3 4.09 us: per_device(): k_unit_all = jnp.concatenate([left_unit, k_unit, right_unit], axis=1)]
    ppermute x2, waiting for transfers between devices: 9.02 us -> 5.63 us  [the longest x1 5.19 us: per_device(): from_right = lax.ppermute(packed, 'seq', [(i + 1, i) for i in range(ends)])]
    convert_element_type x0 -> x2, other arithmetic: none -> 2.86 us  [the longest x1 1.59 us: normalize(): return (unit_rows, factor, (unit_rows * gain_vector).astype(jnp.bfloat16))]
    ppermute x1, starting transfers between devices: 5.37 us -> 2.89 us  [per_device(): lax.ppermute(pack_terms(right_terms[0], right_terms[1]), 'seq', [(i, i +...]
    ppermute x10, starting transfers between devices: 71 us -> 69.2 us  [butterfly_sum(): lax.ppermute(value, axes, [(i, i ^ mask) for i in range(count)])]
    unnamed x26 -> x80, local copies, waits for them, and re-layouts: 10.8 us -> 9.59 us
  transfers between devices with their start and end apart: 14 -> 14, of which waited for: 9 -> 10; matrix products, arithmetic and copies ran while one was open for 8% -> 6% of each run, Pallas kernels for 0% -> 0%
where the time goes in v6:
time: 160 us; the launch traced here: 159 us
  starting transfers between devices  80 us (50%)
  waiting for transfers between devices  29.1 us (18%)
  other arithmetic  21.9 us (14%)
  local copies, waits for them, and re-layouts  15.6 us (10%)
  matrix products  9.2 us (6%)
  between operations  3.31 us (2%)
    ppermute x10, starting transfers between devices, butterfly_sum(): lax.ppermute(value, axes, [(i, i ^ mask) for i in range(count)])  69.2 us
    ppermute x10, waiting for transfers between devices, butterfly_sum(): lax.ppermute(value, axes, [(i, i ^ mask) for i in range(count)])  23.5 us
    unnamed x80, local copies, waits for them, and re-layouts  9.59 us
    ppermute x1, starting transfers between devices, per_device(): from_left = lax.ppermute(packed, 'seq', [(i, i + 1) for i in range(ends)])  5.38 us
    ppermute x1, waiting for transfers between devices, per_device(): from_right = lax.ppermute(packed, 'seq', [(i + 1, i) for i in range(ends)])  5.19 us
    reshape x6, local copies, waits for them, and re-layouts, normalize(): raw_rows.astype(jnp.float32)  4.9 us
    concatenate x3, other arithmetic, per_device(): k_unit_all = jnp.concatenate([left_unit, k_unit, right_unit], axis=1)  4.09 us
  transfers between devices with their start and end apart: 14, of which 10 were waited for; matrix products, arithmetic and copies ran while one was open for 6% of the time, Pallas kernels for 0%

profile of v6, /device:TPU:24, one launch (start us, length us, event | category | flops | bytes accessed | tf_op | source)
XLA Modules:
  0.0 159.2 jit_solution(7377393922256586476)
XLA Ops:
  0.7 1.2 copy.28
  1.9 1.2 copy.29
  3.1 0.9 pad_maximum_fusion.3
  4.0 1.3 collective-permute-start.1
  5.3 5.4 %collective-permute-start = (bf16[1,384,768]{1,2,0:T(8,128)(2,1)}, bf16[1,384,768]{1,2,0:T(8,128)(2,1)}, u32[]{:S(2)}, u32[]{:S(2)}) collective-permute-start(bf16[1,384,768]{1,2,0:T(8,128)(2,1)} %pad_maximum_fusion.3), channel_id=1, source_target_pairs={{0,64},{64,128},{128,192},{192,256},{256,320},{320,384},{384,448},... | collective-permute-start | bytes 1769480 | tf_op jit(solution)/shard_map/ppermute | solution.py:135
  10.7 0.7 compare_reduce_fusion.2
  13.6 0.9 copy.35
  15.0 1.1 copy.45
  16.2 5.2 %collective-permute-done.1 = bf16[1,384,768]{1,2,0:T(8,128)(2,1)S(1)} collective-permute-done((bf16[1,384,768]{1,2,0:T(8,128)(2,1)}, bf16[1,384,768]{1,2,0:T(8,128)(2,1)S(1)}, u32[]{:S(2)}, u32[]{:S(2)}) %collective-permute-start.1) | collective-permute-done | bytes 589856 | tf_op jit(solution)/shard_map/ppermute | solution.py:136
  21.7 0.5 copy-done.18
  22.2 0.4 collective-permute-done
  22.7 1.0 slice_convert_fusion.3
  23.7 1.1 copy.30
  24.9 1.6 multiply_convert_fusion.5
  26.5 1.2 fusion.18
  27.7 1.2 exponential_reduce_fusion
  28.9 1.0 exponential_convert_fusion
  30.1 1.1 pad_maximum_fusion
  31.2 1.6 %multiply_reduce_fusion.3 = (f32[3,384]{1,0:T(4,128)S(1)}, bf16[3,384,128]{1,2,0:T(8,128)(2,1)}) fusion(bf16[3,1,384,128]{2,3,0,1:T(8,128)(2,1)S(1)} %bitcast.104, bf16[3,384,1152]{2,1,0:T(8,128)(2,1)S(1)} %exponential_convert_fusion, bf16[3,1152,128]{1,2,0:T(8,128)(2,1)S(1)} %bitcast.102), kind=kOutput, calls=%fused_computation.35 | convolution fusion | flops 340474752 | bytes 4133376 | tf_op jit(solution)/shard_map/vmap(sqk,skd->sqd)/dot_general | solution.py:83
  32.8 1.0 fusion
  33.8 2.4 %multiply_reduce_fusion.1 = (f32[128]{0:T(128)}, f32[384,3]{0,1:T(4,128)}, f32[1,384,3,128]{1,3,2,0:T(8,128)}) fusion(f32[1,384,3,128]{1,3,2,0:T(8,128)S(1)} %bitcast.90, f32[384,3]{0,1:T(4,128)S(1)} %add_rsqrt_fusion.3, f32[128]{0:T(128)S(1)} %copy-done.33, bf16[3,384,1152]{2,1,0:T(8,128)(2,1)S(1)} %fusion, ...), kind=kOutput, calls=%fused_computation.31 | convolution fusion | flops 343423744 | bytes 4728832 | tf_op jit(solution)/shard_map/vmap(sqk,skd->sqd)/dot_general | solution.py:96
  36.1 1.1 fusion.1
  37.3 1.3 fusion.14
  38.6 0.5 copy-done
  39.1 1.0 multiply_bitcast_fusion.1
  40.1 1.0 copy.46
  41.2 2.1 %multiply_bitcast_fusion = f32[1,384,3,128]{3,1,2,0:T(8,128)} fusion(f32[384,3,128]{2,0,1:T(8,128)} %copy.46, f32[384,3]{0,1:T(4,128)} %copy-done.27), kind=kLoop, calls=%fused_computation.28 | loop fusion | flops 147456 | bytes 1184256 | tf_op jit(solution)/shard_map/concatenate | solution.py:139
  43.3 1.3 copy.44
  44.6 0.9 multiply_bitcast_fusion.2
  45.6 1.9 %fusion.19 = (bf16[1,1152,3,128]{1,3,2,0:T(8,128)(2,1)S(1)}, f32[1,1152,3,128]{1,3,2,0:T(8,128)}) fusion(bf16[384,3,128]{0,2,1:T(8,128)(2,1)S(1)} %bitcast.106, bf16[3,384,1152]{2,1,0:T(8,128)(2,1)S(1)} %exponential_convert_fusion), kind=kOutput, calls=%fused_computation.73 | convolution fusion | flops 340180992 | bytes 5603328 | tf_op jit(solution)/shard_map/hsqk,sqhd->skhd/dot_general | solution.py:107
  47.7 0.5 fusion.2
  48.3 0.6 pad_maximum_fusion.6
  48.9 4.5 %collective-permute-start.4 = (f32[256]{0:T(256)}, f32[256]{0:T(256)}, u32[]{:S(2)}, u32[]{:S(2)}) collective-permute-start(f32[256]{0:T(256)} %pad_maximum_fusion.6), channel_id=1, source_target_pairs={{0,64},{64,0},{128,192},{192,128},{256,320},{320,256},{384,448},{4... | collective-permute-start | bytes 3080 | tf_op jit(solution)/shard_map/ppermute | solution.py:31
  54.0 2.9 %collective-permute-start.2 = (bf16[1,384,768]{1,2,0:T(8,128)(2,1)S(1)}, bf16[1,384,768]{1,2,0:T(8,128)(2,1)}, u32[]{:S(2)}, u32[]{:S(2)}) collective-permute-start(bf16[1,384,768]{1,2,0:T(8,128)(2,1)S(1)} %pad_maximum_fusion.4), channel_id=1, source_target_pairs={{0,64},{64,128},{128,192},{192,256},{256,320},{320,384},{384,448},... | collective-permute-start | bytes 1769480 | tf_op jit(solution)/shard_map/ppermute | solution.py:188
  56.9 0.9 pad_maximum_fusion.5
  57.8 1.3 collective-permute-start.3
  59.1 0.7 fusion.13
  59.8 7.6 %collective-permute-start.5 = (f32[256]{0:T(256)S(1)}, f32[256]{0:T(256)S(1)}, u32[]{:S(2)}, u32[]{:S(2)}) collective-permute-start(f32[256]{0:T(256)S(1)} %fusion.13), channel_id=1, source_target_pairs={{0,128},{64,192},{128,0},{192,64},{256,384},{320,448},{384,256},{4... | collective-permute-start | bytes 3080 | tf_op jit(solution)/shard_map/ppermute | solution.py:31
  67.4 9.1 %collective-permute-done.5 = f32[256]{0:T(256)S(1)} collective-permute-done((f32[256]{0:T(256)S(1)}, f32[256]{0:T(256)S(1)}, u32[]{:S(2)}, u32[]{:S(2)}) %collective-permute-start.5) | collective-permute-done | bytes 1056 | tf_op jit(solution)/shard_map/ppermute | solution.py:31
  76.5 9.1 %collective-permute-start.6 = (f32[256]{0:T(256)S(1)}, f32[256]{0:T(256)S(1)}, u32[]{:S(2)}, u32[]{:S(2)}) collective-permute-start(f32[256]{0:T(256)S(1)} %add.90), channel_id=1, source_target_pairs={{0,256},{64,320},{128,384},{192,448},{256,0},{320,64},{384,128},{4... | collective-permute-start | bytes 3080 | tf_op jit(solution)/shard_map/ppermute | solution.py:31
  85.6 1.5 collective-permute-done.6
  87.2 14.7 %collective-permute-start.7 = (f32[256]{0:T(256)S(1)}, f32[256]{0:T(256)S(1)}, u32[]{:S(2)}, u32[]{:S(2)}) collective-permute-start(f32[256]{0:T(256)S(1)} %add.91), channel_id=1, source_target_pairs={{0,512},{64,576},{128,640},{192,704},{256,768},{320,832},{384,896}... | collective-permute-start | bytes 3080 | tf_op jit(solution)/shard_map/ppermute | solution.py:31
  101.9 1.5 collective-permute-done.7
  103.4 1.9 %collective-permute-start.8 = (f32[256]{0:T(256)S(1)}, f32[256]{0:T(256)S(1)}, u32[]{:S(2)}, u32[]{:S(2)}) collective-permute-start(f32[256]{0:T(256)S(1)} %add.92), channel_id=1, source_target_pairs={{0,16},{16,0},{32,48},{48,32},{1,17},{17,1},{33,49},{49,33},{2,18}... | collective-permute-start | bytes 3080 | tf_op jit(solution)/shard_map/ppermute | solution.py:31
  105.3 1.1 collective-permute-done.8
  106.4 18.5 %collective-permute-start.9 = (f32[256]{0:T(256)S(1)}, f32[256]{0:T(256)S(1)}, u32[]{:S(2)}, u32[]{:S(2)}) collective-permute-start(f32[256]{0:T(256)S(1)} %add.93), channel_id=1, source_target_pairs={{0,544},{16,560},{32,512},{48,528},{64,608},{80,624},{96,576},{112... | collective-permute-start | bytes 3080 | tf_op jit(solution)/shard_map/ppermute | solution.py:31
  124.9 1.5 collective-permute-done.9
  126.5 2.6 %collective-permute-start.10 = (f32[256]{0:T(256)S(1)}, f32[256]{0:T(256)S(1)}, u32[]{:S(2)}, u32[]{:S(2)}) collective-permute-start(f32[256]{0:T(256)S(1)} %add.94), channel_id=1, source_target_pairs={{0,1},{1,0},{2,3},{3,2},{4,5},{5,4},{6,7},{7,6},{8,9},{9,8},{10,11... | collective-permute-start | bytes 3080 | tf_op jit(solution)/shard_map/ppermute | solution.py:31
  129.1 2.8 %collective-permute-done.10 = f32[256]{0:T(256)S(1)} collective-permute-done((f32[256]{0:T(256)S(1)}, f32[256]{0:T(256)S(1)}, u32[]{:S(2)}, u32[]{:S(2)}) %collective-permute-start.10) | collective-permute-done | bytes 1056 | tf_op jit(solution)/shard_map/ppermute | solution.py:31
  131.9 2.1 %collective-permute-start.11 = (f32[256]{0:T(256)S(1)}, f32[256]{0:T(256)S(1)}, u32[]{:S(2)}, u32[]{:S(2)}) collective-permute-start(f32[256]{0:T(256)S(1)} %add.95), channel_id=1, source_target_pairs={{0,3},{1,2},{2,1},{3,0},{4,7},{5,6},{6,5},{7,4},{8,11},{9,10},{10,... | collective-permute-start | bytes 3080 | tf_op jit(solution)/shard_map/ppermute | solution.py:31
  134.1 4.5 %collective-permute-done.11 = f32[256]{0:T(256)S(1)} collective-permute-done((f32[256]{0:T(256)S(1)}, f32[256]{0:T(256)S(1)}, u32[]{:S(2)}, u32[]{:S(2)}) %collective-permute-start.11) | collective-permute-done | bytes 1056 | tf_op jit(solution)/shard_map/ppermute | solution.py:31
  138.6 3.4 %collective-permute-start.12 = (f32[256]{0:T(256)S(1)}, f32[256]{0:T(256)S(1)}, u32[]{:S(2)}, u32[]{:S(2)}) collective-permute-start(f32[256]{0:T(256)S(1)} %add.96), channel_id=1, source_target_pairs={{0,4},{1,5},{2,6},{3,7},{4,0},{5,1},{6,2},{7,3},{8,12},{9,13},{10,... | collective-permute-start | bytes 3080 | tf_op jit(solution)/shard_map/ppermute | solution.py:31
  142.0 0.7 broadcast_multiply_fusion.1
  142.7 1.3 collective-permute-done.12
  144.0 4.7 %collective-permute-start.13 = (f32[256]{0:T(256)S(1)}, f32[256]{0:T(256)S(1)}, u32[]{:S(2)}, u32[]{:S(2)}) collective-permute-start(f32[256]{0:T(256)S(1)} %add.97), channel_id=1, source_target_pairs={{0,12},{1,13},{2,14},{3,15},{4,8},{5,9},{6,10},{7,11},{8,4},{9,5},... | collective-permute-start | bytes 3080 | tf_op jit(solution)/shard_map/ppermute | solution.py:31
  148.7 0.8 multiply_convert_fusion.2
  149.6 0.9 copy.49
  150.5 0.9 copy.50
  151.4 1.2 convert_add_fusion
  152.7 2.0 %fusion.4 = bf16[1,384,3,128]{1,3,2,0:T(8,128)(2,1)} fusion(f32[1,384,3,128]{1,3,2,0:T(8,128)S(1)} %bitcast.108, f32[1,1152,3,128]{1,3,2,0:T(8,128)} %get-tuple-element.50), kind=kLoop, calls=%fused_computation.19 | loop fusion | flops 294912 | bytes 1474560 | tf_op jit(solution)/shard_map/convert_element_type | solution.py:209
  154.7 1.8 %copy.52 = bf16[1,384,384]{2,1,0:T(8,128)(2,1)} copy(bf16[1,384,384]{1,2,0:T(8,128)(2,1)} %bitcast.113) | data formatting | bytes 589824
  156.7 0.5 slice_multiply_fusion
  157.3 0.4 multiply_reduce_fusion
  158.3 0.9 copy.51
  (111 shorter events, 3.3 us)
Async XLA Ops:
  0.6 10.1 %copy-start.35 = (s32[1,1,3]{2,1,0:T(1,128)S(1)}, s32[1,1,3]{2,1,0:T(1,128)}, u32[]{:S(2)}) copy-start(s32[1,1,3]{2,1,0:T(1,128)} %param.13) | copy-start | bytes 40
  0.6 12.9 %copy-start.23 = (bf16[1,384,384]{2,1,0:T(8,128)(2,1)S(1)}, bf16[1,384,384]{2,1,0:T(8,128)(2,1)}, u32[]{:S(2)}) copy-start(bf16[1,384,384]{2,1,0:T(8,128)(2,1)} %param.12) | copy-start | bytes 884740
  1.9 12.6 %copy-start.24 = (bf16[1,384,384]{2,1,0:T(8,128)(2,1)S(1)}, bf16[1,384,384]{2,1,0:T(8,128)(2,1)}, u32[]{:S(2)}) copy-start(bf16[1,384,384]{2,1,0:T(8,128)(2,1)} %param.7) | copy-start | bytes 884740
  3.1 11.6 %copy-start.9 = (bf16[1,384,384]{1,2,0:T(8,128)(2,1)}, bf16[1,384,384]{1,2,0:T(8,128)(2,1)S(1)}, u32[]{:S(2)}) copy-start(bf16[1,384,384]{1,2,0:T(8,128)(2,1)S(1)} %copy.29) | copy-start | bytes 884740
  4.0 17.3 %collective-permute-start.1 = (bf16[1,384,768]{1,2,0:T(8,128)(2,1)}, bf16[1,384,768]{1,2,0:T(8,128)(2,1)S(1)}, u32[]{:S(2)}, u32[]{:S(2)}) collective-permute-start(bf16[1,384,768]{1,2,0:T(8,128)(2,1)} %pad_maximum_fusion.3), channel_id=1, source_target_pairs={{64,0},{128,64},{192,128},{256,192},{320,256},{384,320},{448,384},... | collective-permute-start | bytes 1769480 | tf_op jit(solution)/shard_map/ppermute | solution.py:136
  5.3 17.3 %collective-permute-start = (bf16[1,384,768]{1,2,0:T(8,128)(2,1)}, bf16[1,384,768]{1,2,0:T(8,128)(2,1)}, u32[]{:S(2)}, u32[]{:S(2)}) collective-permute-start(bf16[1,384,768]{1,2,0:T(8,128)(2,1)} %pad_maximum_fusion.3), channel_id=1, source_target_pairs={{0,64},{64,128},{128,192},{192,256},{256,320},{320,384},{384,448},... | collective-permute-start | bytes 1769480 | tf_op jit(solution)/shard_map/ppermute | solution.py:135
  14.7 21.4 %copy-start.4 = (f32[1,384,384]{1,2,0:T(8,128)}, f32[1,384,384]{1,2,0:T(8,128)S(1)}, u32[]{:S(2)}) copy-start(f32[1,384,384]{1,2,0:T(8,128)S(1)} %convert_element_type.125) | copy-start | bytes 1769476
  15.0 9.9 %copy-start.2 = (f32[1,384,3,128]{3,1,2,0:T(8,128)}, f32[1,384,3,128]{3,1,2,0:T(8,128)S(1)}, u32[]{:S(2)}) copy-start(f32[1,384,3,128]{3,1,2,0:T(8,128)S(1)} %copy.32) | copy-start | bytes 1769476
  21.4 0.8 copy-start.18
  21.4 3.4 %copy-start.6 = (f32[1,384,384]{1,2,0:T(8,128)}, f32[1,384,384]{1,2,0:T(8,128)S(1)}, u32[]{:S(2)}) copy-start(f32[1,384,384]{1,2,0:T(8,128)S(1)} %slice_convert_fusion.2) | copy-start | bytes 1769476
  21.7 3.2 %copy-start.28 = (f32[128]{0:T(128)S(1)}, f32[128]{0:T(128)}, u32[]{:S(2)}) copy-start(f32[128]{0:T(128)} %param.11) | copy-start | bytes 1540
  23.7 2.8 %copy-start.8 = (f32[1,384,384]{1,2,0:T(8,128)}, f32[1,384,384]{1,2,0:T(8,128)S(1)}, u32[]{:S(2)}) copy-start(f32[1,384,384]{1,2,0:T(8,128)S(1)} %slice_convert_fusion.3) | copy-start | bytes 1769476
  23.7 2.7 %copy-start.32 = (f32[128]{0:T(128)S(1)}, f32[128]{0:T(128)}, u32[]{:S(2)}) copy-start(f32[128]{0:T(128)} %param.10) | copy-start | bytes 1540
  24.8 2.9 %copy-start.26 = (f32[384,3]{0,1:T(4,128)}, f32[384,3]{0,1:T(4,128)S(1)}, u32[]{:S(2)}) copy-start(f32[384,3]{0,1:T(4,128)S(1)} %add_rsqrt_fusion.2) | copy-start | bytes 13828
  24.8 2.9 %copy-start.27 = (f32[384,3]{0,1:T(4,128)}, f32[384,3]{0,1:T(4,128)S(1)}, u32[]{:S(2)}) copy-start(f32[384,3]{0,1:T(4,128)S(1)} %get-tuple-element.51) | copy-start | bytes 13828
  28.9 1.0 copy-start.10
  28.9 1.2 copy-start.19
  30.1 1.1 copy-start.11
  32.8 1.0 copy-start.33
  37.3 1.8 %copy-start = (f32[1,1152,3,128]{3,1,2,0:T(8,128)}, f32[1,1152,3,128]{3,1,2,0:T(8,128)S(1)}, u32[]{:S(2)}) copy-start(f32[1,1152,3,128]{3,1,2,0:T(8,128)S(1)} %fusion.1) | copy-start | bytes 5308420
  37.3 1.8 %copy-start.13 = (f32[384,3,128]{2,0,1:T(8,128)S(1)}, f32[384,3,128]{2,0,1:T(8,128)}, u32[]{:S(2)}) copy-start(f32[384,3,128]{2,0,1:T(8,128)} %copy.45) | copy-start | bytes 1769476
  37.3 2.9 %copy-start.7 = (f32[1,384,384]{1,2,0:T(8,128)S(1)}, f32[1,384,384]{1,2,0:T(8,128)}, u32[]{:S(2)}) copy-start(f32[1,384,384]{1,2,0:T(8,128)} %copy-done.6) | copy-start | bytes 1769476
  41.2 4.4 %copy-start.12 = (bf16[1,384,384]{1,2,0:T(8,128)(2,1)S(1)}, bf16[1,384,384]{1,2,0:T(8,128)(2,1)}, u32[]{:S(2)}) copy-start(bf16[1,384,384]{1,2,0:T(8,128)(2,1)} %copy.35) | copy-start | bytes 884740
  45.5 2.0 %slice-start = ((f32[1,1152,3,128]{3,1,2,0:T(8,128)}), f32[1,384,3,128]{3,1,2,0:T(8,128)S(1)}, s32[]{:S(2)}) async-start(f32[1,1152,3,128]{3,1,2,0:T(8,128)} %copy-done), calls=%async_computation | async-start | bytes 1179648 | tf_op jit(solution)/shard_map/slice | solution.py:166
  45.5 2.0 %copy-start.14 = (f32[1,384,3,128]{3,1,2,0:T(8,128)S(1)}, f32[1,384,3,128]{3,1,2,0:T(8,128)}, u32[]{:S(2)}) copy-start(f32[1,384,3,128]{3,1,2,0:T(8,128)} %multiply_bitcast_fusion.1) | copy-start | bytes 1769476
  45.6 2.0 %copy-start.15 = (f32[1,384,3,128]{3,1,2,0:T(8,128)S(1)}, f32[1,384,3,128]{3,1,2,0:T(8,128)}, u32[]{:S(2)}) copy-start(f32[1,384,3,128]{3,1,2,0:T(8,128)} %multiply_bitcast_fusion) | copy-start | bytes 1769476
  45.6 2.0 %copy-start.16 = (f32[1,384,3,128]{3,1,2,0:T(8,128)S(1)}, f32[1,384,3,128]{3,1,2,0:T(8,128)}, u32[]{:S(2)}) copy-start(f32[1,384,3,128]{3,1,2,0:T(8,128)} %get-tuple-element.29) | copy-start | bytes 1769476
  45.6 2.1 %copy-start.17 = (f32[1,384,3,128]{3,1,2,0:T(8,128)S(1)}, f32[1,384,3,128]{3,1,2,0:T(8,128)}, u32[]{:S(2)}) copy-start(f32[1,384,3,128]{3,1,2,0:T(8,128)} %get-tuple-element.33) | copy-start | bytes 1769476
  47.7 0.7 copy-start.34
  47.7 5.8 %copy-start.21 = (bf16[1,384,3,128]{3,1,2,0:T(8,128)(2,1)S(1)}, bf16[1,384,3,128]{3,1,2,0:T(8,128)(2,1)}, u32[]{:S(2)}) copy-start(bf16[1,384,3,128]{3,1,2,0:T(8,128)(2,1)} %get-tuple-element.30) | copy-start | bytes 884740
  47.7 6.0 %copy-start.20 = (bf16[1,384,3,128]{3,1,2,0:T(8,128)(2,1)S(1)}, bf16[1,384,3,128]{3,1,2,0:T(8,128)(2,1)}, u32[]{:S(2)}) copy-start(bf16[1,384,3,128]{3,1,2,0:T(8,128)(2,1)} %get-tuple-element.34) | copy-start | bytes 884740
  48.1 5.3 %copy-start.30 = (f32[128]{0:T(128)}, f32[128]{0:T(128)S(1)}, u32[]{:S(2)}) copy-start(f32[128]{0:T(128)S(1)} %fusion.2) | copy-start | bytes 1540
  48.9 10.2 %collective-permute-start.4 = (f32[256]{0:T(256)}, f32[256]{0:T(256)}, u32[]{:S(2)}, u32[]{:S(2)}) collective-permute-start(f32[256]{0:T(256)} %pad_maximum_fusion.6), channel_id=1, source_target_pairs={{0,64},{64,0},{128,192},{192,128},{256,320},{320,256},{384,448},{4... | collective-permute-start | bytes 3080 | tf_op jit(solution)/shard_map/ppermute | solution.py:31
  53.4 95.3 %copy-start.5 = (f32[1,384,384]{1,2,0:T(8,128)S(1)}, f32[1,384,384]{1,2,0:T(8,128)}, u32[]{:S(2)}) copy-start(f32[1,384,384]{1,2,0:T(8,128)} %copy-done.4) | copy-start | bytes 1769476
  53.5 95.3 %copy-start.22 = (f32[1,384,3,128]{1,3,2,0:T(8,128)S(1)}, f32[1,384,3,128]{1,3,2,0:T(8,128)}, u32[]{:S(2)}) copy-start(f32[1,384,3,128]{1,3,2,0:T(8,128)} %get-tuple-element.48) | copy-start | bytes 1769476
  53.9 5.2 %copy-start.31 = (f32[128]{0:T(128)S(1)}, f32[128]{0:T(128)}, u32[]{:S(2)}) copy-start(f32[128]{0:T(128)} %copy-done.30) | copy-start | bytes 1540
  53.9 95.6 %copy-start.25 = (bf16[3,384,128]{1,2,0:T(8,128)(2,1)S(1)}, bf16[3,384,128]{1,2,0:T(8,128)(2,1)}, u32[]{:S(2)}) copy-start(bf16[3,384,128]{1,2,0:T(8,128)(2,1)} %get-tuple-element.47) | copy-start | bytes 884740
  54.0 97.4 %collective-permute-start.2 = (bf16[1,384,768]{1,2,0:T(8,128)(2,1)S(1)}, bf16[1,384,768]{1,2,0:T(8,128)(2,1)}, u32[]{:S(2)}, u32[]{:S(2)}) collective-permute-start(bf16[1,384,768]{1,2,0:T(8,128)(2,1)S(1)} %pad_maximum_fusion.4), channel_id=1, source_target_pairs={{0,64},{64,128},{128,192},{192,256},{256,320},{320,384},{384,448},... | collective-permute-start | bytes 1769480 | tf_op jit(solution)/shard_map/ppermute | solution.py:188
  57.8 93.6 %collective-permute-start.3 = (bf16[1,384,768]{1,2,0:T(8,128)(2,1)}, bf16[1,384,768]{1,2,0:T(8,128)(2,1)S(1)}, u32[]{:S(2)}, u32[]{:S(2)}) collective-permute-start(bf16[1,384,768]{1,2,0:T(8,128)(2,1)} %pad_maximum_fusion.5), channel_id=1, source_target_pairs={{64,0},{128,64},{192,128},{256,192},{320,256},{384,320},{448,384},... | collective-permute-start | bytes 1769480 | tf_op jit(solution)/shard_map/ppermute | solution.py:191
  59.8 16.8 %collective-permute-start.5 = (f32[256]{0:T(256)S(1)}, f32[256]{0:T(256)S(1)}, u32[]{:S(2)}, u32[]{:S(2)}) collective-permute-start(f32[256]{0:T(256)S(1)} %fusion.13), channel_id=1, source_target_pairs={{0,128},{64,192},{128,0},{192,64},{256,384},{320,448},{384,256},{4... | collective-permute-start | bytes 3080 | tf_op jit(solution)/shard_map/ppermute | solution.py:31
  76.5 10.6 %collective-permute-start.6 = (f32[256]{0:T(256)S(1)}, f32[256]{0:T(256)S(1)}, u32[]{:S(2)}, u32[]{:S(2)}) collective-permute-start(f32[256]{0:T(256)S(1)} %add.90), channel_id=1, source_target_pairs={{0,256},{64,320},{128,384},{192,448},{256,0},{320,64},{384,128},{4... | collective-permute-start | bytes 3080 | tf_op jit(solution)/shard_map/ppermute | solution.py:31
  87.2 16.2 %collective-permute-start.7 = (f32[256]{0:T(256)S(1)}, f32[256]{0:T(256)S(1)}, u32[]{:S(2)}, u32[]{:S(2)}) collective-permute-start(f32[256]{0:T(256)S(1)} %add.91), channel_id=1, source_target_pairs={{0,512},{64,576},{128,640},{192,704},{256,768},{320,832},{384,896}... | collective-permute-start | bytes 3080 | tf_op jit(solution)/shard_map/ppermute | solution.py:31
  103.4 3.0 %collective-permute-start.8 = (f32[256]{0:T(256)S(1)}, f32[256]{0:T(256)S(1)}, u32[]{:S(2)}, u32[]{:S(2)}) collective-permute-start(f32[256]{0:T(256)S(1)} %add.92), channel_id=1, source_target_pairs={{0,16},{16,0},{32,48},{48,32},{1,17},{17,1},{33,49},{49,33},{2,18}... | collective-permute-start | bytes 3080 | tf_op jit(solution)/shard_map/ppermute | solution.py:31
  106.4 20.0 %collective-permute-start.9 = (f32[256]{0:T(256)S(1)}, f32[256]{0:T(256)S(1)}, u32[]{:S(2)}, u32[]{:S(2)}) collective-permute-start(f32[256]{0:T(256)S(1)} %add.93), channel_id=1, source_target_pairs={{0,544},{16,560},{32,512},{48,528},{64,608},{80,624},{96,576},{112... | collective-permute-start | bytes 3080 | tf_op jit(solution)/shard_map/ppermute | solution.py:31
  126.5 5.5 %collective-permute-start.10 = (f32[256]{0:T(256)S(1)}, f32[256]{0:T(256)S(1)}, u32[]{:S(2)}, u32[]{:S(2)}) collective-permute-start(f32[256]{0:T(256)S(1)} %add.94), channel_id=1, source_target_pairs={{0,1},{1,0},{2,3},{3,2},{4,5},{5,4},{6,7},{7,6},{8,9},{9,8},{10,11... | collective-permute-start | bytes 3080 | tf_op jit(solution)/shard_map/ppermute | solution.py:31
  131.9 6.7 %collective-permute-start.11 = (f32[256]{0:T(256)S(1)}, f32[256]{0:T(256)S(1)}, u32[]{:S(2)}, u32[]{:S(2)}) collective-permute-start(f32[256]{0:T(256)S(1)} %add.95), channel_id=1, source_target_pairs={{0,3},{1,2},{2,1},{3,0},{4,7},{5,6},{6,5},{7,4},{8,11},{9,10},{10,... | collective-permute-start | bytes 3080 | tf_op jit(solution)/shard_map/ppermute | solution.py:31
  138.6 5.5 %collective-permute-start.12 = (f32[256]{0:T(256)S(1)}, f32[256]{0:T(256)S(1)}, u32[]{:S(2)}, u32[]{:S(2)}) collective-permute-start(f32[256]{0:T(256)S(1)} %add.96), channel_id=1, source_target_pairs={{0,4},{1,5},{2,6},{3,7},{4,0},{5,1},{6,2},{7,3},{8,12},{9,13},{10,... | collective-permute-start | bytes 3080 | tf_op jit(solution)/shard_map/ppermute | solution.py:31
  144.0 7.3 %collective-permute-start.13 = (f32[256]{0:T(256)S(1)}, f32[256]{0:T(256)S(1)}, u32[]{:S(2)}, u32[]{:S(2)}) collective-permute-start(f32[256]{0:T(256)S(1)} %add.97), channel_id=1, source_target_pairs={{0,12},{1,13},{2,14},{3,15},{4,8},{5,9},{6,10},{7,11},{8,4},{9,5},... | collective-permute-start | bytes 3080 | tf_op jit(solution)/shard_map/ppermute | solution.py:31
  152.6 4.6 %copy-start.1 = (f32[1,1152,3,128]{3,1,2,0:T(8,128)S(1)}, f32[1,1152,3,128]{3,1,2,0:T(8,128)}, u32[]{:S(2)}) copy-start(f32[1,1152,3,128]{3,1,2,0:T(8,128)} %copy-done) | copy-start | bytes 5308420
  152.7 4.6 %copy-start.3 = (f32[1,384,3,128]{3,1,2,0:T(8,128)S(1)}, f32[1,384,3,128]{3,1,2,0:T(8,128)}, u32[]{:S(2)}) copy-start(f32[1,384,3,128]{3,1,2,0:T(8,128)} %copy-done.2) | copy-start | bytes 1769476
  152.7 4.6 %copy-start.29 = (f32[128]{0:T(128)S(1)}, f32[128]{0:T(128)}, u32[]{:S(2)}) copy-start(f32[128]{0:T(128)} %param.11) | copy-start | bytes 1540

commit v7 on v5

--- a/solution.py
+++ b/solution.py
@@ -146,17 +146,31 @@
     block_flags = jnp.stack([left_ok, listed(tile_index), right_ok], axis=1)
     allowed = jnp.repeat(block_flags, tile_rows, axis=1)
     grad_out = d_out.reshape(sample_count, tile_rows, head_count, head_size)
-    operands = (
-        jnp.moveaxis(q_norm, 2, 0),
-        jnp.moveaxis(key_all, 2, 0),
-        jnp.moveaxis(value_all, 2, 0),
-        jnp.moveaxis(grad_out, 2, 0),
-    )
-    results = jax.vmap(lambda per_head: head_pass(per_head, allowed, score_scale))(operands)
-    attended, log_total, row_inner, grad_query, attn_weights, grad_scores = results
-    attended = jnp.moveaxis(attended, 0, 2).reshape(sample_count, tile_rows, columns)
-    grad_qnorm = jnp.moveaxis(grad_query, 0, 2)
-    key_every, value_every = key_terms(grad_scores, attn_weights, q_norm, grad_out, score_scale)
+    per_head = []
+    for head in range(head_count):
+        operands = (
+            q_norm[:, :, head],
+            key_all[:, :, head],
+            value_all[:, :, head],
+            grad_out[:, :, head],
+        )
+        attended_h, _, _, grad_query_h, weights_h, grad_scores_h = head_pass(
+            operands, allowed, score_scale
+        )
+        key_h = (
+            jnp.einsum(
+                "sqk,sqd->skd", grad_scores_h, operands[0], preferred_element_type=jnp.float32
+            )
+            * score_scale
+        )
+        value_h = jnp.einsum(
+            "sqk,sqd->skd", weights_h, operands[3], preferred_element_type=jnp.float32
+        )
+        per_head.append((attended_h, grad_query_h, key_h, value_h))
+    attended = jnp.concatenate([part[0] for part in per_head], axis=2)
+    grad_qnorm = jnp.stack([part[1] for part in per_head], axis=2)
+    key_every = jnp.stack([part[2] for part in per_head], axis=2)
+    value_every = jnp.stack([part[3] for part in per_head], axis=2)
     left_terms = (key_every[:, :tile_rows], value_every[:, :tile_rows])
     own_terms = (key_every[:, tile_rows : 2 * tile_rows], value_every[:, tile_rows : 2 * tile_rows])
     right_terms = (key_every[:, 2 * tile_rows :], value_every[:, 2 * tile_rows :])

time: 141 us -> 136 us (0.965); the launches traced: 140 us -> 133 us
  local copies, waits for them, and re-layouts: 12 us -> 8.82 us
  starting transfers between devices: 83.5 us -> 80.6 us
  other arithmetic: 13.9 us -> 12.4 us
    ppermute x1, starting transfers between devices: 5.37 us -> 1.96 us  [per_device(): lax.ppermute(pack_terms(right_terms[0], right_terms[1]), 'seq', [(i, i +...]
    unnamed x26 -> x22, local copies, waits for them, and re-layouts: 10.8 us -> 7.82 us
    another operation x0 -> x3, other arithmetic: none -> 1.65 us  [the longest x1 1.35 us: per_device(): value_every = jnp.stack([part[3] for part in per_head], axis=2)]
    concatenate x2, other arithmetic: 1.77 us -> 0.12 us  [pack_terms(): jnp.concatenate([key_part.reshape(sample_count, tile_rows, -1), value_par...]
  transfers between devices with their start and end apart: 14 -> 14, of which waited for: 9 -> 11; matrix products, arithmetic and copies ran while one was open for 8% -> 5% of each run, Pallas kernels for 0% -> 0%
where the time goes in v7:
time: 136 us; the launch traced here: 133 us
  starting transfers between devices  80.6 us (59%)
  waiting for transfers between devices  20.9 us (15%)
  other arithmetic  12.4 us (9%)
  local copies, waits for them, and re-layouts  8.82 us (6%)
  matrix products  7.46 us (5%)
  between operations  3.1 us (2%)
    ppermute x10, starting transfers between devices, butterfly_sum(): lax.ppermute(value, axes, [(i, i ^ mask) for i in range(count)])  71.4 us
    ppermute x10, waiting for transfers between devices, butterfly_sum(): lax.ppermute(value, axes, [(i, i ^ mask) for i in range(count)])  12 us
    unnamed x22, local copies, waits for them, and re-layouts  7.82 us
    ppermute x1, waiting for transfers between devices, extended_2(): lax.ppermute(head, axis, [((i + 1) % count, i) for i in range(ends)])  7.75 us
    ppermute x1, starting transfers between devices, extended_2(): lax.ppermute(tail, axis, [(i, (i + 1) % count) for i in range(ends)])  4.58 us
  transfers between devices with their start and end apart: 14, of which 11 were waited for; matrix products, arithmetic and copies ran while one was open for 5% of the time, Pallas kernels for 0%

profile of v7, /device:TPU:24, one launch (start us, length us, event | category | flops | bytes accessed | tf_op | source)
XLA Modules:
  0.0 133.2 jit_solution(8034541527861170817)
XLA Ops:
  0.7 1.2 copy.45
  1.9 1.2 copy.46
  3.2 1.3 collective-permute-start.1
  4.5 4.6 %collective-permute-start = (bf16[1,384,768]{1,2,0:T(8,128)(2,1)S(1)}, bf16[1,384,768]{1,2,0:T(8,128)(2,1)S(1)}, u32[]{:S(2)}, u32[]{:S(2)}) collective-permute-start(bf16[1,384,768]{1,2,0:T(8,128)(2,1)S(1)} %pad_maximum_fusion.3), channel_id=1, source_target_pairs={{0,64},{64,128},{128,192},{192,256},{256,320},{320,384},{384,448},... | collective-permute-start | bytes 1769480 | tf_op jit(solution)/shard_map/ppermute | solution.py:19
  9.1 0.7 compare_reduce_fusion.2
  12.5 7.8 %collective-permute-done.1 = bf16[1,384,768]{1,2,0:T(8,128)(2,1)S(1)} collective-permute-done((bf16[1,384,768]{1,2,0:T(8,128)(2,1)S(1)}, bf16[1,384,768]{1,2,0:T(8,128)(2,1)S(1)}, u32[]{:S(2)}, u32[]{:S(2)}) %collective-permute-start.1) | collective-permute-done | bytes 589856 | tf_op jit(solution)/shard_map/ppermute | solution.py:21
  20.3 1.2 collective-permute-done
  22.0 0.5 copy-done.4
  22.5 1.4 %multiply_convert_fusion = (bf16[1,1152,3,128]{1,3,2,0:T(8,128)(2,1)S(1)}, f32[1,1152,3,128]{1,3,2,0:T(8,128)}) fusion(f32[128]{0:T(128)S(1)} %copy-done.4, f32[1,1152,3,128]{1,3,2,0:T(8,128)S(1)} %bitcast.181, f32[1152,3]{0,1:T(4,128)S(1)} %get-tuple-element.53), kind=kLoop, calls=%fused_computation.39 | loop fusion | flops 1327104 | bytes 4438016 | tf_op jit(solution)/shard_map/convert_element_type | solution.py:63
  23.9 0.5 fusion.30
  24.5 0.5 fusion.31
  25.0 0.5 fusion.32
  25.5 0.4 exponential_reduce_fusion
  26.3 0.4 exponential_reduce_fusion.1
  26.7 0.3 exponential_convert_fusion.1
  27.1 0.4 convolution_convert_fusion
  27.5 0.4 convolution_convert_fusion.1
  27.9 0.4 exponential_reduce_fusion.2
  28.3 0.3 exponential_convert_fusion.2
  28.7 0.4 multiply_reduce_fusion.6
  29.1 0.5 fusion.11
  29.6 0.4 fusion.18
  30.0 0.3 fusion.12
  30.3 0.5 fusion.10
  30.8 0.4 fusion.17
  31.2 0.3 fusion.13
  31.5 0.5 fusion.9
  32.0 0.4 fusion.16
  32.4 0.4 fusion.14
  33.2 0.9 copy-done
  34.5 0.7 slice-done
  35.2 0.3 fusion.15
  35.6 4.4 %collective-permute-start.4 = (f32[256]{0:T(256)S(1)}, f32[256]{0:T(256)S(1)}, u32[]{:S(2)}, u32[]{:S(2)}) collective-permute-start(f32[256]{0:T(256)S(1)} %pad_maximum_fusion.8), channel_id=1, source_target_pairs={{0,64},{64,0},{128,192},{192,128},{256,320},{320,256},{384,448},{4... | collective-permute-start | bytes 3080 | tf_op jit(solution)/shard_map/ppermute | solution.py:31
  40.0 0.3 convolution_bitcast_fusion
  40.3 1.2 collective-permute-done.4
  41.5 5.8 %collective-permute-start.5 = (f32[256]{0:T(256)S(1)}, f32[256]{0:T(256)S(1)}, u32[]{:S(2)}, u32[]{:S(2)}) collective-permute-start(f32[256]{0:T(256)S(1)} %fusion.23), channel_id=1, source_target_pairs={{0,128},{64,192},{128,0},{192,64},{256,384},{320,448},{384,256},{4... | collective-permute-start | bytes 3080 | tf_op jit(solution)/shard_map/ppermute | solution.py:31
  47.3 0.3 convolution_bitcast_fusion.1
  47.7 1.2 collective-permute-done.5
  48.9 9.4 %collective-permute-start.6 = (f32[256]{0:T(256)S(1)}, f32[256]{0:T(256)S(1)}, u32[]{:S(2)}, u32[]{:S(2)}) collective-permute-start(f32[256]{0:T(256)S(1)} %add.103), channel_id=1, source_target_pairs={{0,256},{64,320},{128,384},{192,448},{256,0},{320,64},{384,128},{4... | collective-permute-start | bytes 3080 | tf_op jit(solution)/shard_map/ppermute | solution.py:31
  58.3 0.3 convolution_bitcast_fusion.2
  58.6 1.2 collective-permute-done.6
  59.8 15.7 %collective-permute-start.7 = (f32[256]{0:T(256)S(1)}, f32[256]{0:T(256)S(1)}, u32[]{:S(2)}, u32[]{:S(2)}) collective-permute-start(f32[256]{0:T(256)S(1)} %add.104), channel_id=1, source_target_pairs={{0,512},{64,576},{128,640},{192,704},{256,768},{320,832},{384,896}... | collective-permute-start | bytes 3080 | tf_op jit(solution)/shard_map/ppermute | solution.py:31
  75.7 1.3 %collective-permute-done.7 = f32[256]{0:T(256)S(1)} collective-permute-done((f32[256]{0:T(256)S(1)}, f32[256]{0:T(256)S(1)}, u32[]{:S(2)}, u32[]{:S(2)}) %collective-permute-start.7) | collective-permute-done | bytes 1056 | tf_op jit(solution)/shard_map/ppermute | solution.py:31
  77.1 1.9 %collective-permute-start.8 = (f32[256]{0:T(256)S(1)}, f32[256]{0:T(256)S(1)}, u32[]{:S(2)}, u32[]{:S(2)}) collective-permute-start(f32[256]{0:T(256)S(1)} %add.105), channel_id=1, source_target_pairs={{0,16},{16,0},{32,48},{48,32},{1,17},{17,1},{33,49},{49,33},{2,18}... | collective-permute-start | bytes 3080 | tf_op jit(solution)/shard_map/ppermute | solution.py:31
  79.0 1.0 collective-permute-done.8
  80.1 20.6 %collective-permute-start.9 = (f32[256]{0:T(256)S(1)}, f32[256]{0:T(256)S(1)}, u32[]{:S(2)}, u32[]{:S(2)}) collective-permute-start(f32[256]{0:T(256)S(1)} %add.106), channel_id=1, source_target_pairs={{0,544},{16,560},{32,512},{48,528},{64,608},{80,624},{96,576},{112... | collective-permute-start | bytes 3080 | tf_op jit(solution)/shard_map/ppermute | solution.py:31
  100.7 1.5 %collective-permute-done.9 = f32[256]{0:T(256)S(1)} collective-permute-done((f32[256]{0:T(256)S(1)}, f32[256]{0:T(256)S(1)}, u32[]{:S(2)}, u32[]{:S(2)}) %collective-permute-start.9) | collective-permute-done | bytes 1056 | tf_op jit(solution)/shard_map/ppermute | solution.py:31
  102.2 2.6 %collective-permute-start.10 = (f32[256]{0:T(256)S(1)}, f32[256]{0:T(256)S(1)}, u32[]{:S(2)}, u32[]{:S(2)}) collective-permute-start(f32[256]{0:T(256)S(1)} %add.107), channel_id=1, source_target_pairs={{0,1},{1,0},{2,3},{3,2},{4,5},{5,4},{6,7},{7,6},{8,9},{9,8},{10,11... | collective-permute-start | bytes 3080 | tf_op jit(solution)/shard_map/ppermute | solution.py:31
  104.9 2.0 %collective-permute-start.2 = (bf16[1,384,768]{1,2,0:T(8,128)(2,1)S(1)}, bf16[1,384,768]{1,2,0:T(8,128)(2,1)S(1)}, u32[]{:S(2)}, u32[]{:S(2)}) collective-permute-start(bf16[1,384,768]{1,2,0:T(8,128)(2,1)S(1)} %pad_maximum_fusion.5), channel_id=1, source_target_pairs={{0,64},{64,128},{128,192},{192,256},{256,320},{320,384},{384,448},... | collective-permute-start | bytes 1769480 | tf_op jit(solution)/shard_map/ppermute | solution.py:198
  106.9 1.3 collective-permute-start.3
  108.2 3.0 %collective-permute-start.11 = (f32[256]{0:T(256)S(1)}, f32[256]{0:T(256)S(1)}, u32[]{:S(2)}, u32[]{:S(2)}) collective-permute-start(f32[256]{0:T(256)S(1)} %add.108), channel_id=1, source_target_pairs={{0,3},{1,2},{2,1},{3,0},{4,7},{5,6},{6,5},{7,4},{8,11},{9,10},{10,... | collective-permute-start | bytes 3080 | tf_op jit(solution)/shard_map/ppermute | solution.py:31
  111.2 1.3 %pad_maximum_fusion.2 = f32[1,1152,3,128]{1,3,2,0:T(8,128)} fusion(f32[1,1152,1,128]{1,3,2,0:T(8,128)S(1)} %convolution_bitcast_fusion, f32[1,1152,1,128]{1,3,2,0:T(8,128)S(1)} %convolution_bitcast_fusion.1, f32[1,1152,1,128]{1,3,2,0:T(8,128)S(1)} %convolution_bitcast_fusion.2), kind=kLoop, calls=%fused_computation.29 | loop fusion | flops 884736 | bytes 3538944 | tf_op jit(solution)/shard_map/stack | solution.py:173
  112.5 2.3 %collective-permute-done.11 = f32[256]{0:T(256)S(1)} collective-permute-done((f32[256]{0:T(256)S(1)}, f32[256]{0:T(256)S(1)}, u32[]{:S(2)}, u32[]{:S(2)}) %collective-permute-start.11) | collective-permute-done | bytes 1056 | tf_op jit(solution)/shard_map/ppermute | solution.py:31
  114.9 3.4 %collective-permute-start.12 = (f32[256]{0:T(256)S(1)}, f32[256]{0:T(256)S(1)}, u32[]{:S(2)}, u32[]{:S(2)}) collective-permute-start(f32[256]{0:T(256)S(1)} %add.109), channel_id=1, source_target_pairs={{0,4},{1,5},{2,6},{3,7},{4,0},{5,1},{6,2},{7,3},{8,12},{9,13},{10,... | collective-permute-start | bytes 3080 | tf_op jit(solution)/shard_map/ppermute | solution.py:31
  118.3 2.0 %collective-permute-done.12 = f32[256]{0:T(256)S(1)} collective-permute-done((f32[256]{0:T(256)S(1)}, f32[256]{0:T(256)S(1)}, u32[]{:S(2)}, u32[]{:S(2)}) %collective-permute-start.12) | collective-permute-done | bytes 1056 | tf_op jit(solution)/shard_map/ppermute | solution.py:31
  120.3 4.6 %collective-permute-start.13 = (f32[256]{0:T(256)S(1)}, f32[256]{0:T(256)S(1)}, u32[]{:S(2)}, u32[]{:S(2)}) collective-permute-start(f32[256]{0:T(256)S(1)} %add.110), channel_id=1, source_target_pairs={{0,12},{1,13},{2,14},{3,15},{4,8},{5,9},{6,10},{7,11},{8,4},{9,5},... | collective-permute-start | bytes 3080 | tf_op jit(solution)/shard_map/ppermute | solution.py:31
  125.0 0.9 copy.54
  125.9 0.9 copy.55
  127.2 1.2 fusion.20
  128.5 0.9 copy.57
  129.4 0.5 slice_multiply_fusion
  129.9 1.2 multiply_reduce_fusion.1
  131.1 1.2 multiply_convert_fusion.1
  132.3 0.9 copy.56
  (63 shorter events, 3.4 us)
Async XLA Ops:
  0.6 8.4 %copy-start.6 = (s32[1,1,3]{2,1,0:T(1,128)S(1)}, s32[1,1,3]{2,1,0:T(1,128)}, u32[]{:S(2)}) copy-start(s32[1,1,3]{2,1,0:T(1,128)} %param.13) | copy-start | bytes 40
  0.6 11.2 %copy-start.2 = (bf16[1,384,384]{2,1,0:T(8,128)(2,1)S(1)}, bf16[1,384,384]{2,1,0:T(8,128)(2,1)}, u32[]{:S(2)}) copy-start(bf16[1,384,384]{2,1,0:T(8,128)(2,1)} %param.7) | copy-start | bytes 884740
  0.7 11.4 %copy-start.3 = (bf16[1,384,384]{2,1,0:T(8,128)(2,1)S(1)}, bf16[1,384,384]{2,1,0:T(8,128)(2,1)}, u32[]{:S(2)}) copy-start(bf16[1,384,384]{2,1,0:T(8,128)(2,1)} %param.12) | copy-start | bytes 884740
  3.1 9.3 %copy-start.5 = (f32[128]{0:T(128)S(1)}, f32[128]{0:T(128)}, u32[]{:S(2)}) copy-start(f32[128]{0:T(128)} %param.10) | copy-start | bytes 1540
  3.2 17.1 %collective-permute-start.1 = (bf16[1,384,768]{1,2,0:T(8,128)(2,1)S(1)}, bf16[1,384,768]{1,2,0:T(8,128)(2,1)S(1)}, u32[]{:S(2)}, u32[]{:S(2)}) collective-permute-start(bf16[1,384,768]{1,2,0:T(8,128)(2,1)S(1)} %pad_maximum_fusion.3), channel_id=1, source_target_pairs={{64,0},{128,64},{192,128},{256,192},{320,256},{384,320},{448,384},... | collective-permute-start | bytes 1769480 | tf_op jit(solution)/shard_map/ppermute | solution.py:21
  4.5 17.0 %collective-permute-start = (bf16[1,384,768]{1,2,0:T(8,128)(2,1)S(1)}, bf16[1,384,768]{1,2,0:T(8,128)(2,1)S(1)}, u32[]{:S(2)}, u32[]{:S(2)}) collective-permute-start(bf16[1,384,768]{1,2,0:T(8,128)(2,1)S(1)} %pad_maximum_fusion.3), channel_id=1, source_target_pairs={{0,64},{64,128},{128,192},{192,256},{256,320},{320,384},{384,448},... | collective-permute-start | bytes 1769480 | tf_op jit(solution)/shard_map/ppermute | solution.py:19
  21.8 0.7 copy-start.4
  32.9 1.2 copy-start
  34.1 1.1 slice-start
  35.6 5.9 %collective-permute-start.4 = (f32[256]{0:T(256)S(1)}, f32[256]{0:T(256)S(1)}, u32[]{:S(2)}, u32[]{:S(2)}) collective-permute-start(f32[256]{0:T(256)S(1)} %pad_maximum_fusion.8), channel_id=1, source_target_pairs={{0,64},{64,0},{128,192},{192,128},{256,320},{320,256},{384,448},{4... | collective-permute-start | bytes 3080 | tf_op jit(solution)/shard_map/ppermute | solution.py:31
  41.5 7.4 %collective-permute-start.5 = (f32[256]{0:T(256)S(1)}, f32[256]{0:T(256)S(1)}, u32[]{:S(2)}, u32[]{:S(2)}) collective-permute-start(f32[256]{0:T(256)S(1)} %fusion.23), channel_id=1, source_target_pairs={{0,128},{64,192},{128,0},{192,64},{256,384},{320,448},{384,256},{4... | collective-permute-start | bytes 3080 | tf_op jit(solution)/shard_map/ppermute | solution.py:31
  48.9 10.9 %collective-permute-start.6 = (f32[256]{0:T(256)S(1)}, f32[256]{0:T(256)S(1)}, u32[]{:S(2)}, u32[]{:S(2)}) collective-permute-start(f32[256]{0:T(256)S(1)} %add.103), channel_id=1, source_target_pairs={{0,256},{64,320},{128,384},{192,448},{256,0},{320,64},{384,128},{4... | collective-permute-start | bytes 3080 | tf_op jit(solution)/shard_map/ppermute | solution.py:31
  59.8 17.3 %collective-permute-start.7 = (f32[256]{0:T(256)S(1)}, f32[256]{0:T(256)S(1)}, u32[]{:S(2)}, u32[]{:S(2)}) collective-permute-start(f32[256]{0:T(256)S(1)} %add.104), channel_id=1, source_target_pairs={{0,512},{64,576},{128,640},{192,704},{256,768},{320,832},{384,896}... | collective-permute-start | bytes 3080 | tf_op jit(solution)/shard_map/ppermute | solution.py:31
  77.1 3.0 %collective-permute-start.8 = (f32[256]{0:T(256)S(1)}, f32[256]{0:T(256)S(1)}, u32[]{:S(2)}, u32[]{:S(2)}) collective-permute-start(f32[256]{0:T(256)S(1)} %add.105), channel_id=1, source_target_pairs={{0,16},{16,0},{32,48},{48,32},{1,17},{17,1},{33,49},{49,33},{2,18}... | collective-permute-start | bytes 3080 | tf_op jit(solution)/shard_map/ppermute | solution.py:31
  80.1 22.1 %collective-permute-start.9 = (f32[256]{0:T(256)S(1)}, f32[256]{0:T(256)S(1)}, u32[]{:S(2)}, u32[]{:S(2)}) collective-permute-start(f32[256]{0:T(256)S(1)} %add.106), channel_id=1, source_target_pairs={{0,544},{16,560},{32,512},{48,528},{64,608},{80,624},{96,576},{112... | collective-permute-start | bytes 3080 | tf_op jit(solution)/shard_map/ppermute | solution.py:31
  102.2 6.0 %collective-permute-start.10 = (f32[256]{0:T(256)S(1)}, f32[256]{0:T(256)S(1)}, u32[]{:S(2)}, u32[]{:S(2)}) collective-permute-start(f32[256]{0:T(256)S(1)} %add.107), channel_id=1, source_target_pairs={{0,1},{1,0},{2,3},{3,2},{4,5},{5,4},{6,7},{7,6},{8,9},{9,8},{10,11... | collective-permute-start | bytes 3080 | tf_op jit(solution)/shard_map/ppermute | solution.py:31
  104.9 22.1 %collective-permute-start.2 = (bf16[1,384,768]{1,2,0:T(8,128)(2,1)S(1)}, bf16[1,384,768]{1,2,0:T(8,128)(2,1)S(1)}, u32[]{:S(2)}, u32[]{:S(2)}) collective-permute-start(bf16[1,384,768]{1,2,0:T(8,128)(2,1)S(1)} %pad_maximum_fusion.5), channel_id=1, source_target_pairs={{0,64},{64,128},{128,192},{192,256},{256,320},{320,384},{384,448},... | collective-permute-start | bytes 1769480 | tf_op jit(solution)/shard_map/ppermute | solution.py:198
  106.9 20.1 %collective-permute-start.3 = (bf16[1,384,768]{1,2,0:T(8,128)(2,1)S(1)}, bf16[1,384,768]{1,2,0:T(8,128)(2,1)S(1)}, u32[]{:S(2)}, u32[]{:S(2)}) collective-permute-start(bf16[1,384,768]{1,2,0:T(8,128)(2,1)S(1)} %pad_maximum_fusion.6), channel_id=1, source_target_pairs={{64,0},{128,64},{192,128},{256,192},{320,256},{384,320},{448,384},... | collective-permute-start | bytes 1769480 | tf_op jit(solution)/shard_map/ppermute | solution.py:201
  108.2 6.7 %collective-permute-start.11 = (f32[256]{0:T(256)S(1)}, f32[256]{0:T(256)S(1)}, u32[]{:S(2)}, u32[]{:S(2)}) collective-permute-start(f32[256]{0:T(256)S(1)} %add.108), channel_id=1, source_target_pairs={{0,3},{1,2},{2,1},{3,0},{4,7},{5,6},{6,5},{7,4},{8,11},{9,10},{10,... | collective-permute-start | bytes 3080 | tf_op jit(solution)/shard_map/ppermute | solution.py:31
  114.9 5.5 %collective-permute-start.12 = (f32[256]{0:T(256)S(1)}, f32[256]{0:T(256)S(1)}, u32[]{:S(2)}, u32[]{:S(2)}) collective-permute-start(f32[256]{0:T(256)S(1)} %add.109), channel_id=1, source_target_pairs={{0,4},{1,5},{2,6},{3,7},{4,0},{5,1},{6,2},{7,3},{8,12},{9,13},{10,... | collective-permute-start | bytes 3080 | tf_op jit(solution)/shard_map/ppermute | solution.py:31
  120.3 6.7 %collective-permute-start.13 = (f32[256]{0:T(256)S(1)}, f32[256]{0:T(256)S(1)}, u32[]{:S(2)}, u32[]{:S(2)}) collective-permute-start(f32[256]{0:T(256)S(1)} %add.110), channel_id=1, source_target_pairs={{0,12},{1,13},{2,14},{3,15},{4,8},{5,9},{6,10},{7,11},{8,4},{9,5},... | collective-permute-start | bytes 3080 | tf_op jit(solution)/shard_map/ppermute | solution.py:31
  127.1 2.8 %copy-start.1 = (f32[1,1152,3,128]{1,3,2,0:T(8,128)S(1)}, f32[1,1152,3,128]{1,3,2,0:T(8,128)}, u32[]{:S(2)}) copy-start(f32[1,1152,3,128]{1,3,2,0:T(8,128)} %copy-done) | copy-start | bytes 5308420

commit v8 on v7

--- a/solution.py
+++ b/solution.py
@@ -193,14 +193,36 @@
             jnp.sum(near_terms * k_unit_all, axis=(0, 1, 2)),
         ]
     )
-    gain_totals = butterfly_sum(gain_terms, gain_stages())
-    ends = tile_count - 1
-    from_left = lax.ppermute(
-        pack_terms(right_terms[0], right_terms[1]), "seq", [(i, i + 1) for i in range(ends)]
-    )
-    from_right = lax.ppermute(
-        pack_terms(left_terms[0], left_terms[1]), "seq", [(i + 1, i) for i in range(ends)]
-    )
+    even = tile_index % 2 == 0
+    left_pack = pack_terms(left_terms[0], left_terms[1])
+    right_pack = pack_terms(right_terms[0], right_terms[1])
+    gain_hi = lax.optimization_barrier(gain_terms.astype(jnp.bfloat16))
+    gain_rest = gain_terms - gain_hi.astype(jnp.float32)
+    gain_mid = lax.optimization_barrier(gain_rest.astype(jnp.bfloat16))
+    gain_lo = lax.optimization_barrier(
+        (gain_rest - gain_mid.astype(jnp.float32)).astype(jnp.bfloat16)
+    )
+    gain_row = jnp.concatenate([gain_hi, gain_mid, gain_lo])
+    own_gain = gain_row.astype(jnp.float32).reshape(3, -1)
+    width = left_pack.shape[2]
+    gain_row = jnp.pad(gain_row, (0, width - gain_row.shape[0])).reshape(1, 1, width)
+    gain_row = jnp.broadcast_to(gain_row, (sample_count, 1, width))
+    pair_payload = jnp.concatenate([jnp.where(even, right_pack, left_pack), gain_row], axis=1)
+    other_payload = jnp.where(even, left_pack, right_pack)
+    got_pair = lax.ppermute(pair_payload, "seq", [(i, i ^ 1) for i in range(tile_count)])
+    other_pairs = [(i, i + 1 if i % 2 else i - 1) for i in range(tile_count)]
+    got_other = lax.ppermute(
+        other_payload, "seq", [(i, j) for i, j in other_pairs if 0 <= j < tile_count]
+    )
+    got_gain = got_pair[0, tile_rows, : 3 * gain_terms.shape[0]].astype(jnp.float32)
+    got_gain = got_gain.reshape(3, -1)
+    gain_terms = ((own_gain[0] + own_gain[1]) + own_gain[2]) + (
+        (got_gain[0] + got_gain[1]) + got_gain[2]
+    )
+    gain_totals = butterfly_sum(gain_terms, gain_stages()[1:])
+    got_pair = got_pair[:, :tile_rows]
+    from_left = jnp.where(even, got_other, got_pair)
+    from_right = jnp.where(even, got_pair, got_other)
     from_left, from_right, gain_totals = lax.optimization_barrier(
         (from_left, from_right, gain_totals)
     )

time: 136 us -> 148 us (1.088); the launches traced: 133 us -> 147 us
  waiting for transfers between devices: 20.9 us -> 35.4 us
  starting transfers between devices: 80.6 us -> 76.6 us
  other arithmetic: 12.4 us -> 14.8 us
    ppermute x2, waiting for transfers between devices: 0.01 us -> 12.6 us  [the longest x1 12.6 us: per_device(): lax.ppermute(pair_payload, 'seq', [(i, i ^ 1) for i in range(tile_count)])]
    ppermute x10 -> x9, starting transfers between devices: 71.4 us -> 65.7 us  [butterfly_sum(): lax.ppermute(value, axes, [(i, i ^ mask) for i in range(count)])]
    ppermute x10 -> x9, waiting for transfers between devices: 12 us -> 13.9 us  [butterfly_sum(): lax.ppermute(value, axes, [(i, i ^ mask) for i in range(count)])]
    ppermute x2, starting transfers between devices: 3.26 us -> 5.09 us  [the longest x1 4.39 us: per_device(): lax.ppermute(pair_payload, 'seq', [(i, i ^ 1) for i in range(tile_count)])]
    unnamed x22 -> x43, local copies, waits for them, and re-layouts: 7.82 us -> 7.7 us
  transfers between devices with their start and end apart: 14 -> 13, of which waited for: 11 -> 11; matrix products, arithmetic and copies ran while one was open for 5% -> 4% of each run, Pallas kernels for 0% -> 0%
where the time goes in v8:
time: 148 us; the launch traced here: 147 us
  starting transfers between devices  76.6 us (52%)
  waiting for transfers between devices  35.4 us (24%)
  other arithmetic  14.8 us (10%)
  local copies, waits for them, and re-layouts  9.21 us (6%)
  matrix products  8.08 us (5%)
  between operations  3.25 us (2%)
    ppermute x9, starting transfers between devices, butterfly_sum(): lax.ppermute(value, axes, [(i, i ^ mask) for i in range(count)])  65.7 us
    ppermute x9, waiting for transfers between devices, butterfly_sum(): lax.ppermute(value, axes, [(i, i ^ mask) for i in range(count)])  13.9 us
    ppermute x1, waiting for transfers between devices, per_device(): lax.ppermute(pair_payload, 'seq', [(i, i ^ 1) for i in range(tile_count)])  12.6 us
    ppermute x1, waiting for transfers between devices, extended_2(): lax.ppermute(head, axis, [((i + 1) % count, i) for i in range(ends)])  7.73 us
    unnamed x43, local copies, waits for them, and re-layouts  7.7 us
    ppermute x1, starting transfers between devices, extended_2(): lax.ppermute(tail, axis, [(i, (i + 1) % count) for i in range(ends)])  4.58 us
    ppermute x1, starting transfers between devices, per_device(): lax.ppermute(pair_payload, 'seq', [(i, i ^ 1) for i in range(tile_count)])  4.39 us
  transfers between devices with their start and end apart: 13, of which 11 were waited for; matrix products, arithmetic and copies ran while one was open for 4% of the time, Pallas kernels for 0%

profile of v8, /device:TPU:24, one launch (start us, length us, event | category | flops | bytes accessed | tf_op | source)
XLA Modules:
  0.0 147.4 jit_solution(8364692091575035907)
XLA Ops:
  0.7 1.2 copy.63
  1.9 1.2 copy.64
  3.2 1.3 collective-permute-start.1
  4.5 4.6 %collective-permute-start = (bf16[1,384,768]{1,2,0:T(8,128)(2,1)S(1)}, bf16[1,384,768]{1,2,0:T(8,128)(2,1)S(1)}, u32[]{:S(2)}, u32[]{:S(2)}) collective-permute-start(bf16[1,384,768]{1,2,0:T(8,128)(2,1)S(1)} %pad_maximum_fusion.4), channel_id=1, source_target_pairs={{0,64},{64,128},{128,192},{192,256},{256,320},{320,384},{384,448},... | collective-permute-start | bytes 1769480 | tf_op jit(solution)/shard_map/ppermute | solution.py:19
  9.1 0.7 compare_reduce_fusion.2
  12.6 7.7 %collective-permute-done.1 = bf16[1,384,768]{1,2,0:T(8,128)(2,1)S(1)} collective-permute-done((bf16[1,384,768]{1,2,0:T(8,128)(2,1)S(1)}, bf16[1,384,768]{1,2,0:T(8,128)(2,1)S(1)}, u32[]{:S(2)}, u32[]{:S(2)}) %collective-permute-start.1) | collective-permute-done | bytes 589856 | tf_op jit(solution)/shard_map/ppermute | solution.py:21
  20.3 1.2 collective-permute-done
  22.0 0.6 fusion.26
  22.6 1.5 multiply_convert_fusion
  24.1 0.5 fusion.32
  24.6 0.5 fusion.33
  25.1 0.4 exponential_reduce_fusion
  25.6 0.3 exponential_convert_fusion
  25.9 0.4 convolution_convert_fusion
  26.3 0.3 convolution_bitcast_fusion
  26.7 0.4 exponential_reduce_fusion.1
  27.1 0.3 exponential_convert_fusion.1
  27.5 0.4 convolution_convert_fusion.1
  28.2 0.5 fusion.34
  28.7 0.4 exponential_reduce_fusion.2
  29.9 1.1 multiply_reduce_fusion.6
  30.9 0.5 fusion.11
  31.4 0.4 fusion.18
  31.8 0.3 fusion.12
  32.2 0.5 fusion.10
  32.6 0.4 fusion.17
  33.1 0.3 fusion.13
  33.4 0.5 fusion.9
  33.9 0.4 fusion.16
  34.3 0.3 fusion.14
  35.1 0.9 copy-done
  36.1 0.9 fusion.22
  37.0 0.3 fusion.15
  37.9 1.0 broadcast_select_fusion.2
  39.3 4.4 %collective-permute-start.3 = (bf16[1,385,768]{2,1,0:T(8,128)(2,1)S(1)}, bf16[1,385,768]{2,1,0:T(8,128)(2,1)S(1)}, u32[]{:S(2)}, u32[]{:S(2)}) collective-permute-start(bf16[1,385,768]{2,1,0:T(8,128)(2,1)S(1)} %copy.73), channel_id=1, source_target_pairs={{0,64},{64,0},{128,192},{192,128},{256,320},{320,256},{384,448},{4... | collective-permute-start | bytes 1774088 | tf_op jit(solution)/shard_map/ppermute | solution.py:212
  43.7 12.6 %collective-permute-done.3 = bf16[1,385,768]{2,1,0:T(8,128)(2,1)S(1)} collective-permute-done((bf16[1,385,768]{2,1,0:T(8,128)(2,1)S(1)}, bf16[1,385,768]{2,1,0:T(8,128)(2,1)S(1)}, u32[]{:S(2)}, u32[]{:S(2)}) %collective-permute-start.3) | collective-permute-done | bytes 591392 | tf_op jit(solution)/shard_map/ppermute | solution.py:212
  56.3 5.8 %collective-permute-start.4 = (f32[256]{0:T(256)S(1)}, f32[256]{0:T(256)S(1)}, u32[]{:S(2)}, u32[]{:S(2)}) collective-permute-start(f32[256]{0:T(256)S(1)} %add_add_fusion), channel_id=1, source_target_pairs={{0,128},{64,192},{128,0},{192,64},{256,384},{320,448},{384,256},{4... | collective-permute-start | bytes 3080 | tf_op jit(solution)/shard_map/ppermute | solution.py:31
  62.1 1.5 %collective-permute-done.4 = f32[256]{0:T(256)S(1)} collective-permute-done((f32[256]{0:T(256)S(1)}, f32[256]{0:T(256)S(1)}, u32[]{:S(2)}, u32[]{:S(2)}) %collective-permute-start.4) | collective-permute-done | bytes 1056 | tf_op jit(solution)/shard_map/ppermute | solution.py:31
  63.7 9.1 %collective-permute-start.5 = (f32[256]{0:T(256)S(1)}, f32[256]{0:T(256)S(1)}, u32[]{:S(2)}, u32[]{:S(2)}) collective-permute-start(f32[256]{0:T(256)S(1)} %add.129), channel_id=1, source_target_pairs={{0,256},{64,320},{128,384},{192,448},{256,0},{320,64},{384,128},{4... | collective-permute-start | bytes 3080 | tf_op jit(solution)/shard_map/ppermute | solution.py:31
  72.8 1.5 %collective-permute-done.5 = f32[256]{0:T(256)S(1)} collective-permute-done((f32[256]{0:T(256)S(1)}, f32[256]{0:T(256)S(1)}, u32[]{:S(2)}, u32[]{:S(2)}) %collective-permute-start.5) | collective-permute-done | bytes 1056 | tf_op jit(solution)/shard_map/ppermute | solution.py:31
  74.3 15.7 %collective-permute-start.6 = (f32[256]{0:T(256)S(1)}, f32[256]{0:T(256)S(1)}, u32[]{:S(2)}, u32[]{:S(2)}) collective-permute-start(f32[256]{0:T(256)S(1)} %add.130), channel_id=1, source_target_pairs={{0,512},{64,576},{128,640},{192,704},{256,768},{320,832},{384,896}... | collective-permute-start | bytes 3080 | tf_op jit(solution)/shard_map/ppermute | solution.py:31
  90.0 1.5 %collective-permute-done.6 = f32[256]{0:T(256)S(1)} collective-permute-done((f32[256]{0:T(256)S(1)}, f32[256]{0:T(256)S(1)}, u32[]{:S(2)}, u32[]{:S(2)}) %collective-permute-start.6) | collective-permute-done | bytes 1056 | tf_op jit(solution)/shard_map/ppermute | solution.py:31
  91.6 1.9 %collective-permute-start.7 = (f32[256]{0:T(256)S(1)}, f32[256]{0:T(256)S(1)}, u32[]{:S(2)}, u32[]{:S(2)}) collective-permute-start(f32[256]{0:T(256)S(1)} %add.131), channel_id=1, source_target_pairs={{0,16},{16,0},{32,48},{48,32},{1,17},{17,1},{33,49},{49,33},{2,18}... | collective-permute-start | bytes 3080 | tf_op jit(solution)/shard_map/ppermute | solution.py:31
  93.5 1.1 collective-permute-done.7
  94.6 20.4 %collective-permute-start.8 = (f32[256]{0:T(256)S(1)}, f32[256]{0:T(256)S(1)}, u32[]{:S(2)}, u32[]{:S(2)}) collective-permute-start(f32[256]{0:T(256)S(1)} %add.132), channel_id=1, source_target_pairs={{0,544},{16,560},{32,512},{48,528},{64,608},{80,624},{96,576},{112... | collective-permute-start | bytes 3080 | tf_op jit(solution)/shard_map/ppermute | solution.py:31
  115.0 0.7 collective-permute-start.2
  115.7 0.8 collective-permute-done.8
  116.6 2.8 %collective-permute-start.9 = (f32[256]{0:T(256)S(1)}, f32[256]{0:T(256)S(1)}, u32[]{:S(2)}, u32[]{:S(2)}) collective-permute-start(f32[256]{0:T(256)S(1)} %add.133), channel_id=1, source_target_pairs={{0,1},{1,0},{2,3},{3,2},{4,5},{5,4},{6,7},{7,6},{8,9},{9,8},{10,11... | collective-permute-start | bytes 3080 | tf_op jit(solution)/shard_map/ppermute | solution.py:31
  119.3 1.3 pad_maximum_fusion.2
  120.7 1.5 collective-permute-done.9
  122.2 2.1 %collective-permute-start.10 = (f32[256]{0:T(256)S(1)}, f32[256]{0:T(256)S(1)}, u32[]{:S(2)}, u32[]{:S(2)}) collective-permute-start(f32[256]{0:T(256)S(1)} %add.134), channel_id=1, source_target_pairs={{0,3},{1,2},{2,1},{3,0},{4,7},{5,6},{6,5},{7,4},{8,11},{9,10},{10,... | collective-permute-start | bytes 3080 | tf_op jit(solution)/shard_map/ppermute | solution.py:31
  124.3 0.7 slice_bitcast_fusion.36
  125.0 3.8 %collective-permute-done.10 = f32[256]{0:T(256)S(1)} collective-permute-done((f32[256]{0:T(256)S(1)}, f32[256]{0:T(256)S(1)}, u32[]{:S(2)}, u32[]{:S(2)}) %collective-permute-start.10) | collective-permute-done | bytes 1056 | tf_op jit(solution)/shard_map/ppermute | solution.py:31
  128.8 3.4 %collective-permute-start.11 = (f32[256]{0:T(256)S(1)}, f32[256]{0:T(256)S(1)}, u32[]{:S(2)}, u32[]{:S(2)}) collective-permute-start(f32[256]{0:T(256)S(1)} %add.135), channel_id=1, source_target_pairs={{0,4},{1,5},{2,6},{3,7},{4,0},{5,1},{6,2},{7,3},{8,12},{9,13},{10,... | collective-permute-start | bytes 3080 | tf_op jit(solution)/shard_map/ppermute | solution.py:31
  132.3 0.9 copy.75
  133.2 0.9 copy.76
  134.5 4.5 %collective-permute-start.12 = (f32[256]{0:T(256)S(1)}, f32[256]{0:T(256)S(1)}, u32[]{:S(2)}, u32[]{:S(2)}) collective-permute-start(f32[256]{0:T(256)S(1)} %add.136), channel_id=1, source_target_pairs={{0,12},{1,13},{2,14},{3,15},{4,8},{5,9},{6,10},{7,11},{8,4},{9,5},... | collective-permute-start | bytes 3080 | tf_op jit(solution)/shard_map/ppermute | solution.py:31
  139.1 2.1 %collective-permute-done.12 = f32[256]{0:T(256)S(1)} collective-permute-done((f32[256]{0:T(256)S(1)}, f32[256]{0:T(256)S(1)}, u32[]{:S(2)}, u32[]{:S(2)}) %collective-permute-start.12) | collective-permute-done | bytes 1056 | tf_op jit(solution)/shard_map/ppermute | solution.py:31
  141.3 1.2 fusion.20
  142.6 0.9 copy.78
  143.5 0.5 slice_multiply_fusion
  144.0 1.2 multiply_reduce_fusion.1
  145.2 1.2 multiply_convert_fusion.1
  146.5 0.9 copy.77
  (91 shorter events, 4.6 us)
Async XLA Ops:
  0.6 8.4 %copy-start.16 = (s32[1,1,3]{2,1,0:T(1,128)S(1)}, s32[1,1,3]{2,1,0:T(1,128)}, u32[]{:S(2)}) copy-start(s32[1,1,3]{2,1,0:T(1,128)} %param.13) | copy-start | bytes 40
  0.6 11.2 %copy-start.7 = (bf16[1,384,384]{2,1,0:T(8,128)(2,1)S(1)}, bf16[1,384,384]{2,1,0:T(8,128)(2,1)}, u32[]{:S(2)}) copy-start(bf16[1,384,384]{2,1,0:T(8,128)(2,1)} %param.7) | copy-start | bytes 884740
  0.7 11.4 %copy-start.8 = (bf16[1,384,384]{2,1,0:T(8,128)(2,1)S(1)}, bf16[1,384,384]{2,1,0:T(8,128)(2,1)}, u32[]{:S(2)}) copy-start(bf16[1,384,384]{2,1,0:T(8,128)(2,1)} %param.12) | copy-start | bytes 884740
  3.1 9.4 %copy-start.15 = (f32[128]{0:T(128)S(1)}, f32[128]{0:T(128)}, u32[]{:S(2)}) copy-start(f32[128]{0:T(128)} %param.10) | copy-start | bytes 1540
  3.2 17.1 %collective-permute-start.1 = (bf16[1,384,768]{1,2,0:T(8,128)(2,1)S(1)}, bf16[1,384,768]{1,2,0:T(8,128)(2,1)S(1)}, u32[]{:S(2)}, u32[]{:S(2)}) collective-permute-start(bf16[1,384,768]{1,2,0:T(8,128)(2,1)S(1)} %pad_maximum_fusion.4), channel_id=1, source_target_pairs={{64,0},{128,64},{192,128},{256,192},{320,256},{384,320},{448,384},... | collective-permute-start | bytes 1769480 | tf_op jit(solution)/shard_map/ppermute | solution.py:21
  4.5 17.0 %collective-permute-start = (bf16[1,384,768]{1,2,0:T(8,128)(2,1)S(1)}, bf16[1,384,768]{1,2,0:T(8,128)(2,1)S(1)}, u32[]{:S(2)}, u32[]{:S(2)}) collective-permute-start(bf16[1,384,768]{1,2,0:T(8,128)(2,1)S(1)} %pad_maximum_fusion.4), channel_id=1, source_target_pairs={{0,64},{64,128},{128,192},{192,256},{256,320},{320,384},{384,448},... | collective-permute-start | bytes 1769480 | tf_op jit(solution)/shard_map/ppermute | solution.py:19
  12.1 9.5 %copy-start.2 = (bf16[1,384,384]{1,2,0:T(8,128)(2,1)}, bf16[1,384,384]{1,2,0:T(8,128)(2,1)S(1)}, u32[]{:S(2)}) copy-start(bf16[1,384,384]{1,2,0:T(8,128)(2,1)S(1)} %copy.62) | copy-start | bytes 884740
  21.8 0.8 copy-start.14
  26.3 3.6 %copy-start.9 = (bf16[384,128]{0,1:T(8,128)(2,1)}, bf16[384,128]{0,1:T(8,128)(2,1)S(1)}, u32[]{:S(2)}) copy-start(bf16[384,128]{0,1:T(8,128)(2,1)S(1)} %convolution_convert_fusion) | copy-start | bytes 294916
  27.9 2.0 %copy-start.11 = (bf16[384,128]{0,1:T(8,128)(2,1)}, bf16[384,128]{0,1:T(8,128)(2,1)S(1)}, u32[]{:S(2)}) copy-start(bf16[384,128]{0,1:T(8,128)(2,1)S(1)} %convolution_convert_fusion.1) | copy-start | bytes 294916
  34.8 1.2 copy-start
  34.8 1.2 copy-start.3
  36.0 1.1 slice-start
  39.3 17.0 %collective-permute-start.3 = (bf16[1,385,768]{2,1,0:T(8,128)(2,1)S(1)}, bf16[1,385,768]{2,1,0:T(8,128)(2,1)S(1)}, u32[]{:S(2)}, u32[]{:S(2)}) collective-permute-start(bf16[1,385,768]{2,1,0:T(8,128)(2,1)S(1)} %copy.73), channel_id=1, source_target_pairs={{0,64},{64,0},{128,192},{192,128},{256,320},{320,256},{384,448},{4... | collective-permute-start | bytes 1774088 | tf_op jit(solution)/shard_map/ppermute | solution.py:212
  56.3 60.2 %copy-start.5 = (bf16[1,385,768]{2,1,0:T(8,128)(2,1)}, bf16[1,385,768]{2,1,0:T(8,128)(2,1)S(1)}, u32[]{:S(2)}) copy-start(bf16[1,385,768]{2,1,0:T(8,128)(2,1)S(1)} %collective-permute-done.3) | copy-start | bytes 1774084
  56.3 7.4 %collective-permute-start.4 = (f32[256]{0:T(256)S(1)}, f32[256]{0:T(256)S(1)}, u32[]{:S(2)}, u32[]{:S(2)}) collective-permute-start(f32[256]{0:T(256)S(1)} %add_add_fusion), channel_id=1, source_target_pairs={{0,128},{64,192},{128,0},{192,64},{256,384},{320,448},{384,256},{4... | collective-permute-start | bytes 3080 | tf_op jit(solution)/shard_map/ppermute | solution.py:31
  63.7 10.6 %collective-permute-start.5 = (f32[256]{0:T(256)S(1)}, f32[256]{0:T(256)S(1)}, u32[]{:S(2)}, u32[]{:S(2)}) collective-permute-start(f32[256]{0:T(256)S(1)} %add.129), channel_id=1, source_target_pairs={{0,256},{64,320},{128,384},{192,448},{256,0},{320,64},{384,128},{4... | collective-permute-start | bytes 3080 | tf_op jit(solution)/shard_map/ppermute | solution.py:31
  74.3 17.3 %collective-permute-start.6 = (f32[256]{0:T(256)S(1)}, f32[256]{0:T(256)S(1)}, u32[]{:S(2)}, u32[]{:S(2)}) collective-permute-start(f32[256]{0:T(256)S(1)} %add.130), channel_id=1, source_target_pairs={{0,512},{64,576},{128,640},{192,704},{256,768},{320,832},{384,896}... | collective-permute-start | bytes 3080 | tf_op jit(solution)/shard_map/ppermute | solution.py:31
  91.6 3.0 %collective-permute-start.7 = (f32[256]{0:T(256)S(1)}, f32[256]{0:T(256)S(1)}, u32[]{:S(2)}, u32[]{:S(2)}) collective-permute-start(f32[256]{0:T(256)S(1)} %add.131), channel_id=1, source_target_pairs={{0,16},{16,0},{32,48},{48,32},{1,17},{17,1},{33,49},{49,33},{2,18}... | collective-permute-start | bytes 3080 | tf_op jit(solution)/shard_map/ppermute | solution.py:31
  94.6 21.9 %collective-permute-start.8 = (f32[256]{0:T(256)S(1)}, f32[256]{0:T(256)S(1)}, u32[]{:S(2)}, u32[]{:S(2)}) collective-permute-start(f32[256]{0:T(256)S(1)} %add.132), channel_id=1, source_target_pairs={{0,544},{16,560},{32,512},{48,528},{64,608},{80,624},{96,576},{112... | collective-permute-start | bytes 3080 | tf_op jit(solution)/shard_map/ppermute | solution.py:31
  115.0 24.0 %collective-permute-start.2 = (bf16[1,384,768]{1,2,0:T(8,128)(2,1)}, bf16[1,384,768]{1,2,0:T(8,128)(2,1)S(1)}, u32[]{:S(2)}, u32[]{:S(2)}) collective-permute-start(bf16[1,384,768]{1,2,0:T(8,128)(2,1)} %get-tuple-element.55), channel_id=1, source_target_pairs={{64,128},{128,64},{192,256},{256,192},{320,384},{384,320},{448,512... | collective-permute-start | bytes 1769480 | tf_op jit(solution)/shard_map/ppermute | solution.py:214
  116.5 15.7 %copy-start.10 = (bf16[384,128]{0,1:T(8,128)(2,1)S(1)}, bf16[384,128]{0,1:T(8,128)(2,1)}, u32[]{:S(2)}) copy-start(bf16[384,128]{0,1:T(8,128)(2,1)} %copy-done.9) | copy-start | bytes 294916
  116.5 15.7 %copy-start.12 = (bf16[384,128]{0,1:T(8,128)(2,1)S(1)}, bf16[384,128]{0,1:T(8,128)(2,1)}, u32[]{:S(2)}) copy-start(bf16[384,128]{0,1:T(8,128)(2,1)} %copy-done.11) | copy-start | bytes 294916
  116.5 15.7 %copy-start.13 = (bf16[384,128]{0,1:T(8,128)(2,1)S(1)}, bf16[384,128]{0,1:T(8,128)(2,1)}, u32[]{:S(2)}) copy-start(bf16[384,128]{0,1:T(8,128)(2,1)} %get-tuple-element.74) | copy-start | bytes 294916
  116.5 16.6 %copy-start.4 = (bf16[1,384,384]{1,2,0:T(8,128)(2,1)S(1)}, bf16[1,384,384]{1,2,0:T(8,128)(2,1)}, u32[]{:S(2)}) copy-start(bf16[1,384,384]{1,2,0:T(8,128)(2,1)} %get-tuple-element.57) | copy-start | bytes 884740
  116.6 5.6 %collective-permute-start.9 = (f32[256]{0:T(256)S(1)}, f32[256]{0:T(256)S(1)}, u32[]{:S(2)}, u32[]{:S(2)}) collective-permute-start(f32[256]{0:T(256)S(1)} %add.133), channel_id=1, source_target_pairs={{0,1},{1,0},{2,3},{3,2},{4,5},{5,4},{6,7},{7,6},{8,9},{9,8},{10,11... | collective-permute-start | bytes 3080 | tf_op jit(solution)/shard_map/ppermute | solution.py:31
  120.7 13.4 %copy-start.6 = (bf16[1,385,768]{2,1,0:T(8,128)(2,1)S(1)}, bf16[1,385,768]{2,1,0:T(8,128)(2,1)}, u32[]{:S(2)}) copy-start(bf16[1,385,768]{2,1,0:T(8,128)(2,1)} %copy-done.5) | copy-start | bytes 1774084
  122.2 6.7 %collective-permute-start.10 = (f32[256]{0:T(256)S(1)}, f32[256]{0:T(256)S(1)}, u32[]{:S(2)}, u32[]{:S(2)}) collective-permute-start(f32[256]{0:T(256)S(1)} %add.134), channel_id=1, source_target_pairs={{0,3},{1,2},{2,1},{3,0},{4,7},{5,6},{6,5},{7,4},{8,11},{9,10},{10,... | collective-permute-start | bytes 3080 | tf_op jit(solution)/shard_map/ppermute | solution.py:31
  128.8 5.6 %collective-permute-start.11 = (f32[256]{0:T(256)S(1)}, f32[256]{0:T(256)S(1)}, u32[]{:S(2)}, u32[]{:S(2)}) collective-permute-start(f32[256]{0:T(256)S(1)} %add.135), channel_id=1, source_target_pairs={{0,4},{1,5},{2,6},{3,7},{4,0},{5,1},{6,2},{7,3},{8,12},{9,13},{10,... | collective-permute-start | bytes 3080 | tf_op jit(solution)/shard_map/ppermute | solution.py:31
  134.5 6.7 %collective-permute-start.12 = (f32[256]{0:T(256)S(1)}, f32[256]{0:T(256)S(1)}, u32[]{:S(2)}, u32[]{:S(2)}) collective-permute-start(f32[256]{0:T(256)S(1)} %add.136), channel_id=1, source_target_pairs={{0,12},{1,13},{2,14},{3,15},{4,8},{5,9},{6,10},{7,11},{8,4},{9,5},... | collective-permute-start | bytes 3080 | tf_op jit(solution)/shard_map/ppermute | solution.py:31
  141.2 2.8 %copy-start.1 = (f32[1,1152,3,128]{1,3,2,0:T(8,128)S(1)}, f32[1,1152,3,128]{1,3,2,0:T(8,128)}, u32[]{:S(2)}) copy-start(f32[1,1152,3,128]{1,3,2,0:T(8,128)} %copy-done) | copy-start | bytes 5308420

commit v9 on v7

--- a/solution.py
+++ b/solution.py
@@ -193,7 +193,9 @@
             jnp.sum(near_terms * k_unit_all, axis=(0, 1, 2)),
         ]
     )
-    gain_totals = butterfly_sum(gain_terms, gain_stages())
+    stages = gain_stages()
+    off_plane = len(stages) - 4
+    gain_totals = butterfly_sum(gain_terms, stages[:off_plane])
     ends = tile_count - 1
     from_left = lax.ppermute(
         pack_terms(right_terms[0], right_terms[1]), "seq", [(i, i + 1) for i in range(ends)]
@@ -204,6 +206,7 @@
     from_left, from_right, gain_totals = lax.optimization_barrier(
         (from_left, from_right, gain_totals)
     )
+    gain_totals = butterfly_sum(gain_totals, stages[off_plane:])
     incoming = from_left.astype(jnp.float32) + from_right.astype(jnp.float32)
     grad_knorm = own_terms[0] + incoming[..., :columns].reshape(
         sample_count, tile_rows, head_count, head_size

time: 136 us -> 136 us (level); the launches traced: 133 us -> 135 us
  waiting for transfers between devices: 20.9 us -> 27.8 us
  starting transfers between devices: 80.6 us -> 74.1 us
    ppermute x10, starting transfers between devices: 71.4 us -> 62.5 us  [butterfly_sum(): lax.ppermute(value, axes, [(i, i ^ mask) for i in range(count)])]
    ppermute x10, waiting for transfers between devices: 12 us -> 18.9 us  [butterfly_sum(): lax.ppermute(value, axes, [(i, i ^ mask) for i in range(count)])]
    ppermute x1, starting transfers between devices: 1.96 us -> 4.42 us  [per_device(): lax.ppermute(pack_terms(right_terms[0], right_terms[1]), 'seq', [(i, i +...]
    unnamed x22 -> x28, local copies, waits for them, and re-layouts: 7.82 us -> 9.74 us
    concatenate x2, other arithmetic: 0.12 us -> 1.77 us  [pack_terms(): jnp.concatenate([key_part.reshape(sample_count, tile_rows, -1), value_par...]
  transfers between devices with their start and end apart: 14 -> 14, of which waited for: 11 -> 10; matrix products, arithmetic and copies ran while one was open for 5% -> 9% of each run, Pallas kernels for 0% -> 0%
where the time goes in v9:
time: 136 us; the launch traced here: 135 us
  starting transfers between devices  74.1 us (54%)
  waiting for transfers between devices  27.8 us (20%)
  other arithmetic  12.3 us (9%)
  local copies, waits for them, and re-layouts  10.1 us (7%)
  matrix products  7.45 us (5%)
  between operations  3.13 us (2%)
    ppermute x10, starting transfers between devices, butterfly_sum(): lax.ppermute(value, axes, [(i, i ^ mask) for i in range(count)])  62.5 us
    ppermute x10, waiting for transfers between devices, butterfly_sum(): lax.ppermute(value, axes, [(i, i ^ mask) for i in range(count)])  18.9 us
    unnamed x28, local copies, waits for them, and re-layouts  9.74 us
    ppermute x1, waiting for transfers between devices, extended_2(): lax.ppermute(head, axis, [((i + 1) % count, i) for i in range(ends)])  7.74 us
    ppermute x1, starting transfers between devices, extended_2(): lax.ppermute(tail, axis, [(i, (i + 1) % count) for i in range(ends)])  4.58 us
    ppermute x1, starting transfers between devices, per_device(): lax.ppermute(pack_terms(right_terms[0], right_terms[1]), 'seq', [(i, i +...  4.42 us
  transfers between devices with their start and end apart: 14, of which 10 were waited for; matrix products, arithmetic and copies ran while one was open for 9% of the time, Pallas kernels for 0%

profile of v9, /device:TPU:24, one launch (start us, length us, event | category | flops | bytes accessed | tf_op | source)
XLA Modules:
  0.0 134.9 jit_solution(6949826123240208118)
XLA Ops:
  0.7 1.2 copy.45
  1.9 1.2 copy.46
  3.2 1.3 collective-permute-start.1
  4.5 4.6 %collective-permute-start = (bf16[1,384,768]{1,2,0:T(8,128)(2,1)S(1)}, bf16[1,384,768]{1,2,0:T(8,128)(2,1)S(1)}, u32[]{:S(2)}, u32[]{:S(2)}) collective-permute-start(bf16[1,384,768]{1,2,0:T(8,128)(2,1)S(1)} %pad_maximum_fusion.3), channel_id=1, source_target_pairs={{0,64},{64,128},{128,192},{192,256},{256,320},{320,384},{384,448},... | collective-permute-start | bytes 1769480 | tf_op jit(solution)/shard_map/ppermute | solution.py:19
  9.1 0.7 compare_reduce_fusion.2
  12.6 7.7 %collective-permute-done.1 = bf16[1,384,768]{1,2,0:T(8,128)(2,1)S(1)} collective-permute-done((bf16[1,384,768]{1,2,0:T(8,128)(2,1)S(1)}, bf16[1,384,768]{1,2,0:T(8,128)(2,1)S(1)}, u32[]{:S(2)}, u32[]{:S(2)}) %collective-permute-start.1) | collective-permute-done | bytes 589856 | tf_op jit(solution)/shard_map/ppermute | solution.py:21
  20.3 1.2 collective-permute-done
  22.0 0.5 copy-done.7
  22.7 0.5 fusion.30
  23.3 0.5 fusion.31
  23.8 0.4 exponential_reduce_fusion
  24.2 0.3 exponential_convert_fusion
  24.6 0.4 convolution_convert_fusion
  25.0 0.3 convolution_bitcast_fusion
  25.3 0.4 exponential_reduce_fusion.1
  25.8 0.3 exponential_convert_fusion.1
  26.1 0.4 convolution_convert_fusion.1
  26.5 0.3 convolution_bitcast_fusion.1
  26.9 0.5 fusion.32
  27.4 0.4 exponential_reduce_fusion.2
  27.8 0.3 exponential_convert_fusion.2
  28.5 0.4 multiply_reduce_fusion.6
  28.9 0.5 fusion.11
  29.4 0.4 fusion.18
  29.8 0.3 fusion.12
  30.2 0.5 fusion.10
  30.6 0.4 fusion.17
  31.1 0.3 fusion.13
  31.4 0.5 fusion.9
  31.9 0.4 fusion.16
  32.3 0.3 fusion.14
  33.1 0.9 copy-done
  34.1 0.9 fusion.22
  35.0 0.3 fusion.15
  35.4 4.4 %collective-permute-start.4 = (f32[256]{0:T(256)S(1)}, f32[256]{0:T(256)S(1)}, u32[]{:S(2)}, u32[]{:S(2)}) collective-permute-start(f32[256]{0:T(256)S(1)} %pad_maximum_fusion.8), channel_id=1, source_target_pairs={{0,64},{64,0},{128,192},{192,128},{256,320},{320,256},{384,448},{4... | collective-permute-start | bytes 3080 | tf_op jit(solution)/shard_map/ppermute | solution.py:31
  40.1 1.3 collective-permute-done.4
  41.4 5.8 %collective-permute-start.5 = (f32[256]{0:T(256)S(1)}, f32[256]{0:T(256)S(1)}, u32[]{:S(2)}, u32[]{:S(2)}) collective-permute-start(f32[256]{0:T(256)S(1)} %fusion.23), channel_id=1, source_target_pairs={{0,128},{64,192},{128,0},{192,64},{256,384},{320,448},{384,256},{4... | collective-permute-start | bytes 3080 | tf_op jit(solution)/shard_map/ppermute | solution.py:31
  47.2 0.9 pad_maximum_fusion.6
  48.1 0.6 collective-permute-done.5
  48.7 9.4 %collective-permute-start.6 = (f32[256]{0:T(256)S(1)}, f32[256]{0:T(256)S(1)}, u32[]{:S(2)}, u32[]{:S(2)}) collective-permute-start(f32[256]{0:T(256)S(1)} %add.103), channel_id=1, source_target_pairs={{0,256},{64,320},{128,384},{192,448},{256,0},{320,64},{384,128},{4... | collective-permute-start | bytes 3080 | tf_op jit(solution)/shard_map/ppermute | solution.py:31
  58.1 0.9 pad_maximum_fusion.5
  59.0 4.4 %collective-permute-start.2 = (bf16[1,384,768]{1,2,0:T(8,128)(2,1)}, bf16[1,384,768]{1,2,0:T(8,128)(2,1)}, u32[]{:S(2)}, u32[]{:S(2)}) collective-permute-start(bf16[1,384,768]{1,2,0:T(8,128)(2,1)} %pad_maximum_fusion.5), channel_id=1, source_target_pairs={{0,64},{64,128},{128,192},{192,256},{256,320},{320,384},{384,448},... | collective-permute-start | bytes 1769480 | tf_op jit(solution)/shard_map/ppermute | solution.py:200
  63.4 1.3 collective-permute-start.3
  64.7 17.1 %collective-permute-start.7 = (f32[256]{0:T(256)S(1)}, f32[256]{0:T(256)S(1)}, u32[]{:S(2)}, u32[]{:S(2)}) collective-permute-start(f32[256]{0:T(256)S(1)} %add.104), channel_id=1, source_target_pairs={{0,512},{64,576},{128,640},{192,704},{256,768},{320,832},{384,896}... | collective-permute-start | bytes 3080 | tf_op jit(solution)/shard_map/ppermute | solution.py:31
  81.9 7.4 %collective-permute-done.7 = f32[256]{0:T(256)S(1)} collective-permute-done((f32[256]{0:T(256)S(1)}, f32[256]{0:T(256)S(1)}, u32[]{:S(2)}, u32[]{:S(2)}) %collective-permute-start.7) | collective-permute-done | bytes 1056 | tf_op jit(solution)/shard_map/ppermute | solution.py:31
  89.4 1.9 %collective-permute-start.8 = (f32[256]{0:T(256)S(1)}, f32[256]{0:T(256)S(1)}, u32[]{:S(2)}, u32[]{:S(2)}) collective-permute-start(f32[256]{0:T(256)S(1)} %add.105), channel_id=1, source_target_pairs={{0,16},{16,0},{32,48},{48,32},{1,17},{17,1},{33,49},{49,33},{2,18}... | collective-permute-start | bytes 3080 | tf_op jit(solution)/shard_map/ppermute | solution.py:31
  91.3 1.1 collective-permute-done.8
  92.4 11.0 %collective-permute-start.9 = (f32[256]{0:T(256)S(1)}, f32[256]{0:T(256)}, u32[]{:S(2)}, u32[]{:S(2)}) collective-permute-start(f32[256]{0:T(256)S(1)} %add.106), channel_id=1, source_target_pairs={{0,544},{16,560},{32,512},{48,528},{64,608},{80,624},{96,576},{112... | collective-permute-start | bytes 3080 | tf_op jit(solution)/shard_map/ppermute | solution.py:31
  103.4 0.7 pad_maximum_fusion.7
  104.1 1.8 %copy.54 = bf16[1,384,384]{2,1,0:T(8,128)(2,1)} copy(bf16[1,384,384]{1,2,0:T(8,128)(2,1)} %pad_maximum_fusion.7) | data formatting | bytes 589824
  106.0 1.8 %copy.55 = bf16[1,384,384]{2,1,0:T(8,128)(2,1)} copy(bf16[1,384,384]{1,2,0:T(8,128)(2,1)} %get-tuple-element.47) | data formatting | bytes 589824
  107.8 0.7 add.107
  108.5 1.4 %convert_add_fusion = f32[1,384,768]{1,2,0:T(8,128)S(1)} fusion(bf16[1,384,768]{1,2,0:T(8,128)(2,1)} %collective-permute-done.3, bf16[1,384,768]{1,2,0:T(8,128)(2,1)} %collective-permute-done.2), kind=kLoop, calls=%fused_computation.41 | loop fusion | flops 884736 | bytes 2359296 | tf_op jit(solution)/shard_map/add | solution.py:210
  110.0 2.8 %collective-permute-start.10 = (f32[256]{0:T(256)S(1)}, f32[256]{0:T(256)S(1)}, u32[]{:S(2)}, u32[]{:S(2)}) collective-permute-start(f32[256]{0:T(256)S(1)} %add.107), channel_id=1, source_target_pairs={{0,1},{1,0},{2,3},{3,2},{4,5},{5,4},{6,7},{7,6},{8,9},{9,8},{10,11... | collective-permute-start | bytes 3080 | tf_op jit(solution)/shard_map/ppermute | solution.py:31
  112.9 2.6 %collective-permute-done.10 = f32[256]{0:T(256)S(1)} collective-permute-done((f32[256]{0:T(256)S(1)}, f32[256]{0:T(256)S(1)}, u32[]{:S(2)}, u32[]{:S(2)}) %collective-permute-start.10) | collective-permute-done | bytes 1056 | tf_op jit(solution)/shard_map/ppermute | solution.py:31
  115.6 2.1 %collective-permute-start.11 = (f32[256]{0:T(256)S(1)}, f32[256]{0:T(256)S(1)}, u32[]{:S(2)}, u32[]{:S(2)}) collective-permute-start(f32[256]{0:T(256)S(1)} %add.111), channel_id=1, source_target_pairs={{0,3},{1,2},{2,1},{3,0},{4,7},{5,6},{6,5},{7,4},{8,11},{9,10},{10,... | collective-permute-start | bytes 3080 | tf_op jit(solution)/shard_map/ppermute | solution.py:31
  117.7 4.5 %collective-permute-done.11 = f32[256]{0:T(256)S(1)} collective-permute-done((f32[256]{0:T(256)S(1)}, f32[256]{0:T(256)S(1)}, u32[]{:S(2)}, u32[]{:S(2)}) %collective-permute-start.11) | collective-permute-done | bytes 1056 | tf_op jit(solution)/shard_map/ppermute | solution.py:31
  122.2 3.4 %collective-permute-start.12 = (f32[256]{0:T(256)S(1)}, f32[256]{0:T(256)S(1)}, u32[]{:S(2)}, u32[]{:S(2)}) collective-permute-start(f32[256]{0:T(256)S(1)} %add.112), channel_id=1, source_target_pairs={{0,4},{1,5},{2,6},{3,7},{4,0},{5,1},{6,2},{7,3},{8,12},{9,13},{10,... | collective-permute-start | bytes 3080 | tf_op jit(solution)/shard_map/ppermute | solution.py:31
  125.7 0.9 multiply_convert_fusion.1
  126.5 1.2 collective-permute-done.12
  127.7 4.7 %collective-permute-start.13 = (f32[256]{0:T(256)S(1)}, f32[256]{0:T(256)S(1)}, u32[]{:S(2)}, u32[]{:S(2)}) collective-permute-start(f32[256]{0:T(256)S(1)} %add.113), channel_id=1, source_target_pairs={{0,12},{1,13},{2,14},{3,15},{4,8},{5,9},{6,10},{7,11},{8,4},{9,5},... | collective-permute-start | bytes 3080 | tf_op jit(solution)/shard_map/ppermute | solution.py:31
  132.4 0.9 copy.57
  133.3 0.9 copy.56
  134.4 0.5 slice_multiply_fusion
  (69 shorter events, 3.5 us)
Async XLA Ops:
  0.6 8.4 %copy-start.9 = (s32[1,1,3]{2,1,0:T(1,128)S(1)}, s32[1,1,3]{2,1,0:T(1,128)}, u32[]{:S(2)}) copy-start(s32[1,1,3]{2,1,0:T(1,128)} %param.13) | copy-start | bytes 40
  0.6 11.2 %copy-start.5 = (bf16[1,384,384]{2,1,0:T(8,128)(2,1)S(1)}, bf16[1,384,384]{2,1,0:T(8,128)(2,1)}, u32[]{:S(2)}) copy-start(bf16[1,384,384]{2,1,0:T(8,128)(2,1)} %param.7) | copy-start | bytes 884740
  0.7 11.4 %copy-start.6 = (bf16[1,384,384]{2,1,0:T(8,128)(2,1)S(1)}, bf16[1,384,384]{2,1,0:T(8,128)(2,1)}, u32[]{:S(2)}) copy-start(bf16[1,384,384]{2,1,0:T(8,128)(2,1)} %param.12) | copy-start | bytes 884740
  3.1 9.3 %copy-start.8 = (f32[128]{0:T(128)S(1)}, f32[128]{0:T(128)}, u32[]{:S(2)}) copy-start(f32[128]{0:T(128)} %param.10) | copy-start | bytes 1540
  3.2 17.1 %collective-permute-start.1 = (bf16[1,384,768]{1,2,0:T(8,128)(2,1)S(1)}, bf16[1,384,768]{1,2,0:T(8,128)(2,1)S(1)}, u32[]{:S(2)}, u32[]{:S(2)}) collective-permute-start(bf16[1,384,768]{1,2,0:T(8,128)(2,1)S(1)} %pad_maximum_fusion.3), channel_id=1, source_target_pairs={{64,0},{128,64},{192,128},{256,192},{320,256},{384,320},{448,384},... | collective-permute-start | bytes 1769480 | tf_op jit(solution)/shard_map/ppermute | solution.py:21
  4.5 17.0 %collective-permute-start = (bf16[1,384,768]{1,2,0:T(8,128)(2,1)S(1)}, bf16[1,384,768]{1,2,0:T(8,128)(2,1)S(1)}, u32[]{:S(2)}, u32[]{:S(2)}) collective-permute-start(bf16[1,384,768]{1,2,0:T(8,128)(2,1)S(1)} %pad_maximum_fusion.3), channel_id=1, source_target_pairs={{0,64},{64,128},{128,192},{192,256},{256,320},{320,384},{384,448},... | collective-permute-start | bytes 1769480 | tf_op jit(solution)/shard_map/ppermute | solution.py:19
  12.1 9.5 %copy-start.2 = (bf16[1,384,384]{1,2,0:T(8,128)(2,1)}, bf16[1,384,384]{1,2,0:T(8,128)(2,1)S(1)}, u32[]{:S(2)}) copy-start(bf16[1,384,384]{1,2,0:T(8,128)(2,1)S(1)} %copy.44) | copy-start | bytes 884740
  21.8 0.7 copy-start.7
  32.8 1.2 copy-start
  32.8 1.2 copy-start.3
  34.0 1.1 slice-start
  35.4 5.9 %collective-permute-start.4 = (f32[256]{0:T(256)S(1)}, f32[256]{0:T(256)S(1)}, u32[]{:S(2)}, u32[]{:S(2)}) collective-permute-start(f32[256]{0:T(256)S(1)} %pad_maximum_fusion.8), channel_id=1, source_target_pairs={{0,64},{64,0},{128,192},{192,128},{256,320},{320,256},{384,448},{4... | collective-permute-start | bytes 3080 | tf_op jit(solution)/shard_map/ppermute | solution.py:31
  41.4 7.4 %collective-permute-start.5 = (f32[256]{0:T(256)S(1)}, f32[256]{0:T(256)S(1)}, u32[]{:S(2)}, u32[]{:S(2)}) collective-permute-start(f32[256]{0:T(256)S(1)} %fusion.23), channel_id=1, source_target_pairs={{0,128},{64,192},{128,0},{192,64},{256,384},{320,448},{384,256},{4... | collective-permute-start | bytes 3080 | tf_op jit(solution)/shard_map/ppermute | solution.py:31
  48.7 16.0 %collective-permute-start.6 = (f32[256]{0:T(256)S(1)}, f32[256]{0:T(256)S(1)}, u32[]{:S(2)}, u32[]{:S(2)}) collective-permute-start(f32[256]{0:T(256)S(1)} %add.103), channel_id=1, source_target_pairs={{0,256},{64,320},{128,384},{192,448},{256,0},{320,64},{384,128},{4... | collective-permute-start | bytes 3080 | tf_op jit(solution)/shard_map/ppermute | solution.py:31
  59.0 49.5 %collective-permute-start.2 = (bf16[1,384,768]{1,2,0:T(8,128)(2,1)}, bf16[1,384,768]{1,2,0:T(8,128)(2,1)}, u32[]{:S(2)}, u32[]{:S(2)}) collective-permute-start(bf16[1,384,768]{1,2,0:T(8,128)(2,1)} %pad_maximum_fusion.5), channel_id=1, source_target_pairs={{0,64},{64,128},{128,192},{192,256},{256,320},{320,384},{384,448},... | collective-permute-start | bytes 1769480 | tf_op jit(solution)/shard_map/ppermute | solution.py:200
  63.4 45.1 %collective-permute-start.3 = (bf16[1,384,768]{1,2,0:T(8,128)(2,1)}, bf16[1,384,768]{1,2,0:T(8,128)(2,1)}, u32[]{:S(2)}, u32[]{:S(2)}) collective-permute-start(bf16[1,384,768]{1,2,0:T(8,128)(2,1)} %pad_maximum_fusion.6), channel_id=1, source_target_pairs={{64,0},{128,64},{192,128},{256,192},{320,256},{384,320},{448,384},... | collective-permute-start | bytes 1769480 | tf_op jit(solution)/shard_map/ppermute | solution.py:203
  64.7 24.6 %collective-permute-start.7 = (f32[256]{0:T(256)S(1)}, f32[256]{0:T(256)S(1)}, u32[]{:S(2)}, u32[]{:S(2)}) collective-permute-start(f32[256]{0:T(256)S(1)} %add.104), channel_id=1, source_target_pairs={{0,512},{64,576},{128,640},{192,704},{256,768},{320,832},{384,896}... | collective-permute-start | bytes 3080 | tf_op jit(solution)/shard_map/ppermute | solution.py:31
  89.4 3.0 %collective-permute-start.8 = (f32[256]{0:T(256)S(1)}, f32[256]{0:T(256)S(1)}, u32[]{:S(2)}, u32[]{:S(2)}) collective-permute-start(f32[256]{0:T(256)S(1)} %add.105), channel_id=1, source_target_pairs={{0,16},{16,0},{32,48},{48,32},{1,17},{17,1},{33,49},{49,33},{2,18}... | collective-permute-start | bytes 3080 | tf_op jit(solution)/shard_map/ppermute | solution.py:31
  92.4 15.4 %collective-permute-start.9 = (f32[256]{0:T(256)S(1)}, f32[256]{0:T(256)}, u32[]{:S(2)}, u32[]{:S(2)}) collective-permute-start(f32[256]{0:T(256)S(1)} %add.106), channel_id=1, source_target_pairs={{0,544},{16,560},{32,512},{48,528},{64,608},{80,624},{96,576},{112... | collective-permute-start | bytes 3080 | tf_op jit(solution)/shard_map/ppermute | solution.py:31
  109.9 2.9 %copy-start.1 = (f32[1,1152,3,128]{1,3,2,0:T(8,128)S(1)}, f32[1,1152,3,128]{1,3,2,0:T(8,128)}, u32[]{:S(2)}) copy-start(f32[1,1152,3,128]{1,3,2,0:T(8,128)} %copy-done) | copy-start | bytes 5308420
  110.0 5.6 %collective-permute-start.10 = (f32[256]{0:T(256)S(1)}, f32[256]{0:T(256)S(1)}, u32[]{:S(2)}, u32[]{:S(2)}) collective-permute-start(f32[256]{0:T(256)S(1)} %add.107), channel_id=1, source_target_pairs={{0,1},{1,0},{2,3},{3,2},{4,5},{5,4},{6,7},{7,6},{8,9},{9,8},{10,11... | collective-permute-start | bytes 3080 | tf_op jit(solution)/shard_map/ppermute | solution.py:31
  115.6 6.7 %collective-permute-start.11 = (f32[256]{0:T(256)S(1)}, f32[256]{0:T(256)S(1)}, u32[]{:S(2)}, u32[]{:S(2)}) collective-permute-start(f32[256]{0:T(256)S(1)} %add.111), channel_id=1, source_target_pairs={{0,3},{1,2},{2,1},{3,0},{4,7},{5,6},{6,5},{7,4},{8,11},{9,10},{10,... | collective-permute-start | bytes 3080 | tf_op jit(solution)/shard_map/ppermute | solution.py:31
  122.2 5.5 %collective-permute-start.12 = (f32[256]{0:T(256)S(1)}, f32[256]{0:T(256)S(1)}, u32[]{:S(2)}, u32[]{:S(2)}) collective-permute-start(f32[256]{0:T(256)S(1)} %add.112), channel_id=1, source_target_pairs={{0,4},{1,5},{2,6},{3,7},{4,0},{5,1},{6,2},{7,3},{8,12},{9,13},{10,... | collective-permute-start | bytes 3080 | tf_op jit(solution)/shard_map/ppermute | solution.py:31
  126.5 6.8 %copy-start.4 = (bf16[1,384,3,128]{1,3,2,0:T(8,128)(2,1)S(1)}, bf16[1,384,3,128]{1,3,2,0:T(8,128)(2,1)}, u32[]{:S(2)}) copy-start(bf16[1,384,3,128]{1,3,2,0:T(8,128)(2,1)} %multiply_convert_fusion.1) | copy-start | bytes 884740
  127.7 6.7 %collective-permute-start.13 = (f32[256]{0:T(256)S(1)}, f32[256]{0:T(256)S(1)}, u32[]{:S(2)}, u32[]{:S(2)}) collective-permute-start(f32[256]{0:T(256)S(1)} %add.113), channel_id=1, source_target_pairs={{0,12},{1,13},{2,14},{3,15},{4,8},{5,9},{6,10},{7,11},{8,4},{9,5},... | collective-permute-start | bytes 3080 | tf_op jit(solution)/shard_map/ppermute | solution.py:31

commit v10 on v7

--- a/solution.py
+++ b/solution.py
@@ -36,16 +36,15 @@
     seq_count = lax.axis_size("seq")
     head_count = lax.axis_size("head")
     fsdp_count = lax.axis_size("fsdp")
-    stages = []
-    step = 1
-    while step < seq_count:
-        stages.append((("seq",), step))
-        step *= 2
-    stages.append((("head",), 1))
+    stages = [(("head",), 1)]
     half = seq_count // 2
     step = 2
     while step < head_count:
         stages.append((("seq", "head"), half * head_count + step))
+        step *= 2
+    step = 1
+    while step < seq_count:
+        stages.append((("seq",), step))
         step *= 2
     side = math.isqrt(fsdp_count)
     for base in (1, side):

time: 136 us -> 136 us (level)
  waiting for transfers between devices: 20.9 us -> 37 us
  starting transfers between devices: 80.6 us -> 64.5 us
    ppermute x10, waiting for transfers between devices: 12 us -> 28 us  [butterfly_sum(): lax.ppermute(value, axes, [(i, i ^ mask) for i in range(count)])]
    ppermute x10, starting transfers between devices: 71.4 us -> 55.4 us  [butterfly_sum(): lax.ppermute(value, axes, [(i, i ^ mask) for i in range(count)])]
where the time goes in v10:
time: 136 us; the launch traced here: 133 us
  starting transfers between devices  64.5 us (47%)
  waiting for transfers between devices  37 us (27%)
  other arithmetic  12.4 us (9%)
  local copies, waits for them, and re-layouts  8.82 us (6%)
  matrix products  7.46 us (5%)
  between operations  3.1 us (2%)
    ppermute x10, starting transfers between devices, butterfly_sum(): lax.ppermute(value, axes, [(i, i ^ mask) for i in range(count)])  55.4 us
    ppermute x10, waiting for transfers between devices, butterfly_sum(): lax.ppermute(value, axes, [(i, i ^ mask) for i in range(count)])  28 us
    unnamed x22, local copies, waits for them, and re-layouts  7.82 us
    ppermute x1, waiting for transfers between devices, extended_2(): lax.ppermute(head, axis, [((i + 1) % count, i) for i in range(ends)])  7.75 us
    ppermute x1, starting transfers between devices, extended_2(): lax.ppermute(tail, axis, [(i, (i + 1) % count) for i in range(ends)])  4.58 us
  transfers between devices with their start and end apart: 14, of which 11 were waited for; matrix products, arithmetic and copies ran while one was open for 5% of the time, Pallas kernels for 0%

profile of v10, /device:TPU:24, one launch (start us, length us, event | category | flops | bytes accessed | tf_op | source)
XLA Modules:
  0.0 133.2 jit_solution(10607548048604905126)
XLA Ops:
  0.7 1.2 copy.45
  1.9 1.2 copy.46
  3.2 1.3 collective-permute-start.1
  4.5 4.6 %collective-permute-start = (bf16[1,384,768]{1,2,0:T(8,128)(2,1)S(1)}, bf16[1,384,768]{1,2,0:T(8,128)(2,1)S(1)}, u32[]{:S(2)}, u32[]{:S(2)}) collective-permute-start(bf16[1,384,768]{1,2,0:T(8,128)(2,1)S(1)} %pad_maximum_fusion.3), channel_id=1, source_target_pairs={{0,64},{64,128},{128,192},{192,256},{256,320},{320,384},{384,448},... | collective-permute-start | bytes 1769480 | tf_op jit(solution)/shard_map/ppermute | solution.py:19
  9.1 0.7 compare_reduce_fusion.2
  12.5 7.8 %collective-permute-done.1 = bf16[1,384,768]{1,2,0:T(8,128)(2,1)S(1)} collective-permute-done((bf16[1,384,768]{1,2,0:T(8,128)(2,1)S(1)}, bf16[1,384,768]{1,2,0:T(8,128)(2,1)S(1)}, u32[]{:S(2)}, u32[]{:S(2)}) %collective-permute-start.1) | collective-permute-done | bytes 589856 | tf_op jit(solution)/shard_map/ppermute | solution.py:21
  20.3 1.2 collective-permute-done
  22.0 0.5 copy-done.4
  22.5 1.4 %multiply_convert_fusion = (bf16[1,1152,3,128]{1,3,2,0:T(8,128)(2,1)S(1)}, f32[1,1152,3,128]{1,3,2,0:T(8,128)}) fusion(f32[128]{0:T(128)S(1)} %copy-done.4, f32[1,1152,3,128]{1,3,2,0:T(8,128)S(1)} %bitcast.181, f32[1152,3]{0,1:T(4,128)S(1)} %get-tuple-element.53), kind=kLoop, calls=%fused_computation.39 | loop fusion | flops 1327104 | bytes 4438016 | tf_op jit(solution)/shard_map/convert_element_type | solution.py:62
  23.9 0.5 fusion.30
  24.5 0.5 fusion.31
  25.0 0.5 fusion.32
  25.5 0.4 exponential_reduce_fusion
  26.0 0.3 exponential_convert_fusion
  26.3 0.4 exponential_reduce_fusion.1
  26.7 0.3 exponential_convert_fusion.1
  27.1 0.4 convolution_convert_fusion
  27.5 0.4 convolution_convert_fusion.1
  27.9 0.4 exponential_reduce_fusion.2
  28.3 0.3 exponential_convert_fusion.2
  28.7 0.4 multiply_reduce_fusion.6
  29.1 0.5 fusion.11
  29.6 0.4 fusion.18
  30.0 0.3 fusion.12
  30.3 0.5 fusion.10
  30.8 0.4 fusion.17
  31.2 0.3 fusion.13
  31.5 0.5 fusion.9
  32.0 0.4 fusion.16
  32.4 0.4 fusion.14
  33.2 0.9 copy-done
  34.5 0.7 slice-done
  35.2 0.3 fusion.15
  35.6 1.9 %collective-permute-start.4 = (f32[256]{0:T(256)S(1)}, f32[256]{0:T(256)S(1)}, u32[]{:S(2)}, u32[]{:S(2)}) collective-permute-start(f32[256]{0:T(256)S(1)} %pad_maximum_fusion.8), channel_id=1, source_target_pairs={{0,16},{16,0},{32,48},{48,32},{1,17},{17,1},{33,49},{49,33},{2,18}... | collective-permute-start | bytes 3080 | tf_op jit(solution)/shard_map/ppermute | solution.py:31
  37.8 0.8 collective-permute-done.4
  38.6 26.7 %collective-permute-start.5 = (f32[256]{0:T(256)S(1)}, f32[256]{0:T(256)S(1)}, u32[]{:S(2)}, u32[]{:S(2)}) collective-permute-start(f32[256]{0:T(256)S(1)} %fusion.23), channel_id=1, source_target_pairs={{0,544},{16,560},{32,512},{48,528},{64,608},{80,624},{96,576},{112... | collective-permute-start | bytes 3080 | tf_op jit(solution)/shard_map/ppermute | solution.py:31
  65.3 0.3 convolution_bitcast_fusion.1
  65.6 1.2 collective-permute-done.5
  66.8 1.9 %collective-permute-start.6 = (f32[256]{0:T(256)S(1)}, f32[256]{0:T(256)S(1)}, u32[]{:S(2)}, u32[]{:S(2)}) collective-permute-start(f32[256]{0:T(256)S(1)} %add.103), channel_id=1, source_target_pairs={{0,64},{64,0},{128,192},{192,128},{256,320},{320,256},{384,448},{4... | collective-permute-start | bytes 3080 | tf_op jit(solution)/shard_map/ppermute | solution.py:31
  68.8 0.3 convolution_bitcast_fusion.2
  69.1 3.2 %collective-permute-done.6 = f32[256]{0:T(256)S(1)} collective-permute-done((f32[256]{0:T(256)S(1)}, f32[256]{0:T(256)S(1)}, u32[]{:S(2)}, u32[]{:S(2)}) %collective-permute-start.6) | collective-permute-done | bytes 1056 | tf_op jit(solution)/shard_map/ppermute | solution.py:31
  72.3 1.9 %collective-permute-start.7 = (f32[256]{0:T(256)S(1)}, f32[256]{0:T(256)S(1)}, u32[]{:S(2)}, u32[]{:S(2)}) collective-permute-start(f32[256]{0:T(256)S(1)} %add.104), channel_id=1, source_target_pairs={{0,128},{64,192},{128,0},{192,64},{256,384},{320,448},{384,256},{4... | collective-permute-start | bytes 3080 | tf_op jit(solution)/shard_map/ppermute | solution.py:31
  74.4 4.2 %collective-permute-done.7 = f32[256]{0:T(256)S(1)} collective-permute-done((f32[256]{0:T(256)S(1)}, f32[256]{0:T(256)S(1)}, u32[]{:S(2)}, u32[]{:S(2)}) %collective-permute-start.7) | collective-permute-done | bytes 1056 | tf_op jit(solution)/shard_map/ppermute | solution.py:31
  78.6 4.3 %collective-permute-start.8 = (f32[256]{0:T(256)S(1)}, f32[256]{0:T(256)S(1)}, u32[]{:S(2)}, u32[]{:S(2)}) collective-permute-start(f32[256]{0:T(256)S(1)} %add.105), channel_id=1, source_target_pairs={{0,256},{64,320},{128,384},{192,448},{256,0},{320,64},{384,128},{4... | collective-permute-start | bytes 3080 | tf_op jit(solution)/shard_map/ppermute | solution.py:31
  83.0 5.0 %collective-permute-done.8 = f32[256]{0:T(256)S(1)} collective-permute-done((f32[256]{0:T(256)S(1)}, f32[256]{0:T(256)S(1)}, u32[]{:S(2)}, u32[]{:S(2)}) %collective-permute-start.8) | collective-permute-done | bytes 1056 | tf_op jit(solution)/shard_map/ppermute | solution.py:31
  88.0 5.0 %collective-permute-start.9 = (f32[256]{0:T(256)S(1)}, f32[256]{0:T(256)S(1)}, u32[]{:S(2)}, u32[]{:S(2)}) collective-permute-start(f32[256]{0:T(256)S(1)} %add.106), channel_id=1, source_target_pairs={{0,512},{64,576},{128,640},{192,704},{256,768},{320,832},{384,896}... | collective-permute-start | bytes 3080 | tf_op jit(solution)/shard_map/ppermute | solution.py:31
  93.1 9.1 %collective-permute-done.9 = f32[256]{0:T(256)S(1)} collective-permute-done((f32[256]{0:T(256)S(1)}, f32[256]{0:T(256)S(1)}, u32[]{:S(2)}, u32[]{:S(2)}) %collective-permute-start.9) | collective-permute-done | bytes 1056 | tf_op jit(solution)/shard_map/ppermute | solution.py:31
  102.2 2.6 %collective-permute-start.10 = (f32[256]{0:T(256)S(1)}, f32[256]{0:T(256)S(1)}, u32[]{:S(2)}, u32[]{:S(2)}) collective-permute-start(f32[256]{0:T(256)S(1)} %add.107), channel_id=1, source_target_pairs={{0,1},{1,0},{2,3},{3,2},{4,5},{5,4},{6,7},{7,6},{8,9},{9,8},{10,11... | collective-permute-start | bytes 3080 | tf_op jit(solution)/shard_map/ppermute | solution.py:31
  104.9 2.0 %collective-permute-start.2 = (bf16[1,384,768]{1,2,0:T(8,128)(2,1)S(1)}, bf16[1,384,768]{1,2,0:T(8,128)(2,1)S(1)}, u32[]{:S(2)}, u32[]{:S(2)}) collective-permute-start(bf16[1,384,768]{1,2,0:T(8,128)(2,1)S(1)} %pad_maximum_fusion.5), channel_id=1, source_target_pairs={{0,64},{64,128},{128,192},{192,256},{256,320},{320,384},{384,448},... | collective-permute-start | bytes 1769480 | tf_op jit(solution)/shard_map/ppermute | solution.py:197
  106.9 1.3 collective-permute-start.3
  108.2 3.0 %collective-permute-start.11 = (f32[256]{0:T(256)S(1)}, f32[256]{0:T(256)S(1)}, u32[]{:S(2)}, u32[]{:S(2)}) collective-permute-start(f32[256]{0:T(256)S(1)} %add.108), channel_id=1, source_target_pairs={{0,3},{1,2},{2,1},{3,0},{4,7},{5,6},{6,5},{7,4},{8,11},{9,10},{10,... | collective-permute-start | bytes 3080 | tf_op jit(solution)/shard_map/ppermute | solution.py:31
  111.2 1.3 %pad_maximum_fusion.2 = f32[1,1152,3,128]{1,3,2,0:T(8,128)} fusion(f32[1,1152,1,128]{1,3,2,0:T(8,128)S(1)} %convolution_bitcast_fusion, f32[1,1152,1,128]{1,3,2,0:T(8,128)S(1)} %convolution_bitcast_fusion.1, f32[1,1152,1,128]{1,3,2,0:T(8,128)S(1)} %convolution_bitcast_fusion.2), kind=kLoop, calls=%fused_computation.29 | loop fusion | flops 884736 | bytes 3538944 | tf_op jit(solution)/shard_map/stack | solution.py:172
  112.5 2.3 %collective-permute-done.11 = f32[256]{0:T(256)S(1)} collective-permute-done((f32[256]{0:T(256)S(1)}, f32[256]{0:T(256)S(1)}, u32[]{:S(2)}, u32[]{:S(2)}) %collective-permute-start.11) | collective-permute-done | bytes 1056 | tf_op jit(solution)/shard_map/ppermute | solution.py:31
  114.9 3.4 %collective-permute-start.12 = (f32[256]{0:T(256)S(1)}, f32[256]{0:T(256)S(1)}, u32[]{:S(2)}, u32[]{:S(2)}) collective-permute-start(f32[256]{0:T(256)S(1)} %add.109), channel_id=1, source_target_pairs={{0,4},{1,5},{2,6},{3,7},{4,0},{5,1},{6,2},{7,3},{8,12},{9,13},{10,... | collective-permute-start | bytes 3080 | tf_op jit(solution)/shard_map/ppermute | solution.py:31
  118.3 2.0 %collective-permute-done.12 = f32[256]{0:T(256)S(1)} collective-permute-done((f32[256]{0:T(256)S(1)}, f32[256]{0:T(256)S(1)}, u32[]{:S(2)}, u32[]{:S(2)}) %collective-permute-start.12) | collective-permute-done | bytes 1056 | tf_op jit(solution)/shard_map/ppermute | solution.py:31
  120.3 4.6 %collective-permute-start.13 = (f32[256]{0:T(256)S(1)}, f32[256]{0:T(256)S(1)}, u32[]{:S(2)}, u32[]{:S(2)}) collective-permute-start(f32[256]{0:T(256)S(1)} %add.110), channel_id=1, source_target_pairs={{0,12},{1,13},{2,14},{3,15},{4,8},{5,9},{6,10},{7,11},{8,4},{9,5},... | collective-permute-start | bytes 3080 | tf_op jit(solution)/shard_map/ppermute | solution.py:31
  125.0 0.9 copy.54
  125.9 0.9 copy.55
  127.2 1.2 fusion.20
  128.5 0.9 copy.57
  129.4 0.5 slice_multiply_fusion
  129.9 1.2 multiply_reduce_fusion.1
  131.1 1.2 multiply_convert_fusion.1
  132.3 0.9 copy.56
  (63 shorter events, 3.4 us)
Async XLA Ops:
  0.6 8.4 %copy-start.6 = (s32[1,1,3]{2,1,0:T(1,128)S(1)}, s32[1,1,3]{2,1,0:T(1,128)}, u32[]{:S(2)}) copy-start(s32[1,1,3]{2,1,0:T(1,128)} %param.13) | copy-start | bytes 40
  0.6 11.2 %copy-start.2 = (bf16[1,384,384]{2,1,0:T(8,128)(2,1)S(1)}, bf16[1,384,384]{2,1,0:T(8,128)(2,1)}, u32[]{:S(2)}) copy-start(bf16[1,384,384]{2,1,0:T(8,128)(2,1)} %param.7) | copy-start | bytes 884740
  0.7 11.4 %copy-start.3 = (bf16[1,384,384]{2,1,0:T(8,128)(2,1)S(1)}, bf16[1,384,384]{2,1,0:T(8,128)(2,1)}, u32[]{:S(2)}) copy-start(bf16[1,384,384]{2,1,0:T(8,128)(2,1)} %param.12) | copy-start | bytes 884740
  3.1 9.3 %copy-start.5 = (f32[128]{0:T(128)S(1)}, f32[128]{0:T(128)}, u32[]{:S(2)}) copy-start(f32[128]{0:T(128)} %param.10) | copy-start | bytes 1540
  3.2 17.1 %collective-permute-start.1 = (bf16[1,384,768]{1,2,0:T(8,128)(2,1)S(1)}, bf16[1,384,768]{1,2,0:T(8,128)(2,1)S(1)}, u32[]{:S(2)}, u32[]{:S(2)}) collective-permute-start(bf16[1,384,768]{1,2,0:T(8,128)(2,1)S(1)} %pad_maximum_fusion.3), channel_id=1, source_target_pairs={{64,0},{128,64},{192,128},{256,192},{320,256},{384,320},{448,384},... | collective-permute-start | bytes 1769480 | tf_op jit(solution)/shard_map/ppermute | solution.py:21
  4.5 17.0 %collective-permute-start = (bf16[1,384,768]{1,2,0:T(8,128)(2,1)S(1)}, bf16[1,384,768]{1,2,0:T(8,128)(2,1)S(1)}, u32[]{:S(2)}, u32[]{:S(2)}) collective-permute-start(bf16[1,384,768]{1,2,0:T(8,128)(2,1)S(1)} %pad_maximum_fusion.3), channel_id=1, source_target_pairs={{0,64},{64,128},{128,192},{192,256},{256,320},{320,384},{384,448},... | collective-permute-start | bytes 1769480 | tf_op jit(solution)/shard_map/ppermute | solution.py:19
  21.8 0.7 copy-start.4
  32.9 1.2 copy-start
  34.1 1.1 slice-start
  35.6 3.0 %collective-permute-start.4 = (f32[256]{0:T(256)S(1)}, f32[256]{0:T(256)S(1)}, u32[]{:S(2)}, u32[]{:S(2)}) collective-permute-start(f32[256]{0:T(256)S(1)} %pad_maximum_fusion.8), channel_id=1, source_target_pairs={{0,16},{16,0},{32,48},{48,32},{1,17},{17,1},{33,49},{49,33},{2,18}... | collective-permute-start | bytes 3080 | tf_op jit(solution)/shard_map/ppermute | solution.py:31
  38.6 28.2 %collective-permute-start.5 = (f32[256]{0:T(256)S(1)}, f32[256]{0:T(256)S(1)}, u32[]{:S(2)}, u32[]{:S(2)}) collective-permute-start(f32[256]{0:T(256)S(1)} %fusion.23), channel_id=1, source_target_pairs={{0,544},{16,560},{32,512},{48,528},{64,608},{80,624},{96,576},{112... | collective-permute-start | bytes 3080 | tf_op jit(solution)/shard_map/ppermute | solution.py:31
  66.8 5.5 %collective-permute-start.6 = (f32[256]{0:T(256)S(1)}, f32[256]{0:T(256)S(1)}, u32[]{:S(2)}, u32[]{:S(2)}) collective-permute-start(f32[256]{0:T(256)S(1)} %add.103), channel_id=1, source_target_pairs={{0,64},{64,0},{128,192},{192,128},{256,320},{320,256},{384,448},{4... | collective-permute-start | bytes 3080 | tf_op jit(solution)/shard_map/ppermute | solution.py:31
  72.3 6.3 %collective-permute-start.7 = (f32[256]{0:T(256)S(1)}, f32[256]{0:T(256)S(1)}, u32[]{:S(2)}, u32[]{:S(2)}) collective-permute-start(f32[256]{0:T(256)S(1)} %add.104), channel_id=1, source_target_pairs={{0,128},{64,192},{128,0},{192,64},{256,384},{320,448},{384,256},{4... | collective-permute-start | bytes 3080 | tf_op jit(solution)/shard_map/ppermute | solution.py:31
  78.6 9.4 %collective-permute-start.8 = (f32[256]{0:T(256)S(1)}, f32[256]{0:T(256)S(1)}, u32[]{:S(2)}, u32[]{:S(2)}) collective-permute-start(f32[256]{0:T(256)S(1)} %add.105), channel_id=1, source_target_pairs={{0,256},{64,320},{128,384},{192,448},{256,0},{320,64},{384,128},{4... | collective-permute-start | bytes 3080 | tf_op jit(solution)/shard_map/ppermute | solution.py:31
  88.0 14.2 %collective-permute-start.9 = (f32[256]{0:T(256)S(1)}, f32[256]{0:T(256)S(1)}, u32[]{:S(2)}, u32[]{:S(2)}) collective-permute-start(f32[256]{0:T(256)S(1)} %add.106), channel_id=1, source_target_pairs={{0,512},{64,576},{128,640},{192,704},{256,768},{320,832},{384,896}... | collective-permute-start | bytes 3080 | tf_op jit(solution)/shard_map/ppermute | solution.py:31
  102.2 6.0 %collective-permute-start.10 = (f32[256]{0:T(256)S(1)}, f32[256]{0:T(256)S(1)}, u32[]{:S(2)}, u32[]{:S(2)}) collective-permute-start(f32[256]{0:T(256)S(1)} %add.107), channel_id=1, source_target_pairs={{0,1},{1,0},{2,3},{3,2},{4,5},{5,4},{6,7},{7,6},{8,9},{9,8},{10,11... | collective-permute-start | bytes 3080 | tf_op jit(solution)/shard_map/ppermute | solution.py:31
  104.9 22.1 %collective-permute-start.2 = (bf16[1,384,768]{1,2,0:T(8,128)(2,1)S(1)}, bf16[1,384,768]{1,2,0:T(8,128)(2,1)S(1)}, u32[]{:S(2)}, u32[]{:S(2)}) collective-permute-start(bf16[1,384,768]{1,2,0:T(8,128)(2,1)S(1)} %pad_maximum_fusion.5), channel_id=1, source_target_pairs={{0,64},{64,128},{128,192},{192,256},{256,320},{320,384},{384,448},... | collective-permute-start | bytes 1769480 | tf_op jit(solution)/shard_map/ppermute | solution.py:197
  106.9 20.1 %collective-permute-start.3 = (bf16[1,384,768]{1,2,0:T(8,128)(2,1)S(1)}, bf16[1,384,768]{1,2,0:T(8,128)(2,1)S(1)}, u32[]{:S(2)}, u32[]{:S(2)}) collective-permute-start(bf16[1,384,768]{1,2,0:T(8,128)(2,1)S(1)} %pad_maximum_fusion.6), channel_id=1, source_target_pairs={{64,0},{128,64},{192,128},{256,192},{320,256},{384,320},{448,384},... | collective-permute-start | bytes 1769480 | tf_op jit(solution)/shard_map/ppermute | solution.py:200
  108.2 6.7 %collective-permute-start.11 = (f32[256]{0:T(256)S(1)}, f32[256]{0:T(256)S(1)}, u32[]{:S(2)}, u32[]{:S(2)}) collective-permute-start(f32[256]{0:T(256)S(1)} %add.108), channel_id=1, source_target_pairs={{0,3},{1,2},{2,1},{3,0},{4,7},{5,6},{6,5},{7,4},{8,11},{9,10},{10,... | collective-permute-start | bytes 3080 | tf_op jit(solution)/shard_map/ppermute | solution.py:31
  114.9 5.5 %collective-permute-start.12 = (f32[256]{0:T(256)S(1)}, f32[256]{0:T(256)S(1)}, u32[]{:S(2)}, u32[]{:S(2)}) collective-permute-start(f32[256]{0:T(256)S(1)} %add.109), channel_id=1, source_target_pairs={{0,4},{1,5},{2,6},{3,7},{4,0},{5,1},{6,2},{7,3},{8,12},{9,13},{10,... | collective-permute-start | bytes 3080 | tf_op jit(solution)/shard_map/ppermute | solution.py:31
  120.3 6.7 %collective-permute-start.13 = (f32[256]{0:T(256)S(1)}, f32[256]{0:T(256)S(1)}, u32[]{:S(2)}, u32[]{:S(2)}) collective-permute-start(f32[256]{0:T(256)S(1)} %add.110), channel_id=1, source_target_pairs={{0,12},{1,13},{2,14},{3,15},{4,8},{5,9},{6,10},{7,11},{8,4},{9,5},... | collective-permute-start | bytes 3080 | tf_op jit(solution)/shard_map/ppermute | solution.py:31
  127.1 2.8 %copy-start.1 = (f32[1,1152,3,128]{1,3,2,0:T(8,128)S(1)}, f32[1,1152,3,128]{1,3,2,0:T(8,128)}, u32[]{:S(2)}) copy-start(f32[1,1152,3,128]{1,3,2,0:T(8,128)} %copy-done) | copy-start | bytes 5308420
